TPU v7x, 128 devices: a whole 4x4x4 slice. The times are simulated.
128 devices in a mesh: chain: 32 (over z, x, core), dp: 4 (over y).
Axes of the slice: x: 4, y: 4, z: 4, core: 2. Of those that a mesh axis runs over, the one named last changes fastest.
Arguments:
- hidden: bfloat16 [4, 4096, 4096], P('dp', 'chain'), may hold values from -6 to 6
- w_bc: bfloat16 [4096, 256], replicated, may hold values from -0.046875 to 0.046875
- xs: bfloat16 [4, 4096, 4096], P('dp', 'chain'), may hold values from -6 to 6
- dt_raw: float32 [4, 4096, 32], P('dp', 'chain'), may hold values from -4 to 4
- a_log: float32 [32], replicated, as said below
- d_out: bfloat16 [4, 4096, 4096], P('dp', 'chain'), may hold values from -6 to 6
Outputs:
- d_xs: bfloat16 [4, 4096, 4096], P('dp', 'chain')
- d_wbc: float32 [4096, 256], replicated
- d_alog: float32 [32], replicated
Inputs may be any that keep to these rules, and one draw needn't show every extreme that they name: exp(a_log) lies between 0.3 / 4096 and 0.05.
All inputs are finite; a program needn't handle non-finite values.
Results may differ from a plain program's by a relative error of at most 0.0058.
Values sent between devices are 32-bit elements; how exact they have to be, the bound alone decides.
No kernel may reach another device: no remote copies, remote signals or barrier semaphores. Data moves between devices by JAX's collectives and lax.ppermute only.
A program may use at most 448 MiB of HBM per device.

v0:
```python
import jax
import jax.numpy as jnp
from jax import lax
from jax.sharding import PartitionSpec as P

GROUP = 128


HIGH = lax.Precision.HIGHEST


def entering(value, axis, join, neutral, backward):
    count, mine = (lax.axis_size(axis), lax.axis_index(axis))
    pieces = jax.tree.map(lambda part: lax.all_gather(part, axis), value)
    if backward:
        pieces = jax.tree.map(lambda part: part[::-1], pieces)
        mine = count - 1 - mine
    so_far = jax.tree.map(
        lambda part, zero: jnp.full_like(part, 0) + jnp.asarray(zero, part.dtype), value, neutral
    )

    def turn(position, so_far):
        longer = join(so_far, jax.tree.map(lambda part: part[position], pieces))
        return jax.tree.map(lambda new, old: jnp.where(position < mine, new, old), longer, so_far)

    return lax.fori_loop(0, count - 1, turn, so_far)


def block_forward(bc, x, dt_raw, a_log, h_in):
    length = x.shape[0]
    heads = h_in.shape[0]
    width = h_in.shape[1]
    state = h_in.shape[2]
    blocks = length // GROUP
    step = jax.nn.softplus(dt_raw)
    logdec = -step * jnp.exp(a_log)[None, :]
    b_in = bc[:, :state].astype(jnp.float32).reshape(blocks, GROUP, state)
    c_out = bc[:, state:].astype(jnp.float32).reshape(blocks, GROUP, state)
    inputs = (x.astype(jnp.float32).reshape(length, heads, width) * step[:, :, None]).reshape(
        blocks, GROUP, heads, width
    )
    decays = jnp.transpose(logdec.reshape(blocks, GROUP, heads), (0, 2, 1))
    rows = jnp.arange(GROUP, dtype=jnp.int32)
    causal = rows[:, None] >= rows[None, :]
    cum = jnp.cumsum(decays, axis=2)
    diff = cum[:, :, :, None] - cum[:, :, None, :]
    weights = jnp.exp(jnp.where(causal[None, None, :, :], diff, -jnp.inf))
    scores = jnp.einsum("ktn,ksn->kts", c_out, b_in, precision=HIGH)
    mixing = weights * scores[:, None, :, :]
    y_intra = jnp.einsum("khts,kshp->kthp", mixing, inputs, precision=HIGH)
    ends = cum[:, :, -1]
    edge = jnp.concatenate([jnp.zeros((1, heads), jnp.float32), jnp.cumsum(ends, axis=0)], axis=0)
    tail = jnp.transpose(jnp.exp(ends[:, :, None] - cum), (0, 2, 1))
    fresh = jnp.einsum("kshp,ksn->khpn", inputs * tail[:, :, :, None], b_in, precision=HIGH)
    targets = jnp.arange(blocks + 1, dtype=jnp.int32)
    sources = jnp.arange(blocks, dtype=jnp.int32)
    before = sources[None, :] < targets[:, None]
    gap = edge[:, None, :] - edge[None, 1:, :]
    carry_weight = jnp.exp(jnp.where(before[:, :, None], gap, -jnp.inf))
    starts = (
        jnp.einsum("kjh,jhpn->khpn", carry_weight, fresh, precision=HIGH)
        + jnp.exp(edge)[:, :, None, None] * h_in[None]
    )
    y_inter = (
        jnp.einsum("ktn,khpn->kthp", c_out, starts[:blocks], precision=HIGH)
        * jnp.exp(jnp.transpose(cum, (0, 2, 1)))[:, :, :, None]
    )
    return ((y_intra + y_inter).reshape(length, heads * width), starts[blocks])


def link_states(earlier, later):
    return (earlier[0] * later[0], later[0][:, None, None] * earlier[1] + later[1])


def per_device(hidden, w_bc, xs, dt_raw, a_log, d_out):
    tokens_here = hidden[0]
    channels = xs[0]
    step_raw = dt_raw[0]
    upstream = d_out[0].astype(jnp.float32)
    heads = a_log.shape[0]
    width = channels.shape[1] // heads
    state = w_bc.shape[1] // 2
    length = channels.shape[0]
    bc = jnp.dot(tokens_here, w_bc, preferred_element_type=jnp.float32).astype(jnp.bfloat16)
    zero_state = jnp.zeros((heads, width, state), jnp.float32)
    ones_heads = jnp.ones((heads,), jnp.float32)
    step_sizes = jax.nn.softplus(step_raw)
    log_decay = -step_sizes * jnp.exp(a_log)[None, :]
    running = jnp.cumsum(log_decay, axis=0)
    b_rows = bc[:, :state].astype(jnp.float32)
    c_rows = bc[:, state:].astype(jnp.float32)
    tail_weight = jnp.exp(running[-1:, :] - running) * step_sizes
    weighted = channels.astype(jnp.float32).reshape(length, heads, width) * tail_weight[:, :, None]
    own_state = jnp.einsum("thp,tn->hpn", weighted, b_rows, precision=HIGH)
    scaled_grad = upstream.reshape(length, heads, width) * jnp.exp(running)[:, :, None]
    back_term = jnp.einsum("thp,tn->hpn", scaled_grad, c_rows, precision=HIGH)
    total_decay = jnp.exp(running[-1])
    _, incoming = entering(
        (total_decay, own_state), "chain", link_states, (ones_heads, zero_state), False
    )
    _, outgoing_grad = entering(
        (total_decay, back_term), "chain", link_states, (ones_heads, zero_state), True
    )

    def whole_block(bc_in, x_in, alog_in):
        return block_forward(bc_in, x_in, step_raw, alog_in, incoming)

    _, pull_all = jax.vjp(whole_block, bc, channels, a_log)
    d_bc, d_x, d_rate = pull_all((upstream, outgoing_grad))
    d_weight = lax.dot_general(
        tokens_here, d_bc, (((0,), (0,)), ((), ())), preferred_element_type=jnp.float32
    )
    d_wbc, d_alog = lax.psum((d_weight, d_rate), ("chain", "dp"))
    return (d_x[None], d_wbc, d_alog)


def solution(mesh):
    return jax.shard_map(
        per_device,
        mesh=mesh,
        in_specs=(
            P("dp", "chain", None),
            P(),
            P("dp", "chain", None),
            P("dp", "chain", None),
            P(),
            P("dp", "chain", None),
        ),
        out_specs=(P("dp", "chain", None), P(), P()),
        check_vma=False,
    )
```

profile of v0, /device:TPU:1, one launch (start us, length us, event | category | flops | bytes accessed | tf_op | source)
XLA Modules:
  0.0 746.9 jit_solution(12456178090833216467)
XLA Ops:
  26.7 25.3 %all-gather.2 = f32[32,1,32]{2,1,0:T(1,128)S(1)} all-gather(f32[1,1,32]{2,1,0:T(1,128)S(1)} %get-tuple-element.271), channel_id=1, replica_groups=mesh['chain'=32,'dp'=4] {'chain'}, dimensions={0}, use_global_device_ids=true | all-gather | bytes 4224 | tf_op jit(solution)/shard_map/all_gather | solution.py:14
  66.5 6.4 fusion.35
  77.1 143.6 %all-gather.6.cloned.1.call-done = f32[1024,128,128]{2,1,0:T(8,128)} async-done(((f32[32,128,128]{2,1,0:T(8,128)}), f32[1024,128,128]{2,1,0:T(8,128)}) %all-gather.6.cloned.1.call-update) | async-done | bytes 67108880 | tf_op jit(solution)/shard_map/all_gather | solution.py:14
  220.7 45.3 %rev.7 = f32[32,32,128,128]{3,2,1,0:T(8,128)} reverse(f32[32,32,128,128]{3,2,1,0:T(8,128)} %bitcast.8), dimensions={0} | reverse | bytes 134217728 | tf_op jit(solution)/shard_map/rev | solution.py:16
  266.0 126.9 %while.28 = (s32[]{:T(128)}, f32[32,128,128]{2,1,0:T(8,128)}, s32[]{:T(128)}, f32[32,32]{1,0:T(8,128)S(1)}, f32[32,32,128,128]{3,2,1,0:T(8,128)}, /*index=5*/s32[]{:T(128)}, s32[]{:T(128)}) while((s32[]{:T(128)}, f32[32,128,128]{2,1,0:T(8,128)}, s32[]{:T(128)}, f32[32,32]{1,0:T(8,128)S(1)}, f32[32,32,128,128]{3,2,1,0:T(8,128)}, ...), condition=%wide.region_2.3_spmd.clone, body=%wide.region_1.2_spmd.clone.sunk | while | flops 2097156 | bytes 6291945 | solution.py:26
  281.1 5.2 fusion.121
  286.3 5.1 fusion.121
  295.3 4.3 fusion.121
  307.6 4.1 fusion.121
  319.5 4.1 fusion.121
  327.5 4.1 fusion.121
  331.6 4.1 fusion.121
  339.5 4.8 fusion.121
  352.3 4.3 fusion.121
  364.4 4.1 fusion.121
  384.3 4.6 fusion.121
  400.4 5.8 bitcast_add_fusion.2
  413.8 4.4 multiply_bitcast_fusion.1
  423.8 86.7 %while.29 = (s32[]{:T(128)}, f32[32,128,128]{2,1,0:T(8,128)S(1)}, s32[]{:T(128)}, f32[32,32]{1,0:T(8,128)}, f32[32,32,128,128]{3,2,1,0:T(8,128)}, /*index=5*/s32[]{:T(128)}, s32[]{:T(128)}) while((s32[]{:T(128)}, f32[32,128,128]{2,1,0:T(8,128)S(1)}, s32[]{:T(128)}, f32[32,32]{1,0:T(8,128)}, f32[32,32,128,128]{3,2,1,0:T(8,128)}, ...), condition=%wide.region_5.6_spmd.clone, body=%wide.region_4.5_spmd.clone.sunk | while | flops 2097156 | bytes 6291945 | solution.py:26
  515.9 51.8 %fusion.3 = f32[32,1,2,1]{2,1,3,0:T(1,128)S(1)} fusion(f32[32,128,128,1]{2,3,1,0:T(1,128)S(1)} %bitcast.247, f32[32,128,128,2]{2,1,0,3:T(8,128)S(1)} %get-tuple-element.264), kind=kOutput, calls=%fused_computation.12 | convolution fusion | flops 12582912 | bytes 6291712 | tf_op jit(solution)/shard_map/transpose(jvp(kjh,jhpn->khpn))/dot_general | solution.py:61
  568.0 5.7 fusion.36
  586.0 66.2 %psum.15 = f32[32]{0:T(128)} all-reduce(f32[32]{0:T(128)S(1)} %exponential_multiply_fusion.1), channel_id=1, replica_groups=mesh['chain'=32,'dp'=4] {'chain','dp'}, use_global_device_ids=true, to_apply=%region_17.18 | all-reduce | flops 32 | bytes 256 | tf_op jit(solution)/shard_map/psum | solution.py:113
  652.2 82.2 %all-reduce.9.cloned.1.call-done = f32[4096,256]{0,1:T(8,128)} async-done(((f32[4096,256]{0,1:T(8,128)}), f32[4096,256]{0,1:T(8,128)}) %all-reduce.9.cloned.1.call-update) | async-done | bytes 4194320 | tf_op jit(solution)/shard_map/psum | solution.py:113
  734.4 5.7 copy.81
  (245 shorter events, 240.4 us)
Async XLA Ops:
  7.2 4.6 copy-start
  7.2 4.6 copy-start.13
  7.2 213.5 %all-gather.6.cloned.1.call-start = ((), (), s32[]{:S(2)}) async-start(), calls=%async_computation.1 | async-start | bytes 69206016 | tf_op jit(solution)/shard_map/all_gather | solution.py:14
  15.9 408.0 %all-gather.8.cloned.1.call-start = ((), (), s32[]{:S(2)}) async-start(), calls=%async_computation.2 | async-start | bytes 69206016 | tf_op jit(solution)/shard_map/all_gather | solution.py:14
  23.7 710.7 %all-reduce.9.cloned.1.call-start = ((), (), s32[]{:S(2)}) async-start(), calls=%async_computation | async-start | bytes 8388608 | tf_op jit(solution)/shard_map/psum | solution.py:113
  23.8 28.3 %copy-start.18 = (f32[1,128,32]{1,2,0:T(8,128)S(1)}, f32[1,128,32]{1,2,0:T(8,128)}, u32[]{:S(2)}) copy-start(f32[1,128,32]{1,2,0:T(8,128)} %param.13) | copy-start | bytes 49156
  66.2 10.9 %copy-start.26 = (pred[2]{0:T(512)(128)(4,1)}, pred[2]{0:T(512)(128)(4,1)S(1)}, u32[]{:S(2)}) copy-start(pred[2]{0:T(512)(128)(4,1)S(1)} %iota_compare_fusion.1) | copy-start | bytes 10
  66.2 6.7 copy-start.17
  66.4 331.9 %copy-start.20 = (f32[32]{0:T(128)}, f32[32]{0:T(128)S(1)}, u32[]{:S(2)}) copy-start(f32[32]{0:T(128)S(1)} %slice_reduce_fusion) | copy-start | bytes 388
  66.5 6.6 copy-start.3
  77.1 315.8 %copy-start.24 = (f32[32,2]{0,1:T(2,128)}, f32[32,2]{0,1:T(2,128)S(1)}, u32[]{:S(2)}) copy-start(f32[32,2]{0,1:T(2,128)S(1)} %fusion.108) | copy-start | bytes 772
  392.9 2.9 copy-start.10
  510.5 3.1 copy-start.12
  510.5 3.0 copy-start.25
  515.9 51.9 %copy-start.21 = (f32[32]{0:T(128)S(1)}, f32[32]{0:T(128)}, u32[]{:S(2)}) copy-start(f32[32]{0:T(128)} %copy-done.20) | copy-start | bytes 388
  515.9 51.9 %copy-start.27 = (pred[2]{0:T(512)(128)(4,1)S(1)}, pred[2]{0:T(512)(128)(4,1)}, u32[]{:S(2)}) copy-start(pred[2]{0:T(512)(128)(4,1)} %copy-done.26) | copy-start | bytes 10
  568.0 6.0 copy-start.5
  568.0 6.0 copy-start.7
  574.0 3.5 copy-start.14
  580.9 3.5 copy-start.16
  580.9 3.6 copy-start.22
  580.9 3.6 copy-start.23
  580.9 5.1 copy-start.29
  734.4 5.7 copy-start.1
  (9 other events, 12.9 us)
Sparse Core Ops, SparseCore 0:
  16.0 204.6 all-gather.5
  223.0 199.9 all-gather.7
  580.3 154.0 all-reduce.8
where the time goes:
time: 754 us; the launch traced here: 747 us
  waiting for transfers between devices  226 us (30%)
  other arithmetic  210 us (28%)
  local copies, waits for them, and re-layouts  107 us (14%)
  matrix products  97.2 us (13%)
  blocking collectives  91.6 us (12%)
  between operations  14.4 us (2%)
    select_n x62, other arithmetic, turn(): jnp.where(position < mine, new, old)  191 us
    all_gather x2, waiting for transfers between devices, entering(): pieces = jax.tree.map(lambda part: lax.all_gather(part, axis), value)  144 us
    psum x1, waiting for transfers between devices, per_device(): d_wbc, d_alog = lax.psum((d_weight, d_rate), ('chain', 'dp'))  82.2 us
    psum x1, blocking collectives, per_device(): d_wbc, d_alog = lax.psum((d_weight, d_rate), ('chain', 'dp'))  66.2 us
    dot_general x1, matrix products, block_forward(): jnp.einsum('kjh,jhpn->khpn', carry_weight, fresh, precision=HIGH)  51.8 us
    rev x2, local copies, waits for them, and re-layouts, entering(): pieces = jax.tree.map(lambda part: part[::-1], pieces)  45.3 us
    all_gather x1, blocking collectives, entering(): pieces = jax.tree.map(lambda part: lax.all_gather(part, axis), value)  25.3 us
    mul x62, local copies, waits for them, and re-layouts, link_states(): later[0][:, None, None] * earlier[1] + later[1]  21.5 us
  transfers between devices with their start and end apart: 3, of which 2 were waited for; matrix products, arithmetic and copies ran while one was open for 32% of the time, Pallas kernels for 0%

commit v1 on v0

--- a/solution.py
+++ b/solution.py
@@ -9,21 +9,25 @@
 HIGH = lax.Precision.HIGHEST
 
 
-def entering(value, axis, join, neutral, backward):
-    count, mine = (lax.axis_size(axis), lax.axis_index(axis))
-    pieces = jax.tree.map(lambda part: lax.all_gather(part, axis), value)
-    if backward:
-        pieces = jax.tree.map(lambda part: part[::-1], pieces)
-        mine = count - 1 - mine
-    so_far = jax.tree.map(
-        lambda part, zero: jnp.full_like(part, 0) + jnp.asarray(zero, part.dtype), value, neutral
-    )
-
-    def turn(position, so_far):
-        longer = join(so_far, jax.tree.map(lambda part: part[position], pieces))
-        return jax.tree.map(lambda new, old: jnp.where(position < mine, new, old), longer, so_far)
-
-    return lax.fori_loop(0, count - 1, turn, so_far)
+def exchange(log_total, own_state, back_term):
+    count, mine = (lax.axis_size("chain"), lax.axis_index("chain"))
+    heads, width, state = own_state.shape
+    per = heads // count
+    both = jnp.stack([own_state, back_term], axis=1)
+    parts = lax.all_to_all(both, "chain", 0, 0, tiled=True).reshape(count, per, 2, width * state)
+    logs = lax.all_gather(log_total, "chain")
+    mine_logs = lax.dynamic_slice_in_dim(logs, mine * per, per, axis=1)
+    edge = jnp.cumsum(mine_logs, axis=0) - mine_logs
+    after = edge + mine_logs
+    pos = jnp.arange(count, dtype=jnp.int32)
+    earlier = pos[None, :] < pos[:, None]
+    fwd_w = jnp.exp(jnp.where(earlier[:, :, None], edge[:, None, :] - after[None, :, :], -jnp.inf))
+    bwd_w = jnp.exp(jnp.where(earlier.T[:, :, None], edge[None, :, :] - after[:, None, :], -jnp.inf))
+    inc = jnp.einsum("djh,jhx->dhx", fwd_w, parts[:, :, 0], precision=HIGH)
+    out = jnp.einsum("djh,jhx->dhx", bwd_w, parts[:, :, 1], precision=HIGH)
+    res = jnp.stack([inc, out], axis=2).reshape(count * per, 2, width, state)
+    back = lax.all_to_all(res, "chain", 0, 0, tiled=True)
+    return back[:, 0], back[:, 1]
 
 
 def block_forward(bc, x, dt_raw, a_log, h_in):
@@ -68,10 +72,6 @@
     return ((y_intra + y_inter).reshape(length, heads * width), starts[blocks])
 
 
-def link_states(earlier, later):
-    return (earlier[0] * later[0], later[0][:, None, None] * earlier[1] + later[1])
-
-
 def per_device(hidden, w_bc, xs, dt_raw, a_log, d_out):
     tokens_here = hidden[0]
     channels = xs[0]
@@ -82,8 +82,6 @@
     state = w_bc.shape[1] // 2
     length = channels.shape[0]
     bc = jnp.dot(tokens_here, w_bc, preferred_element_type=jnp.float32).astype(jnp.bfloat16)
-    zero_state = jnp.zeros((heads, width, state), jnp.float32)
-    ones_heads = jnp.ones((heads,), jnp.float32)
     step_sizes = jax.nn.softplus(step_raw)
     log_decay = -step_sizes * jnp.exp(a_log)[None, :]
     running = jnp.cumsum(log_decay, axis=0)
@@ -94,13 +92,7 @@
     own_state = jnp.einsum("thp,tn->hpn", weighted, b_rows, precision=HIGH)
     scaled_grad = upstream.reshape(length, heads, width) * jnp.exp(running)[:, :, None]
     back_term = jnp.einsum("thp,tn->hpn", scaled_grad, c_rows, precision=HIGH)
-    total_decay = jnp.exp(running[-1])
-    _, incoming = entering(
-        (total_decay, own_state), "chain", link_states, (ones_heads, zero_state), False
-    )
-    _, outgoing_grad = entering(
-        (total_decay, back_term), "chain", link_states, (ones_heads, zero_state), True
-    )
+    incoming, outgoing_grad = exchange(running[-1], own_state, back_term)
 
     def whole_block(bc_in, x_in, alog_in):
         return block_forward(bc_in, x_in, step_raw, alog_in, incoming)

time: 754 us -> 453 us (0.60)
  other arithmetic: 210 us -> 20 us
  waiting for transfers between devices: 226 us -> 106 us
  local copies, waits for them, and re-layouts: 107 us -> 60.5 us
  blocking collectives: 91.6 us -> 131 us
  starting transfers between devices: 0.12 us -> 16.6 us
    select_n x62 -> x1, other arithmetic: 191 us -> 0.05 us  [per_device(): step_sizes = jax.nn.softplus(step_raw)]
    all_gather x2 -> x0, waiting for transfers between devices: 144 us -> none  [entering(): pieces = jax.tree.map(lambda part: lax.all_gather(part, axis), value)]
    rev x2 -> x0, local copies, waits for them, and re-layouts: 45.3 us -> none  [entering(): pieces = jax.tree.map(lambda part: part[::-1], pieces)]
    all_gather x1, blocking collectives: 25.3 us -> 64.8 us  [exchange(): logs = lax.all_gather(log_total, 'chain')]
    all_to_all x0 -> x2, waiting for transfers between devices: none -> 24.2 us  [the longest x1 24.2 us: exchange(): back = lax.all_to_all(res, 'chain', 0, 0, tiled=True)]
    mul x62 -> x1, local copies, waits for them, and re-layouts: 21.5 us -> 2.75 us  [block_forward(): jnp.exp(edge)[:, :, None, None] * h_in[None]]
    all_to_all x0 -> x2, starting transfers between devices: none -> 16.6 us  [the longest x1 9.48 us: exchange(): lax.all_to_all(both, 'chain', 0, 0, tiled=True)]
    slice x0 -> x1, local copies, waits for them, and re-layouts: none -> 7.82 us  [exchange(): inc = jnp.einsum('djh,jhx->dhx', fwd_w, parts[:, :, 0], precision=HIGH)]
  transfers between devices with their start and end apart: 3 -> 3, of which waited for: 2 -> 2; matrix products, arithmetic and copies ran while one was open for 32% -> 7% of each run, Pallas kernels for 0% -> 0%
where the time goes in v1:
time: 453 us; the launch traced here: 447 us
  blocking collectives  131 us (29%)
  waiting for transfers between devices  106 us (23%)
  matrix products  98 us (22%)
  local copies, waits for them, and re-layouts  60.5 us (13%)
  other arithmetic  20 us (4%)
  starting transfers between devices  16.6 us (4%)
  between operations  14.7 us (3%)
    psum x1, waiting for transfers between devices, per_device(): d_wbc, d_alog = lax.psum((d_weight, d_rate), ('chain', 'dp'))  81.8 us
    psum x1, blocking collectives, per_device(): d_wbc, d_alog = lax.psum((d_weight, d_rate), ('chain', 'dp'))  66.6 us
    all_gather x1, blocking collectives, exchange(): logs = lax.all_gather(log_total, 'chain')  64.8 us
    dot_general x1, matrix products, block_forward(): jnp.einsum('kjh,jhpn->khpn', carry_weight, fresh, precision=HIGH)  51.8 us
    all_to_all x1, waiting for transfers between devices, exchange(): back = lax.all_to_all(res, 'chain', 0, 0, tiled=True)  24.2 us
    unnamed x70, local copies, waits for them, and re-layouts  14.3 us
    dot_general x3, matrix products, block_forward(): jnp.einsum('ktn,khpn->kthp', c_out, starts[:blocks], precision=HIGH)  13.2 us
    dot_general x2, matrix products, block_forward(): y_intra = jnp.einsum('khts,kshp->kthp', mixing, inputs, precision=HIGH)  10.7 us
  transfers between devices with their start and end apart: 3, of which 2 were waited for; matrix products, arithmetic and copies ran while one was open for 7% of the time, Pallas kernels for 0%

profile of v1, /device:TPU:1, one launch (start us, length us, event | category | flops | bytes accessed | tf_op | source)
XLA Modules:
  0.0 447.2 jit_solution(2360385607508101729)
XLA Ops:
  12.4 3.0 copy.65
  24.5 9.5 %all-to-all-start = ((f32[32,2,128,128]{3,2,1,0:T(8,128)}), f32[32,2,128,128]{3,2,1,0:T(8,128)}, u32[]{:S(2)}, u32[]{:S(2)}) async-start(f32[32,2,128,128]{3,2,1,0:T(8,128)} %copy.68), calls=%async_computation | async-start | bytes 8388608 | tf_op jit(solution)/shard_map/all_to_all | solution.py:17
  34.0 64.8 %all-gather = f32[32,1,32]{2,1,0:T(1,128)S(1)} all-gather(f32[1,1,32]{2,1,0:T(1,128)S(1)} %get-tuple-element.29), channel_id=1, replica_groups=mesh['chain'=32,'dp'=4] {'chain'}, dimensions={0}, use_global_device_ids=true | all-gather | bytes 4224 | tf_op jit(solution)/shard_map/all_gather | solution.py:18
  99.1 6.0 %reshape.570 = f32[32,1,2,16384]{3,2,0,1:T(2,128)} reshape(f32[32,2,128,128]{3,2,1,0:T(8,128)} %all-to-all-done) | data formatting | bytes 8388608 | tf_op jit(solution)/shard_map/reshape | solution.py:17
  105.1 7.8 %fusion.142 = (f32[32,1,1,16384]{3,2,0,1:T(1,128)S(1)}, f32[32,1,1,16384]{3,2,0,1:T(1,128)S(1)}) fusion(f32[32,1,2,16384]{3,2,0,1:T(2,128)} %reshape.570), kind=kLoop, calls=%fused_computation.169 | loop fusion | bytes 8388608 | tf_op jit(solution)/shard_map/slice | solution.py:26
  112.9 3.2 fusion.42
  116.2 3.3 fusion.45
  122.5 7.1 %all-to-all-start.1 = ((f32[32,2,128,128]{3,2,1,0:T(8,128)}), f32[32,2,128,128]{3,2,1,0:T(8,128)}, u32[]{:S(2)}, u32[]{:S(2)}) async-start(f32[32,2,128,128]{3,2,1,0:T(8,128)} %pad_maximum_fusion.1), calls=%async_computation.1 | async-start | bytes 8388608 | tf_op jit(solution)/shard_map/all_to_all | solution.py:29
  135.1 2.8 mul.223
  147.0 4.9 %fusion.51 = (f32[32,128]{1,0:T(8,128)}, f32[32,128]{1,0:T(8,128)}, f32[128,128]{0,1:T(8,128)S(1)}) fusion(f32[128,128]{0,1:T(8,128)S(1)} %fusion.103, f32[32,128]{1,0:T(8,128)S(1)} %bitcast.279, pred[128,128]{0,1:T(8,128)(4,1)S(1)} %iota_compare_fusion, bf16[32,128,128]{2,1,0:T(8,128)(2,1)S(1)} %bitcast.278, f32[128,32,128]{2,1,0:T(8,128)S(1)} %bitcast.272, ...), kind=kOutput, calls=%fused_computation.58 | convolution fusion | flops 810524672 | bytes 3358720 | tf_op jit(solution)/shard_map/transpose(jvp(khts,kshp->kthp))/dot_general | solution.py:54
  152.1 4.0 fusion.33
  156.1 24.2 %all-to-all-done.1 = f32[32,2,128,128]{3,2,1,0:T(8,128)} async-done(((f32[32,2,128,128]{3,2,1,0:T(8,128)}), f32[32,2,128,128]{3,2,1,0:T(8,128)}, u32[]{:S(2)}, u32[]{:S(2)}) %all-to-all-start.1) | async-done | bytes 4194336 | tf_op jit(solution)/shard_map/all_to_all | solution.py:29
  183.5 3.1 multiply_reduce_fusion
  191.2 5.8 %bitcast_add_fusion = f32[1,128,32,128]{1,3,2,0:T(8,128)} fusion(f32[32,128,128]{2,1,0:T(8,128)} %get-tuple-element.38, bf16[32,128,128]{2,1,0:T(8,128)(2,1)} %bitcast.277, f32[128,128]{0,1:T(8,128)S(1)} %fusion.103, f32[32,128]{1,0:T(8,128)S(1)} %bitcast.280, f32[128,32]{0,1:T(8,128)} %get-tuple-element.34, pred[128,128]{0,1:T(8,128)(4,1)} %copy-done.18), kind=kOutput, calls=%fused_computation.21 | convolution fusion | flops 807927808 | bytes 5357568 | tf_op jit(solution)/shard_map/transpose(jvp(khts,kshp->kthp))/dot_general | solution.py:54
  197.1 2.9 copy.83
  201.9 3.1 mul.227
  205.0 4.4 multiply_bitcast_fusion.1
  212.4 3.4 fusion.67
  219.6 51.8 %fusion.1 = f32[32,1,2,1]{2,1,3,0:T(1,128)S(1)} fusion(f32[32,128,128,1]{2,3,1,0:T(1,128)S(1)} %bitcast.273, f32[32,128,128,2]{2,1,0,3:T(8,128)S(1)} %copy-done.13), kind=kOutput, calls=%fused_computation.8 | convolution fusion | flops 12582912 | bytes 6291712 | tf_op jit(solution)/shard_map/transpose(jvp(kjh,jhpn->khpn))/dot_general | solution.py:65
  271.6 5.7 %fusion.52 = f32[128,128]{1,0:T(8,128)S(1)} fusion(f32[2,32,128,128]{3,2,1,0:T(8,128)} %multiply_bitcast_fusion, f32[128,32,128]{2,1,0:T(8,128)} %bitcast.267, f32[32,128,128]{2,1,0:T(8,128)S(1)} %get-tuple-element.21, f32[1,32]{1,0:T(1,128)S(1)} %slice.47), kind=kOutput, calls=%fused_computation.60 | convolution fusion | flops 806354944 | bytes 6357120 | tf_op jit(solution)/shard_map/transpose(jvp(ktn,khpn->kthp))/dot_general | solution.py:69
  281.0 3.5 multiply_reduce_fusion.1
  286.1 66.6 %psum.15 = f32[32]{0:T(128)} all-reduce(f32[32]{0:T(128)S(1)} %exponential_multiply_fusion.1), channel_id=1, replica_groups=mesh['chain'=32,'dp'=4] {'chain','dp'}, use_global_device_ids=true, to_apply=%region_14.15 | all-reduce | flops 32 | bytes 256 | tf_op jit(solution)/shard_map/psum | solution.py:105
  352.7 81.8 %all-reduce.9.cloned.1.call-done = f32[4096,256]{0,1:T(8,128)} async-done(((f32[4096,256]{0,1:T(8,128)}), f32[4096,256]{0,1:T(8,128)}) %all-reduce.9.cloned.1.call-update) | async-done | bytes 4194320 | tf_op jit(solution)/shard_map/psum | solution.py:105
  434.5 5.7 %copy.94 = f32[4096,256]{1,0:T(8,128)} copy(f32[4096,256]{0,1:T(8,128)} %all-reduce.9.cloned.1.call-done) | data formatting | bytes 8388608
  (128 shorter events, 54.1 us)
Async XLA Ops:
  7.2 10.0 %copy-start = (bf16[4096,256]{1,0:T(8,128)(2,1)S(1)}, bf16[4096,256]{1,0:T(8,128)(2,1)}, u32[]{:S(2)}) copy-start(bf16[4096,256]{1,0:T(8,128)(2,1)} %param.7) | copy-start | bytes 6291460
  12.4 3.1 copy-start.8
  24.5 74.6 %all-to-all-start = ((f32[32,2,128,128]{3,2,1,0:T(8,128)}), f32[32,2,128,128]{3,2,1,0:T(8,128)}, u32[]{:S(2)}, u32[]{:S(2)}) async-start(f32[32,2,128,128]{3,2,1,0:T(8,128)} %copy.68), calls=%async_computation | async-start | bytes 8388608 | tf_op jit(solution)/shard_map/all_to_all | solution.py:17
  122.5 7.2 %copy-start.9 = (bf16[1,128,4096]{2,1,0:T(8,128)(2,1)S(1)}, bf16[1,128,4096]{2,1,0:T(8,128)(2,1)}, u32[]{:S(2)}) copy-start(bf16[1,128,4096]{2,1,0:T(8,128)(2,1)} %param.11) | copy-start | bytes 3145732
  122.5 57.8 %all-to-all-start.1 = ((f32[32,2,128,128]{3,2,1,0:T(8,128)}), f32[32,2,128,128]{3,2,1,0:T(8,128)}, u32[]{:S(2)}, u32[]{:S(2)}) async-start(f32[32,2,128,128]{3,2,1,0:T(8,128)} %pad_maximum_fusion.1), calls=%async_computation.1 | async-start | bytes 8388608 | tf_op jit(solution)/shard_map/all_to_all | solution.py:29
  129.7 304.8 %all-reduce.9.cloned.1.call-start = ((), (), s32[]{:S(2)}) async-start(), calls=%async_computation.2 | async-start | bytes 8388608 | tf_op jit(solution)/shard_map/psum | solution.py:105
  144.7 7.3 %copy-start.3 = (f32[16,8,32,128]{3,2,1,0:T(8,128)}, f32[16,8,32,128]{3,2,1,0:T(8,128)S(1)}, u32[]{:S(2)}) copy-start(f32[16,8,32,128]{3,2,1,0:T(8,128)S(1)} %copy.118) | copy-start | bytes 6291460
  144.8 11.3 %copy-start.26 = (pred[2]{0:T(512)(128)(4,1)}, pred[2]{0:T(512)(128)(4,1)S(1)}, u32[]{:S(2)}) copy-start(pred[2]{0:T(512)(128)(4,1)S(1)} %iota_compare_fusion.5) | copy-start | bytes 10
  144.8 7.1 %copy-start.18 = (pred[128,128]{0,1:T(8,128)(4,1)}, pred[128,128]{0,1:T(8,128)(4,1)S(1)}, u32[]{:S(2)}) copy-start(pred[128,128]{0,1:T(8,128)(4,1)S(1)} %iota_compare_fusion) | copy-start | bytes 49156
  145.0 44.1 %copy-start.20 = (f32[32]{0:T(128)}, f32[32]{0:T(128)S(1)}, u32[]{:S(2)}) copy-start(f32[32]{0:T(128)S(1)} %slice_reduce_fusion) | copy-start | bytes 388
  156.1 27.0 %copy-start.24 = (f32[32,2]{0,1:T(2,128)}, f32[32,2]{0,1:T(2,128)S(1)}, u32[]{:S(2)}) copy-start(f32[32,2]{0,1:T(2,128)S(1)} %fusion.139) | copy-start | bytes 772
  183.5 3.1 copy-start.4
  183.5 3.2 copy-start.10
  212.4 3.5 copy-start.25
  215.9 3.7 copy-start.13
  219.6 51.9 %copy-start.21 = (f32[32]{0:T(128)S(1)}, f32[32]{0:T(128)}, u32[]{:S(2)}) copy-start(f32[32]{0:T(128)} %copy-done.20) | copy-start | bytes 388
  219.6 51.9 %copy-start.27 = (pred[2]{0:T(512)(128)(4,1)S(1)}, pred[2]{0:T(512)(128)(4,1)}, u32[]{:S(2)}) copy-start(pred[2]{0:T(512)(128)(4,1)} %copy-done.26) | copy-start | bytes 10
  219.6 52.0 %copy-start.28 = (f32[2,32]{1,0:T(2,128)S(1)}, f32[2,32]{1,0:T(2,128)}, u32[]{:S(2)}) copy-start(f32[2,32]{1,0:T(2,128)} %get-tuple-element.19) | copy-start | bytes 772
  271.6 5.9 %copy-start.14 = (bf16[1,128,4096]{2,1,0:T(8,128)(2,1)S(1)}, bf16[1,128,4096]{2,1,0:T(8,128)(2,1)}, u32[]{:S(2)}) copy-start(bf16[1,128,4096]{2,1,0:T(8,128)(2,1)} %param.6) | copy-start | bytes 3145732
  281.0 3.5 copy-start.17
  281.0 3.6 copy-start.22
  281.0 3.6 copy-start.23
  281.0 5.1 %copy-start.30 = (f32[32]{0:T(128)S(1)}, f32[32]{0:T(128)}, u32[]{:S(2)}) copy-start(f32[32]{0:T(128)} %param.10) | copy-start | bytes 388
  434.5 5.7 %copy-start.1 = (bf16[4096,256]{1,0:T(8,128)(2,1)S(1)}, bf16[4096,256]{1,0:T(8,128)(2,1)}, u32[]{:S(2)}) copy-start(bf16[4096,256]{1,0:T(8,128)(2,1)} %param.7) | copy-start | bytes 6291460
  (10 other events, 18.7 us)
Sparse Core Ops, SparseCore 0:
  280.4 154.0 all-reduce.8

commit v2 on v1

--- a/solution.py
+++ b/solution.py
@@ -13,10 +13,18 @@
     count, mine = (lax.axis_size("chain"), lax.axis_index("chain"))
     heads, width, state = own_state.shape
     per = heads // count
-    both = jnp.stack([own_state, back_term], axis=1)
-    parts = lax.all_to_all(both, "chain", 0, 0, tiled=True).reshape(count, per, 2, width * state)
-    logs = lax.all_gather(log_total, "chain")
-    mine_logs = lax.dynamic_slice_in_dim(logs, mine * per, per, axis=1)
+    size = width * state
+    both = jnp.concatenate(
+        [
+            own_state.reshape(heads, size),
+            back_term.reshape(heads, size),
+            jnp.broadcast_to(log_total[:, None], (heads, 128)),
+        ],
+        axis=1,
+    )
+    sent = lax.all_to_all(both, "chain", 0, 0, tiled=True).reshape(count, per, 2 * size + 128)
+    parts = sent[:, :, : 2 * size].reshape(count, per, 2, size)
+    mine_logs = sent[:, :, 2 * size]
     edge = jnp.cumsum(mine_logs, axis=0) - mine_logs
     after = edge + mine_logs
     pos = jnp.arange(count, dtype=jnp.int32)
@@ -102,8 +110,10 @@
     d_weight = lax.dot_general(
         tokens_here, d_bc, (((0,), (0,)), ((), ())), preferred_element_type=jnp.float32
     )
-    d_wbc, d_alog = lax.psum((d_weight, d_rate), ("chain", "dp"))
-    return (d_x[None], d_wbc, d_alog)
+    rows = d_weight.shape[0]
+    rate_rows = jnp.zeros((8, d_weight.shape[1]), jnp.float32).at[0, : heads].set(d_rate)
+    summed = lax.psum(jnp.concatenate([d_weight, rate_rows], axis=0), ("chain", "dp"))
+    return (d_x[None], summed[:rows], summed[rows, :heads])
 
 
 def solution(mesh):

time: 453 us -> 471 us (1.040)
  waiting for transfers between devices: 106 us -> 178 us
  blocking collectives: 131 us -> 60.6 us
  local copies, waits for them, and re-layouts: 60.5 us -> 87.7 us
  starting transfers between devices: 16.6 us -> 5.66 us
    psum x1, waiting for transfers between devices: 81.8 us -> 154 us  [per_device(): lax.psum(jnp.concatenate([d_weight, rate_rows], axis=0), ('chain', 'dp'))]
    psum x1 -> x0, blocking collectives: 66.6 us -> none  [per_device(): d_wbc, d_alog = lax.psum((d_weight, d_rate), ('chain', 'dp'))]
    all_gather x1 -> x0, blocking collectives: 64.8 us -> none  [exchange(): logs = lax.all_gather(log_total, 'chain')]
    all_to_all x0 -> x1, blocking collectives: none -> 60.6 us  [exchange(): lax.all_to_all(both, 'chain', 0, 0, tiled=True)]
    slice x0 -> x4, local copies, waits for them, and re-layouts: none -> 20.1 us  [the longest x1 14.1 us: exchange(): parts = sent[:, :, :2 * size].reshape(count, per, 2, size)]
    all_to_all x1 -> x0, starting transfers between devices: 9.48 us -> none  [exchange(): lax.all_to_all(both, 'chain', 0, 0, tiled=True)]
    unnamed x70 -> x80, local copies, waits for them, and re-layouts: 14.3 us -> 17.5 us
  transfers between devices with their start and end apart: 3 -> 2, of which waited for: 2 -> 2; matrix products, arithmetic and copies ran while one was open for 7% -> 5% of each run, Pallas kernels for 0% -> 0%
where the time goes in v2:
time: 471 us; the launch traced here: 463 us
  waiting for transfers between devices  178 us (38%)
  matrix products  93.7 us (20%)
  local copies, waits for them, and re-layouts  87.7 us (19%)
  blocking collectives  60.6 us (13%)
  other arithmetic  22.1 us (5%)
  between operations  14.8 us (3%)
  starting transfers between devices  5.66 us (1%)
    psum x1, waiting for transfers between devices, per_device(): lax.psum(jnp.concatenate([d_weight, rate_rows], axis=0), ('chain', 'dp'))  154 us
    all_to_all x1, blocking collectives, exchange(): lax.all_to_all(both, 'chain', 0, 0, tiled=True)  60.6 us
    dot_general x1, matrix products, block_forward(): jnp.einsum('kjh,jhpn->khpn', carry_weight, fresh, precision=HIGH)  51.6 us
    all_to_all x1, waiting for transfers between devices, exchange(): back = lax.all_to_all(res, 'chain', 0, 0, tiled=True)  24.2 us
    unnamed x80, local copies, waits for them, and re-layouts  17.5 us
    slice x1, local copies, waits for them, and re-layouts, exchange(): parts = sent[:, :, :2 * size].reshape(count, per, 2, size)  14.1 us
    dot_general x3, matrix products, block_forward(): jnp.einsum('ktn,khpn->kthp', c_out, starts[:blocks], precision=HIGH)  11.1 us
    dot_general x2, matrix products, block_forward(): y_intra = jnp.einsum('khts,kshp->kthp', mixing, inputs, precision=HIGH)  10.7 us
  transfers between devices with their start and end apart: 2, of which 2 were waited for; matrix products, arithmetic and copies ran while one was open for 5% of the time, Pallas kernels for 0%

profile of v2, /device:TPU:1, one launch (start us, length us, event | category | flops | bytes accessed | tf_op | source)
XLA Modules:
  0.0 462.7 jit_solution(10281075249835503898)
XLA Ops:
  12.4 3.0 copy.67
  24.4 3.0 all_to_all.9
  27.5 60.6 %all_to_all.14 = f32[32,1,32896]{2,1,0:T(1,128)S(1)} all-to-all(f32[32,1,32896]{2,1,0:T(1,128)S(1)} %all_to_all.9), channel_id=1, replica_groups=mesh['chain'=32,'dp'=4] {'chain'}, dimensions={0} | all-to-all | bytes 8421376 | tf_op jit(solution)/shard_map/all_to_all | solution.py:25
  90.4 14.1 %slice_reduce_fusion = f32[32,32768]{1,0:T(8,128)} fusion(f32[32,1,32896]{2,1,0:T(1,128)} %copy-done.10), kind=kLoop, calls=%fused_computation.4 | loop fusion | bytes 8388608 | tf_op jit(solution)/shard_map/slice | solution.py:26
  104.5 6.7 %reshape.636 = f32[32,1,2,16384]{3,2,0,1:T(2,128)} reshape(f32[32,32768]{1,0:T(8,128)} %slice_reduce_fusion) | data formatting | bytes 8388608 | tf_op jit(solution)/shard_map/reshape | solution.py:26
  111.3 7.8 %fusion.137 = (f32[32,1,1,16384]{3,2,0,1:T(1,128)S(1)}, f32[32,1,1,16384]{3,2,0,1:T(1,128)S(1)}) fusion(f32[32,1,2,16384]{3,2,0,1:T(2,128)} %reshape.636), kind=kLoop, calls=%fused_computation.174 | loop fusion | bytes 8388608 | tf_op jit(solution)/shard_map/slice | solution.py:34
  119.1 3.3 fusion.36
  122.7 3.2 fusion.39
  128.7 5.6 %all-to-all-start.1 = ((f32[32,2,128,128]{3,2,1,0:T(8,128)}), f32[32,2,128,128]{3,2,1,0:T(8,128)}, u32[]{:S(2)}, u32[]{:S(2)}) async-start(f32[32,2,128,128]{3,2,1,0:T(8,128)} %pad_maximum_fusion.1), calls=%async_computation.1 | async-start | bytes 8388608 | tf_op jit(solution)/shard_map/all_to_all | solution.py:37
  151.7 4.9 %fusion.45 = (f32[32,128]{1,0:T(8,128)}, f32[32,128]{1,0:T(8,128)}, f32[128,128]{0,1:T(8,128)S(1)}) fusion(f32[128,128]{0,1:T(8,128)S(1)} %fusion.97, f32[32,128]{1,0:T(8,128)S(1)} %bitcast.294, pred[128,128]{0,1:T(8,128)(4,1)S(1)} %iota_compare_fusion.1, bf16[32,128,128]{2,1,0:T(8,128)(2,1)S(1)} %bitcast.293, f32[128,32,128]{2,1,0:T(8,128)S(1)} %bitcast.285, ...), kind=kOutput, calls=%fused_computation.61 | convolution fusion | flops 810524672 | bytes 3358720 | tf_op jit(solution)/shard_map/transpose(jvp(khts,kshp->kthp))/dot_general | solution.py:62
  156.8 4.0 fusion.33
  160.8 24.2 %all-to-all-done.1 = f32[32,2,128,128]{3,2,1,0:T(8,128)} async-done(((f32[32,2,128,128]{3,2,1,0:T(8,128)}), f32[32,2,128,128]{3,2,1,0:T(8,128)}, u32[]{:S(2)}, u32[]{:S(2)}) %all-to-all-start.1) | async-done | bytes 4194336 | tf_op jit(solution)/shard_map/all_to_all | solution.py:37
  188.2 3.1 multiply_reduce_fusion
  195.9 5.8 %bitcast_add_fusion = f32[1,128,32,128]{1,3,2,0:T(8,128)} fusion(f32[32,128,128]{2,1,0:T(8,128)} %get-tuple-element.50, bf16[32,128,128]{2,1,0:T(8,128)(2,1)} %bitcast.292, f32[128,128]{0,1:T(8,128)S(1)} %fusion.97, f32[32,128]{1,0:T(8,128)S(1)} %bitcast.295, f32[128,32]{0,1:T(8,128)} %get-tuple-element.42, pred[128,128]{0,1:T(8,128)(4,1)} %copy-done.23), kind=kOutput, calls=%fused_computation.26 | convolution fusion | flops 807927808 | bytes 5357568 | tf_op jit(solution)/shard_map/transpose(jvp(khts,kshp->kthp))/dot_general | solution.py:62
  201.7 2.9 copy.83
  206.6 2.9 mul.227
  209.5 4.4 multiply_bitcast_fusion.1
  222.0 51.6 %fusion.1 = f32[32,1,2,1]{2,1,3,0:T(1,128)S(1)} fusion(f32[32,128,128,1]{2,3,1,0:T(1,128)S(1)} %bitcast.286, f32[32,128,128,2]{2,1,0,3:T(8,128)S(1)} %copy-done.18), kind=kOutput, calls=%fused_computation.11 | convolution fusion | flops 12582912 | bytes 6291712 | tf_op jit(solution)/shard_map/transpose(jvp(kjh,jhpn->khpn))/dot_general | solution.py:73
  273.9 3.6 multiply_reduce_fusion.1
  278.0 3.5 fusion.46
  281.5 3.4 fusion.61
  290.1 153.9 %all-reduce.10.cloned.1.call-done = f32[4104,256]{0,1:T(8,128)} async-done(((f32[4104,256]{0,1:T(8,128)}), f32[4104,256]{0,1:T(8,128)}) %all-reduce.10.cloned.1.call-update) | async-done | bytes 4202512 | tf_op jit(solution)/shard_map/psum | solution.py:115
  444.0 4.6 slice.83
  448.6 5.7 %copy.95 = f32[4096,256]{1,0:T(8,128)} copy(f32[4096,256]{0,1:T(8,128)} %slice.83) | data formatting | bytes 8388608
  (146 shorter events, 61.8 us)
Async XLA Ops:
  7.2 9.9 %copy-start = (bf16[4096,256]{1,0:T(8,128)(2,1)S(1)}, bf16[4096,256]{1,0:T(8,128)(2,1)}, u32[]{:S(2)}) copy-start(bf16[4096,256]{1,0:T(8,128)(2,1)} %param.9) | copy-start | bytes 6291460
  128.7 5.7 %copy-start.14 = (bf16[1,128,4096]{2,1,0:T(8,128)(2,1)S(1)}, bf16[1,128,4096]{2,1,0:T(8,128)(2,1)}, u32[]{:S(2)}) copy-start(bf16[1,128,4096]{2,1,0:T(8,128)(2,1)} %param.13) | copy-start | bytes 3145732
  128.7 56.3 %all-to-all-start.1 = ((f32[32,2,128,128]{3,2,1,0:T(8,128)}), f32[32,2,128,128]{3,2,1,0:T(8,128)}, u32[]{:S(2)}, u32[]{:S(2)}) async-start(f32[32,2,128,128]{3,2,1,0:T(8,128)} %pad_maximum_fusion.1), calls=%async_computation.1 | async-start | bytes 8388608 | tf_op jit(solution)/shard_map/all_to_all | solution.py:37
  134.3 309.7 %all-reduce.10.cloned.1.call-start = ((), (), s32[]{:S(2)}) async-start(), calls=%async_computation.2 | async-start | bytes 8650752 | tf_op jit(solution)/shard_map/psum | solution.py:115
  149.5 7.3 %copy-start.3 = (f32[16,8,32,128]{3,2,1,0:T(8,128)}, f32[16,8,32,128]{3,2,1,0:T(8,128)S(1)}, u32[]{:S(2)}) copy-start(f32[16,8,32,128]{3,2,1,0:T(8,128)S(1)} %copy.123) | copy-start | bytes 6291460
  149.5 11.3 %copy-start.31 = (pred[2]{0:T(512)(128)(4,1)}, pred[2]{0:T(512)(128)(4,1)S(1)}, u32[]{:S(2)}) copy-start(pred[2]{0:T(512)(128)(4,1)S(1)} %iota_compare_fusion.6) | copy-start | bytes 10
  149.5 7.1 %copy-start.23 = (pred[128,128]{0,1:T(8,128)(4,1)}, pred[128,128]{0,1:T(8,128)(4,1)S(1)}, u32[]{:S(2)}) copy-start(pred[128,128]{0,1:T(8,128)(4,1)S(1)} %iota_compare_fusion.1) | copy-start | bytes 49156
  149.7 44.1 %copy-start.25 = (f32[32]{0:T(128)}, f32[32]{0:T(128)S(1)}, u32[]{:S(2)}) copy-start(f32[32]{0:T(128)S(1)} %slice_reduce_fusion.2) | copy-start | bytes 388
  160.8 26.9 %copy-start.29 = (f32[32,2]{0,1:T(2,128)}, f32[32,2]{0,1:T(2,128)S(1)}, u32[]{:S(2)}) copy-start(f32[32,2]{0,1:T(2,128)S(1)} %fusion.134) | copy-start | bytes 772
  218.3 3.7 copy-start.18
  222.0 51.7 %copy-start.26 = (f32[32]{0:T(128)S(1)}, f32[32]{0:T(128)}, u32[]{:S(2)}) copy-start(f32[32]{0:T(128)} %copy-done.25) | copy-start | bytes 388
  222.0 51.7 %copy-start.32 = (pred[2]{0:T(512)(128)(4,1)S(1)}, pred[2]{0:T(512)(128)(4,1)}, u32[]{:S(2)}) copy-start(pred[2]{0:T(512)(128)(4,1)} %copy-done.31) | copy-start | bytes 10
  222.0 51.8 %copy-start.33 = (f32[2,32]{1,0:T(2,128)S(1)}, f32[2,32]{1,0:T(2,128)}, u32[]{:S(2)}) copy-start(f32[2,32]{1,0:T(2,128)} %get-tuple-element.29) | copy-start | bytes 772
  273.9 3.7 copy-start.4
  273.9 4.1 copy-start.11
  277.9 3.5 copy-start.6
  277.9 3.5 copy-start.8
  281.5 3.5 copy-start.34
  281.5 3.9 copy-start.22
  281.5 3.9 copy-start.27
  281.5 3.9 copy-start.28
  281.5 5.4 %copy-start.35 = (f32[32]{0:T(128)S(1)}, f32[32]{0:T(128)}, u32[]{:S(2)}) copy-start(f32[32]{0:T(128)} %param.12) | copy-start | bytes 388
  281.5 5.5 %copy-start.19 = (bf16[1,128,4096]{2,1,0:T(8,128)(2,1)S(1)}, bf16[1,128,4096]{2,1,0:T(8,128)(2,1)}, u32[]{:S(2)}) copy-start(bf16[1,128,4096]{2,1,0:T(8,128)(2,1)} %param.8) | copy-start | bytes 3145732
  448.6 7.1 %copy-start.1 = (bf16[4096,256]{1,0:T(8,128)(2,1)S(1)}, bf16[4096,256]{1,0:T(8,128)(2,1)}, u32[]{:S(2)}) copy-start(bf16[4096,256]{1,0:T(8,128)(2,1)} %param.9) | copy-start | bytes 6291460
  (14 other events, 30.7 us)
Sparse Core Ops, SparseCore 0:
  290.2 153.7 all-reduce.9

commit v3 on v1

--- a/solution.py
+++ b/solution.py
@@ -35,41 +35,29 @@
     heads = h_in.shape[0]
     width = h_in.shape[1]
     state = h_in.shape[2]
-    blocks = length // GROUP
     step = jax.nn.softplus(dt_raw)
     logdec = -step * jnp.exp(a_log)[None, :]
-    b_in = bc[:, :state].astype(jnp.float32).reshape(blocks, GROUP, state)
-    c_out = bc[:, state:].astype(jnp.float32).reshape(blocks, GROUP, state)
-    inputs = (x.astype(jnp.float32).reshape(length, heads, width) * step[:, :, None]).reshape(
-        blocks, GROUP, heads, width
+    b_in = bc[:, :state].astype(jnp.float32)
+    c_out = bc[:, state:].astype(jnp.float32)
+    inputs = x.astype(jnp.float32).reshape(length, heads, width) * step[:, :, None]
+    decays = jnp.transpose(logdec, (1, 0))
+    rows = jnp.arange(length, dtype=jnp.int32)
+    causal = rows[:, None] >= rows[None, :]
+    cum = jnp.cumsum(decays, axis=1)
+    diff = cum[:, :, None] - cum[:, None, :]
+    weights = jnp.exp(jnp.where(causal[None, :, :], diff, -jnp.inf))
+    scores = jnp.einsum("tn,sn->ts", c_out, b_in, precision=HIGH)
+    mixing = weights * scores[None, :, :]
+    y_intra = jnp.einsum("hts,shp->thp", mixing, inputs, precision=HIGH)
+    ends = cum[:, -1]
+    tail = jnp.transpose(jnp.exp(ends[:, None] - cum), (1, 0))
+    fresh = jnp.einsum("shp,sn->hpn", inputs * tail[:, :, None], b_in, precision=HIGH)
+    h_end = fresh + jnp.exp(ends)[:, None, None] * h_in
+    y_inter = (
+        jnp.einsum("tn,hpn->thp", c_out, h_in, precision=HIGH)
+        * jnp.exp(jnp.transpose(cum, (1, 0)))[:, :, None]
     )
-    decays = jnp.transpose(logdec.reshape(blocks, GROUP, heads), (0, 2, 1))
-    rows = jnp.arange(GROUP, dtype=jnp.int32)
-    causal = rows[:, None] >= rows[None, :]
-    cum = jnp.cumsum(decays, axis=2)
-    diff = cum[:, :, :, None] - cum[:, :, None, :]
-    weights = jnp.exp(jnp.where(causal[None, None, :, :], diff, -jnp.inf))
-    scores = jnp.einsum("ktn,ksn->kts", c_out, b_in, precision=HIGH)
-    mixing = weights * scores[:, None, :, :]
-    y_intra = jnp.einsum("khts,kshp->kthp", mixing, inputs, precision=HIGH)
-    ends = cum[:, :, -1]
-    edge = jnp.concatenate([jnp.zeros((1, heads), jnp.float32), jnp.cumsum(ends, axis=0)], axis=0)
-    tail = jnp.transpose(jnp.exp(ends[:, :, None] - cum), (0, 2, 1))
-    fresh = jnp.einsum("kshp,ksn->khpn", inputs * tail[:, :, :, None], b_in, precision=HIGH)
-    targets = jnp.arange(blocks + 1, dtype=jnp.int32)
-    sources = jnp.arange(blocks, dtype=jnp.int32)
-    before = sources[None, :] < targets[:, None]
-    gap = edge[:, None, :] - edge[None, 1:, :]
-    carry_weight = jnp.exp(jnp.where(before[:, :, None], gap, -jnp.inf))
-    starts = (
-        jnp.einsum("kjh,jhpn->khpn", carry_weight, fresh, precision=HIGH)
-        + jnp.exp(edge)[:, :, None, None] * h_in[None]
-    )
-    y_inter = (
-        jnp.einsum("ktn,khpn->kthp", c_out, starts[:blocks], precision=HIGH)
-        * jnp.exp(jnp.transpose(cum, (0, 2, 1)))[:, :, :, None]
-    )
-    return ((y_intra + y_inter).reshape(length, heads * width), starts[blocks])
+    return ((y_intra + y_inter).reshape(length, heads * width), h_end)
 
 
 def per_device(hidden, w_bc, xs, dt_raw, a_log, d_out):

time: 453 us -> 385 us (0.85)
  matrix products: 98 us -> 37.1 us
  waiting for transfers between devices: 106 us -> 120 us
  local copies, waits for them, and re-layouts: 60.5 us -> 47.6 us
  other arithmetic: 20 us -> 11.9 us
    dot_general x12 -> x9, matrix products: 84.7 us -> 23.9 us  [the longest x2 8.82 us: block_forward(): jnp.einsum('shp,sn->hpn', inputs * tail[:, :, None], b_in, precision=HIGH)]
    all_to_all x1, waiting for transfers between devices: 24.2 us -> 40.9 us  [exchange(): back = lax.all_to_all(res, 'chain', 0, 0, tiled=True)]
    mul x8 -> x4, local copies, waits for them, and re-layouts: 13.4 us -> 9.45 us  [the longest x2 4.87 us: block_forward(): jnp.einsum('tn,hpn->thp', c_out, h_in, precision=HIGH)]
    unnamed x70 -> x53, local copies, waits for them, and re-layouts: 14.3 us -> 11.7 us
  transfers between devices with their start and end apart: 3 -> 3, of which waited for: 2 -> 2; matrix products, arithmetic and copies ran while one was open for 7% -> 5% of each run, Pallas kernels for 0% -> 0%
where the time goes in v3:
time: 385 us; the launch traced here: 380 us
  blocking collectives  132 us (34%)
  waiting for transfers between devices  120 us (31%)
  local copies, waits for them, and re-layouts  47.6 us (12%)
  matrix products  37.1 us (10%)
  starting transfers between devices  16.5 us (4%)
  between operations  14.7 us (4%)
  other arithmetic  11.9 us (3%)
    psum x1, waiting for transfers between devices, per_device(): d_wbc, d_alog = lax.psum((d_weight, d_rate), ('chain', 'dp'))  79.5 us
    psum x1, blocking collectives, per_device(): d_wbc, d_alog = lax.psum((d_weight, d_rate), ('chain', 'dp'))  67.2 us
    all_gather x1, blocking collectives, exchange(): logs = lax.all_gather(log_total, 'chain')  64.8 us
    all_to_all x1, waiting for transfers between devices, exchange(): back = lax.all_to_all(res, 'chain', 0, 0, tiled=True)  40.9 us
    unnamed x53, local copies, waits for them, and re-layouts  11.7 us
    all_to_all x1, starting transfers between devices, exchange(): lax.all_to_all(both, 'chain', 0, 0, tiled=True)  9.48 us
    dot_general x2, matrix products, block_forward(): jnp.einsum('shp,sn->hpn', inputs * tail[:, :, None], b_in, precision=HIGH)  8.82 us
    slice x1, local copies, waits for them, and re-layouts, exchange(): inc = jnp.einsum('djh,jhx->dhx', fwd_w, parts[:, :, 0], precision=HIGH)  7.82 us
  transfers between devices with their start and end apart: 3, of which 2 were waited for; matrix products, arithmetic and copies ran while one was open for 5% of the time, Pallas kernels for 0%

profile of v3, /device:TPU:1, one launch (start us, length us, event | category | flops | bytes accessed | tf_op | source)
XLA Modules:
  0.0 380.3 jit_solution(4541985935464102691)
XLA Ops:
  7.2 2.7 copy.109
  17.0 2.3 copy.114
  19.3 9.5 %all-to-all-start = ((f32[32,2,128,128]{3,2,1,0:T(8,128)}), f32[32,2,128,128]{3,2,1,0:T(8,128)}, u32[]{:S(2)}, u32[]{:S(2)}) async-start(f32[32,2,128,128]{3,2,1,0:T(8,128)} %copy.114), calls=%async_computation | async-start | bytes 8388608 | tf_op jit(solution)/shard_map/all_to_all | solution.py:17
  28.8 64.8 %all-gather = f32[32,1,32]{2,1,0:T(1,128)S(1)} all-gather(f32[1,1,32]{2,1,0:T(1,128)S(1)} %get-tuple-element.30), channel_id=1, replica_groups=mesh['chain'=32,'dp'=4] {'chain'}, dimensions={0}, use_global_device_ids=true | all-gather | bytes 4224 | tf_op jit(solution)/shard_map/all_gather | solution.py:18
  93.8 6.3 %reshape.316 = f32[32,1,2,16384]{3,2,0,1:T(2,128)} reshape(f32[32,2,128,128]{3,2,1,0:T(8,128)} %all-to-all-done) | data formatting | bytes 8388608 | tf_op jit(solution)/shard_map/reshape | solution.py:17
  100.2 7.8 %fusion.101 = (f32[32,1,1,16384]{3,2,0,1:T(1,128)S(1)}, f32[32,1,1,16384]{3,2,0,1:T(1,128)S(1)}) fusion(f32[32,1,2,16384]{3,2,0,1:T(2,128)} %reshape.316), kind=kLoop, calls=%fused_computation.129 | loop fusion | bytes 8388608 | tf_op jit(solution)/shard_map/slice | solution.py:26
  108.0 3.3 fusion.31
  111.7 3.3 fusion.28
  117.6 6.9 %all-to-all-start.1 = ((f32[32,2,128,128]{3,2,1,0:T(8,128)}), f32[32,2,128,128]{3,2,1,0:T(8,128)}, u32[]{:S(2)}, u32[]{:S(2)}) async-start(f32[32,2,128,128]{3,2,1,0:T(8,128)} %pad_maximum_fusion.1), calls=%async_computation.1 | async-start | bytes 8388608 | tf_op jit(solution)/shard_map/all_to_all | solution.py:29
  125.3 3.2 fusion.38
  131.4 2.9 copy.132
  134.4 40.9 %all-to-all-done.1 = f32[32,2,128,128]{3,2,1,0:T(8,128)} async-done(((f32[32,2,128,128]{3,2,1,0:T(8,128)}), f32[32,2,128,128]{3,2,1,0:T(8,128)}, u32[]{:S(2)}, u32[]{:S(2)}) %all-to-all-start.1) | async-done | bytes 4194336 | tf_op jit(solution)/shard_map/all_to_all | solution.py:29
  175.2 2.7 fusion.1
  178.7 4.0 %multiply_reduce_fusion.1 = (f32[128,32]{0,1:T(8,128)S(1)}, f32[128,32,128]{0,2,1:T(8,128)}) fusion(f32[128,32,128]{0,2,1:T(8,128)S(1)} %bitcast.193, f32[128,32]{0,1:T(8,128)S(1)} %copy.127, f32[32,2,128,128]{3,2,1,0:T(8,128)} %all-to-all-done.1, bf16[128,256]{1,0:T(8,128)(2,1)S(1)} %convolution_convert_fusion), kind=kOutput, calls=%fused_computation.28 | convolution fusion | flops 806875136 | bytes 6356992 | tf_op jit(solution)/shard_map/transpose(jvp(shp,sn->hpn))/dot_general | solution.py:54
  182.9 2.6 multiply_reduce_fusion
  187.1 3.1 copy.133
  194.8 2.9 mul.146
  200.2 4.8 %fusion.42 = f32[128,128]{1,0:T(8,128)S(1)} fusion(f32[32,2,128,128]{3,2,1,0:T(8,128)} %all-to-all-done.1, f32[128,32,128]{2,1,0:T(8,128)S(1)} %bitcast.198), kind=kOutput, calls=%fused_computation.48 | convolution fusion | flops 805306368 | bytes 4259840 | tf_op jit(solution)/shard_map/transpose(jvp(shp,sn->hpn))/dot_general | solution.py:54
  205.2 5.0 %fusion.39 = f32[128,128]{1,0:T(8,128)S(1)} fusion(f32[32,2,128,128]{3,2,1,0:T(8,128)} %all-to-all-done.1, f32[128,32,128]{2,1,0:T(8,128)S(1)} %bitcast.199), kind=kOutput, calls=%fused_computation.47 | convolution fusion | flops 805306368 | bytes 4259840 | tf_op jit(solution)/shard_map/transpose(jvp(tn,hpn->thp))/dot_general | solution.py:57
  210.4 2.7 convolution_bitcast_fusion
  214.7 67.2 %psum.15 = f32[32]{0:T(128)} all-reduce(f32[32]{0:T(128)S(1)} %exponential_multiply_fusion.1), channel_id=1, replica_groups=mesh['chain'=32,'dp'=4] {'chain','dp'}, use_global_device_ids=true, to_apply=%region_13.14 | all-reduce | flops 32 | bytes 256 | tf_op jit(solution)/shard_map/psum | solution.py:93
  282.0 3.7 fusion.12
  287.9 79.5 %all-reduce.5.cloned.1.call-done = f32[4096,256]{0,1:T(8,128)} async-done(((f32[4096,256]{0,1:T(8,128)}), f32[4096,256]{0,1:T(8,128)}) %all-reduce.5.cloned.1.call-update) | async-done | bytes 4194320 | tf_op jit(solution)/shard_map/psum | solution.py:93
  367.4 5.7 %copy.142 = f32[4096,256]{1,0:T(8,128)} copy(f32[4096,256]{0,1:T(8,128)} %all-reduce.5.cloned.1.call-done) | data formatting | bytes 8388608
  (96 shorter events, 27.6 us)
Async XLA Ops:
  7.2 4.9 %copy-start = (bf16[4096,256]{1,0:T(8,128)(2,1)S(1)}, bf16[4096,256]{1,0:T(8,128)(2,1)}, u32[]{:S(2)}) copy-start(bf16[4096,256]{1,0:T(8,128)(2,1)} %param.7) | copy-start | bytes 6291460
  7.2 2.7 copy-start.15
  7.2 2.8 copy-start.20
  13.8 1.6 copy-start.2
  19.3 74.6 %all-to-all-start = ((f32[32,2,128,128]{3,2,1,0:T(8,128)}), f32[32,2,128,128]{3,2,1,0:T(8,128)}, u32[]{:S(2)}, u32[]{:S(2)}) async-start(f32[32,2,128,128]{3,2,1,0:T(8,128)} %copy.114), calls=%async_computation | async-start | bytes 8388608 | tf_op jit(solution)/shard_map/all_to_all | solution.py:17
  117.6 57.6 %all-to-all-start.1 = ((f32[32,2,128,128]{3,2,1,0:T(8,128)}), f32[32,2,128,128]{3,2,1,0:T(8,128)}, u32[]{:S(2)}, u32[]{:S(2)}) async-start(f32[32,2,128,128]{3,2,1,0:T(8,128)} %pad_maximum_fusion.1), calls=%async_computation.1 | async-start | bytes 8388608 | tf_op jit(solution)/shard_map/all_to_all | solution.py:29
  124.6 242.9 %all-reduce.5.cloned.1.call-start = ((), (), s32[]{:S(2)}) async-start(), calls=%async_computation.2 | async-start | bytes 8388608 | tf_op jit(solution)/shard_map/psum | solution.py:93
  125.0 3.5 copy-start.11
  125.2 3.3 copy-start.16
  125.3 3.2 copy-start.13
  134.4 48.4 %copy-start.18 = (f32[32]{0:T(128)}, f32[32]{0:T(128)S(1)}, u32[]{:S(2)}) copy-start(f32[32]{0:T(128)S(1)} %slice_bitcast_fusion.12) | copy-start | bytes 388
  182.8 2.7 copy-start.6
  182.8 2.7 copy-start.7
  182.8 2.7 copy-start.8
  182.9 2.7 copy-start.19
  185.6 4.6 %copy-start.9 = (f32[128,32]{0,1:T(8,128)}, f32[128,32]{0,1:T(8,128)S(1)}, u32[]{:S(2)}) copy-start(f32[128,32]{0,1:T(8,128)S(1)} %copy.124) | copy-start | bytes 49156
  187.1 3.1 copy-start.3
  205.2 5.2 %copy-start.4 = (bf16[1,128,4096]{2,1,0:T(8,128)(2,1)S(1)}, bf16[1,128,4096]{2,1,0:T(8,128)(2,1)}, u32[]{:S(2)}) copy-start(bf16[1,128,4096]{2,1,0:T(8,128)(2,1)} %param.6) | copy-start | bytes 3145732
  213.2 68.8 %copy-start.5 = (f32[128,32,128]{0,2,1:T(8,128)S(1)}, f32[128,32,128]{0,2,1:T(8,128)}, u32[]{:S(2)}) copy-start(f32[128,32,128]{0,2,1:T(8,128)} %get-tuple-element.35) | copy-start | bytes 6291460
  213.2 68.8 %copy-start.10 = (f32[128,32]{0,1:T(8,128)S(1)}, f32[128,32]{0,1:T(8,128)}, u32[]{:S(2)}) copy-start(f32[128,32]{0,1:T(8,128)} %copy-done.9) | copy-start | bytes 49156
  213.2 68.8 %copy-start.12 = (f32[32,128]{1,0:T(8,128)S(1)}, f32[32,128]{1,0:T(8,128)}, u32[]{:S(2)}) copy-start(f32[32,128]{1,0:T(8,128)} %copy-done.11) | copy-start | bytes 49156
  213.2 68.8 %copy-start.14 = (f32[128,128]{0,1:T(8,128)S(1)}, f32[128,128]{0,1:T(8,128)}, u32[]{:S(2)}) copy-start(f32[128,128]{0,1:T(8,128)} %copy-done.13) | copy-start | bytes 196612
  213.2 68.8 %copy-start.17 = (pred[128,128]{0,1:T(8,128)(4,1)S(1)}, pred[128,128]{0,1:T(8,128)(4,1)}, u32[]{:S(2)}) copy-start(pred[128,128]{0,1:T(8,128)(4,1)} %copy-done.16) | copy-start | bytes 49156
  367.4 5.7 %copy-start.1 = (bf16[4096,256]{1,0:T(8,128)(2,1)S(1)}, bf16[4096,256]{1,0:T(8,128)(2,1)}, u32[]{:S(2)}) copy-start(bf16[4096,256]{1,0:T(8,128)(2,1)} %param.7) | copy-start | bytes 6291460
  (1 other events, 1.5 us)
Sparse Core Ops, SparseCore 0:
  213.4 154.0 all-reduce.4

commit v4 on v3

--- a/solution.py
+++ b/solution.py
@@ -13,10 +13,13 @@
     count, mine = (lax.axis_size("chain"), lax.axis_index("chain"))
     heads, width, state = own_state.shape
     per = heads // count
-    both = jnp.stack([own_state, back_term], axis=1)
-    parts = lax.all_to_all(both, "chain", 0, 0, tiled=True).reshape(count, per, 2, width * state)
-    logs = lax.all_gather(log_total, "chain")
-    mine_logs = lax.dynamic_slice_in_dim(logs, mine * per, per, axis=1)
+    marks = jnp.broadcast_to(log_total[:, None, None], (heads, 8, state))
+    both = jnp.stack(
+        [jnp.concatenate([own_state, marks], axis=1), jnp.concatenate([back_term, marks], axis=1)], axis=1
+    )
+    sent = lax.all_to_all(both, "chain", 0, 0, tiled=True).reshape(count, per, 2, width + 8, state)
+    parts = sent[:, :, :, :width].reshape(count, per, 2, width * state)
+    mine_logs = sent[:, :, 0, width, 0]
     edge = jnp.cumsum(mine_logs, axis=0) - mine_logs
     after = edge + mine_logs
     pos = jnp.arange(count, dtype=jnp.int32)

time: 385 us -> 379 us (0.984)
  starting transfers between devices: 16.5 us -> 5 us
  local copies, waits for them, and re-layouts: 47.6 us -> 53 us
    all_gather x1 -> x0, blocking collectives: 64.8 us -> none  [exchange(): logs = lax.all_gather(log_total, 'chain')]
    all_to_all x0 -> x1, blocking collectives: none -> 63 us  [exchange(): lax.all_to_all(both, 'chain', 0, 0, tiled=True)]
    all_to_all x1 -> x0, starting transfers between devices: 9.48 us -> none  [exchange(): lax.all_to_all(both, 'chain', 0, 0, tiled=True)]
    unnamed x53 -> x48, local copies, waits for them, and re-layouts: 11.7 us -> 16.1 us
  transfers between devices with their start and end apart: 3 -> 2, of which waited for: 2 -> 2; matrix products, arithmetic and copies ran while one was open for 5% -> 5% of each run, Pallas kernels for 0% -> 0%
where the time goes in v4:
time: 379 us; the launch traced here: 374 us
  blocking collectives  130 us (34%)
  waiting for transfers between devices  119 us (31%)
  local copies, waits for them, and re-layouts  53 us (14%)
  matrix products  39.3 us (10%)
  between operations  14.7 us (4%)
  other arithmetic  12.7 us (3%)
  starting transfers between devices  5 us (1%)
    psum x1, waiting for transfers between devices, per_device(): d_wbc, d_alog = lax.psum((d_weight, d_rate), ('chain', 'dp'))  79.6 us
    psum x1, blocking collectives, per_device(): d_wbc, d_alog = lax.psum((d_weight, d_rate), ('chain', 'dp'))  67.2 us
    all_to_all x1, blocking collectives, exchange(): lax.all_to_all(both, 'chain', 0, 0, tiled=True)  63 us
    all_to_all x1, waiting for transfers between devices, exchange(): back = lax.all_to_all(res, 'chain', 0, 0, tiled=True)  39.4 us
    unnamed x48, local copies, waits for them, and re-layouts  16.1 us
    slice x1, local copies, waits for them, and re-layouts, exchange(): inc = jnp.einsum('djh,jhx->dhx', fwd_w, parts[:, :, 0], precision=HIGH)  9.86 us
    dot_general x2, matrix products, block_forward(): jnp.einsum('shp,sn->hpn', inputs * tail[:, :, None], b_in, precision=HIGH)  8.98 us
  transfers between devices with their start and end apart: 2, of which 2 were waited for; matrix products, arithmetic and copies ran while one was open for 5% of the time, Pallas kernels for 0%

profile of v4, /device:TPU:1, one launch (start us, length us, event | category | flops | bytes accessed | tf_op | source)
XLA Modules:
  0.0 373.9 jit_solution(9224759551163795798)
XLA Ops:
  9.2 2.6 copy.101
  18.7 63.0 %all_to_all.10 = f32[32,2,136,128]{3,2,1,0:T(8,128)S(1)} all-to-all(f32[32,2,136,128]{3,2,1,0:T(8,128)S(1)} %copy.106), channel_id=1, replica_groups=mesh['chain'=32,'dp'=4] {'chain'}, dimensions={0} | all-to-all | bytes 8912896 | tf_op jit(solution)/shard_map/all_to_all | solution.py:20
  82.1 2.6 slice.46
  84.7 6.3 %reshape.367 = f32[32,1,2,16384]{3,2,0,1:T(2,128)} reshape(f32[32,1,2,128,128]{4,3,2,0,1:T(8,128)} %slice.46) | data formatting | bytes 8388608 | tf_op jit(solution)/shard_map/reshape | solution.py:21
  91.0 9.9 %fusion.101 = (f32[32,1,1,16384]{3,2,0,1:T(1,128)}, f32[32,1,1,16384]{3,2,0,1:T(1,128)}) fusion(f32[32,1,2,16384]{3,2,0,1:T(2,128)} %reshape.367), kind=kLoop, calls=%fused_computation.130 | loop fusion | bytes 8388608 | tf_op jit(solution)/shard_map/slice | solution.py:29
  101.0 4.8 %fusion.27 = f32[4,8,128,128]{3,1,2,0:T(8,128)S(1)} fusion(f32[32,1,1,16384]{3,2,0,1:T(1,128)} %get-tuple-element.25, f32[32]{0:T(128)S(1)} %get-tuple-element.21, f32[32]{0:T(128)S(1)} %get-tuple-element.22), kind=kOutput, calls=%fused_computation.44 | convolution fusion | flops 201329664 | bytes 4194560 | tf_op jit(solution)/shard_map/djh,jhx->dhx/dot_general | solution.py:29
  107.4 3.3 fusion.30
  111.0 2.3 pad_maximum_fusion.1
  113.3 5.0 %all-to-all-start.1 = ((f32[32,2,128,128]{3,2,1,0:T(8,128)}), f32[32,2,128,128]{3,2,1,0:T(8,128)}, u32[]{:S(2)}, u32[]{:S(2)}) async-start(f32[32,2,128,128]{3,2,1,0:T(8,128)} %pad_maximum_fusion.1), calls=%async_computation.1 | async-start | bytes 8388608 | tf_op jit(solution)/shard_map/all_to_all | solution.py:32
  119.1 3.8 %fusion.36 = (f32[32,128]{1,0:T(8,128)}, f32[32,128]{1,0:T(8,128)}, f32[128,128]{0,1:T(8,128)S(1)}) fusion(f32[128,128]{0,1:T(8,128)S(1)} %fusion.75, f32[32,128]{1,0:T(8,128)S(1)} %reduce_window_sum.41, pred[128,128]{0,1:T(8,128)(4,1)S(1)} %iota_compare_fusion, bf16[32,128,128]{2,1,0:T(8,128)(2,1)S(1)} %bitcast.196, f32[128,32,128]{0,2,1:T(8,128)S(1)} %bitcast.191, ...), kind=kOutput, calls=%fused_computation.47 | convolution fusion | flops 810524672 | bytes 3358720 | tf_op jit(solution)/shard_map/transpose(jvp(hts,shp->thp))/dot_general | solution.py:54
  126.6 2.9 copy.122
  129.5 39.4 %all-to-all-done.1 = f32[32,2,128,128]{3,2,1,0:T(8,128)} async-done(((f32[32,2,128,128]{3,2,1,0:T(8,128)}), f32[32,2,128,128]{3,2,1,0:T(8,128)}, u32[]{:S(2)}, u32[]{:S(2)}) %all-to-all-start.1) | async-done | bytes 4194336 | tf_op jit(solution)/shard_map/all_to_all | solution.py:32
  168.9 4.0 %multiply_reduce_fusion.1 = (f32[128,32]{0,1:T(8,128)S(1)}, f32[128,32,128]{0,2,1:T(8,128)}) fusion(f32[128,32,128]{0,2,1:T(8,128)S(1)} %bitcast.192, f32[128,32]{0,1:T(8,128)S(1)} %copy.117, f32[32,2,128,128]{3,2,1,0:T(8,128)} %all-to-all-done.1, bf16[128,256]{1,0:T(8,128)(2,1)S(1)} %convolution_convert_fusion), kind=kOutput, calls=%fused_computation.32 | convolution fusion | flops 806875136 | bytes 6356992 | tf_op jit(solution)/shard_map/transpose(jvp(shp,sn->hpn))/dot_general | solution.py:57
  173.0 2.7 fusion.3
  175.9 2.6 multiply_reduce_fusion
  186.7 3.2 copy.123
  193.7 4.8 %fusion.37 = f32[128,128]{1,0:T(8,128)S(1)} fusion(f32[32,2,128,128]{3,2,1,0:T(8,128)} %all-to-all-done.1, f32[128,32,128]{2,1,0:T(8,128)S(1)} %bitcast.199), kind=kOutput, calls=%fused_computation.49 | convolution fusion | flops 805306368 | bytes 4259840 | tf_op jit(solution)/shard_map/transpose(jvp(tn,hpn->thp))/dot_general | solution.py:60
  198.8 5.0 %fusion.40 = f32[128,128]{1,0:T(8,128)S(1)} fusion(f32[32,2,128,128]{3,2,1,0:T(8,128)} %all-to-all-done.1, f32[128,32,128]{2,1,0:T(8,128)S(1)} %bitcast.200), kind=kOutput, calls=%fused_computation.50 | convolution fusion | flops 805306368 | bytes 4259840 | tf_op jit(solution)/shard_map/transpose(jvp(shp,sn->hpn))/dot_general | solution.py:57
  204.0 2.7 convolution_bitcast_fusion
  208.2 67.2 %psum.15 = f32[32]{0:T(128)} all-reduce(f32[32]{0:T(128)S(1)} %exponential_multiply_fusion.1), channel_id=1, replica_groups=mesh['chain'=32,'dp'=4] {'chain','dp'}, use_global_device_ids=true, to_apply=%region_13.14 | all-reduce | flops 32 | bytes 256 | tf_op jit(solution)/shard_map/psum | solution.py:96
  275.5 3.7 fusion.14
  279.2 2.3 copy.131
  281.4 79.6 %all-reduce.5.cloned.1.call-done = f32[4096,256]{0,1:T(8,128)} async-done(((f32[4096,256]{0,1:T(8,128)}), f32[4096,256]{0,1:T(8,128)}) %all-reduce.5.cloned.1.call-update) | async-done | bytes 4194320 | tf_op jit(solution)/shard_map/psum | solution.py:96
  361.0 5.7 %copy.132 = f32[4096,256]{1,0:T(8,128)} copy(f32[4096,256]{0,1:T(8,128)} %all-reduce.5.cloned.1.call-done) | data formatting | bytes 8388608
  (94 shorter events, 30.0 us)
Async XLA Ops:
  7.2 6.3 %copy-start = (bf16[4096,256]{1,0:T(8,128)(2,1)S(1)}, bf16[4096,256]{1,0:T(8,128)(2,1)}, u32[]{:S(2)}) copy-start(bf16[4096,256]{1,0:T(8,128)(2,1)} %param.7) | copy-start | bytes 6291460
  13.5 1.9 copy-start.2
  105.8 1.6 copy-start.5
  113.3 5.7 %copy-start.3 = (f32[1,128,4096]{1,2,0:T(8,128)S(1)}, f32[1,128,4096]{1,2,0:T(8,128)}, u32[]{:S(2)}) copy-start(f32[1,128,4096]{1,2,0:T(8,128)} %copy.101) | copy-start | bytes 6291460
  113.3 55.6 %all-to-all-start.1 = ((f32[32,2,128,128]{3,2,1,0:T(8,128)}), f32[32,2,128,128]{3,2,1,0:T(8,128)}, u32[]{:S(2)}, u32[]{:S(2)}) async-start(f32[32,2,128,128]{3,2,1,0:T(8,128)} %pad_maximum_fusion.1), calls=%async_computation.1 | async-start | bytes 8388608 | tf_op jit(solution)/shard_map/all_to_all | solution.py:32
  118.3 242.8 %all-reduce.5.cloned.1.call-start = ((), (), s32[]{:S(2)}) async-start(), calls=%async_computation.2 | async-start | bytes 8388608 | tf_op jit(solution)/shard_map/psum | solution.py:96
  118.8 4.1 %copy-start.11 = (f32[32,128]{1,0:T(8,128)}, f32[32,128]{1,0:T(8,128)S(1)}, u32[]{:S(2)}) copy-start(f32[32,128]{1,0:T(8,128)S(1)} %reduce_window_sum.41) | copy-start | bytes 49156
  118.9 3.9 %copy-start.15 = (pred[128,128]{0,1:T(8,128)(4,1)}, pred[128,128]{0,1:T(8,128)(4,1)S(1)}, u32[]{:S(2)}) copy-start(pred[128,128]{0,1:T(8,128)(4,1)S(1)} %iota_compare_fusion) | copy-start | bytes 49156
  119.0 3.8 %copy-start.13 = (f32[128,128]{0,1:T(8,128)}, f32[128,128]{0,1:T(8,128)S(1)}, u32[]{:S(2)}) copy-start(f32[128,128]{0,1:T(8,128)S(1)} %fusion.75) | copy-start | bytes 196612
  129.5 46.3 %copy-start.17 = (f32[32]{0:T(128)}, f32[32]{0:T(128)S(1)}, u32[]{:S(2)}) copy-start(f32[32]{0:T(128)S(1)} %slice_bitcast_fusion.13) | copy-start | bytes 388
  175.9 2.6 copy-start.9
  175.9 2.6 copy-start.18
  183.3 1.8 copy-start.10
  186.7 3.2 copy-start.4
  192.1 1.6 copy-start.6
  198.8 5.2 %copy-start.7 = (bf16[1,128,4096]{2,1,0:T(8,128)(2,1)S(1)}, bf16[1,128,4096]{2,1,0:T(8,128)(2,1)}, u32[]{:S(2)}) copy-start(bf16[1,128,4096]{2,1,0:T(8,128)(2,1)} %param.6) | copy-start | bytes 3145732
  206.7 1.5 copy-start.19
  206.7 68.8 %copy-start.8 = (f32[128,32,128]{0,2,1:T(8,128)S(1)}, f32[128,32,128]{0,2,1:T(8,128)}, u32[]{:S(2)}) copy-start(f32[128,32,128]{0,2,1:T(8,128)} %get-tuple-element.37) | copy-start | bytes 6291460
  206.7 68.8 %copy-start.12 = (f32[32,128]{1,0:T(8,128)S(1)}, f32[32,128]{1,0:T(8,128)}, u32[]{:S(2)}) copy-start(f32[32,128]{1,0:T(8,128)} %copy-done.11) | copy-start | bytes 49156
  206.7 68.8 %copy-start.14 = (f32[128,128]{0,1:T(8,128)S(1)}, f32[128,128]{0,1:T(8,128)}, u32[]{:S(2)}) copy-start(f32[128,128]{0,1:T(8,128)} %copy-done.13) | copy-start | bytes 196612
  206.7 68.8 %copy-start.16 = (pred[128,128]{0,1:T(8,128)(4,1)S(1)}, pred[128,128]{0,1:T(8,128)(4,1)}, u32[]{:S(2)}) copy-start(pred[128,128]{0,1:T(8,128)(4,1)} %copy-done.15) | copy-start | bytes 49156
  361.0 5.7 %copy-start.1 = (bf16[4096,256]{1,0:T(8,128)(2,1)S(1)}, bf16[4096,256]{1,0:T(8,128)(2,1)}, u32[]{:S(2)}) copy-start(bf16[4096,256]{1,0:T(8,128)(2,1)} %param.7) | copy-start | bytes 6291460
Sparse Core Ops, SparseCore 0:
  206.9 154.1 all-reduce.4

commit v5 on v4

--- a/solution.py
+++ b/solution.py
@@ -93,7 +93,20 @@
     d_weight = lax.dot_general(
         tokens_here, d_bc, (((0,), (0,)), ((), ())), preferred_element_type=jnp.float32
     )
-    d_wbc, d_alog = lax.psum((d_weight, d_rate), ("chain", "dp"))
+    axes = ("chain", "dp")
+    total = lax.axis_size(axes)
+    rows, cols = d_weight.shape
+    chunk = rows // total
+    rate_rows = jnp.zeros((8, cols), jnp.float32).at[0, :heads].set(d_rate)
+    parcel = jnp.concatenate(
+        [d_weight.reshape(total, chunk, cols), jnp.broadcast_to(rate_rows[None], (total, 8, cols))], axis=1
+    )
+    pieces = lax.all_to_all(parcel, axes, 0, 0, tiled=True)
+    mine_sum = jnp.sum(pieces, axis=0)
+    spread = jnp.broadcast_to(mine_sum[None], (total, chunk + 8, cols))
+    gathered = lax.all_to_all(spread, axes, 0, 0, tiled=True)
+    d_wbc = gathered[:, :chunk].reshape(rows, cols)
+    d_alog = gathered[0, chunk, :heads]
     return (d_x[None], d_wbc, d_alog)
 
 

time: 379 us -> 378 us (level); the launches traced: 374 us -> 380 us
  waiting for transfers between devices: 119 us -> 99.1 us
  starting transfers between devices: 5 us -> 24.5 us
  between operations: 14.7 us -> 1.25 us
  local copies, waits for them, and re-layouts: 53 us -> 61.2 us
  other arithmetic: 12.7 us -> 19.3 us
  blocking collectives: 130 us -> 135 us
    psum x1 -> x0, waiting for transfers between devices: 79.6 us -> none  [per_device(): d_wbc, d_alog = lax.psum((d_weight, d_rate), ('chain', 'dp'))]
    all_to_all x0 -> x1, blocking collectives: none -> 72.1 us  [per_device(): pieces = lax.all_to_all(parcel, axes, 0, 0, tiled=True)]
    psum x1 -> x0, blocking collectives: 67.2 us -> none  [per_device(): d_wbc, d_alog = lax.psum((d_weight, d_rate), ('chain', 'dp'))]
    all_to_all x0 -> x1, waiting for transfers between devices: none -> 58.1 us  [per_device(): gathered = lax.all_to_all(spread, axes, 0, 0, tiled=True)]
    all_to_all x1, starting transfers between devices: 4.96 us -> 19.4 us  [exchange(): back = lax.all_to_all(res, 'chain', 0, 0, tiled=True)]
    unnamed x48 -> x47, local copies, waits for them, and re-layouts: 16.1 us -> 10.3 us
    dot_general x0 -> x1, local copies, waits for them, and re-layouts: none -> 5.63 us  [per_device(): lax.dot_general(tokens_here, d_bc, (((0,), (0,)), ((), ())), preferred_el...]
    all_to_all x0 -> x1, starting transfers between devices: none -> 5.07 us  [per_device(): gathered = lax.all_to_all(spread, axes, 0, 0, tiled=True)]
  transfers between devices with their start and end apart: 2 -> 2, of which waited for: 2 -> 2; matrix products, arithmetic and copies ran while one was open for 5% -> 4% of each run, Pallas kernels for 0% -> 0%
where the time goes in v5:
time: 378 us; the launch traced here: 380 us
  blocking collectives  135 us (36%)
  waiting for transfers between devices  99.1 us (26%)
  local copies, waits for them, and re-layouts  61.2 us (16%)
  matrix products  39.2 us (10%)
  starting transfers between devices  24.5 us (6%)
  other arithmetic  19.3 us (5%)
    all_to_all x1, blocking collectives, per_device(): pieces = lax.all_to_all(parcel, axes, 0, 0, tiled=True)  72.1 us
    all_to_all x1, blocking collectives, exchange(): lax.all_to_all(both, 'chain', 0, 0, tiled=True)  63 us
    all_to_all x1, waiting for transfers between devices, per_device(): gathered = lax.all_to_all(spread, axes, 0, 0, tiled=True)  58.1 us
    all_to_all x1, waiting for transfers between devices, exchange(): back = lax.all_to_all(res, 'chain', 0, 0, tiled=True)  41 us
    all_to_all x1, starting transfers between devices, exchange(): back = lax.all_to_all(res, 'chain', 0, 0, tiled=True)  19.4 us
    unnamed x47, local copies, waits for them, and re-layouts  10.3 us
    slice x1, local copies, waits for them, and re-layouts, exchange(): inc = jnp.einsum('djh,jhx->dhx', fwd_w, parts[:, :, 0], precision=HIGH)  9.86 us
    dot_general x2, matrix products, block_forward(): jnp.einsum('shp,sn->hpn', inputs * tail[:, :, None], b_in, precision=HIGH)  9.55 us
  transfers between devices with their start and end apart: 2, of which 2 were waited for; matrix products, arithmetic and copies ran while one was open for 4% of the time, Pallas kernels for 0%

profile of v5, /device:TPU:1, one launch (start us, length us, event | category | flops | bytes accessed | tf_op | source)
XLA Modules:
  0.0 379.6 jit_solution(17539072382937257920)
XLA Ops:
  12.2 63.0 %all_to_all.20 = f32[32,2,136,128]{3,2,1,0:T(8,128)S(1)} all-to-all(f32[32,2,136,128]{3,2,1,0:T(8,128)S(1)} %copy.106), channel_id=1, replica_groups=mesh['chain'=32,'dp'=4] {'chain'}, dimensions={0} | all-to-all | bytes 8912896 | tf_op jit(solution)/shard_map/all_to_all | solution.py:20
  78.2 6.1 %reshape.408 = f32[32,1,2,16384]{3,2,0,1:T(2,128)} reshape(f32[32,1,2,128,128]{4,3,2,0,1:T(8,128)} %slice.70) | data formatting | bytes 8388608 | tf_op jit(solution)/shard_map/reshape | solution.py:21
  84.2 9.9 %fusion.101 = (f32[32,1,1,16384]{3,2,0,1:T(1,128)}, f32[32,1,1,16384]{3,2,0,1:T(1,128)}) fusion(f32[32,1,2,16384]{3,2,0,1:T(2,128)} %reshape.408), kind=kLoop, calls=%fused_computation.132 | loop fusion | bytes 8388608 | tf_op jit(solution)/shard_map/slice | solution.py:29
  94.2 4.8 %fusion.27 = f32[4,8,128,128]{3,1,2,0:T(8,128)S(1)} fusion(f32[32,1,1,16384]{3,2,0,1:T(1,128)} %get-tuple-element.37, f32[32]{0:T(128)S(1)} %get-tuple-element.33, f32[32]{0:T(128)S(1)} %get-tuple-element.34), kind=kOutput, calls=%fused_computation.45 | convolution fusion | flops 201329664 | bytes 4194560 | tf_op jit(solution)/shard_map/djh,jhx->dhx/dot_general | solution.py:29
  100.6 3.3 fusion.30
  106.5 19.4 %all-to-all-start.1 = ((f32[32,2,128,128]{3,2,1,0:T(8,128)}), f32[32,2,128,128]{3,2,1,0:T(8,128)}, u32[]{:S(2)}, u32[]{:S(2)}) async-start(f32[32,2,128,128]{3,2,1,0:T(8,128)} %pad_maximum_fusion.2), calls=%async_computation.1 | async-start | bytes 8388608 | tf_op jit(solution)/shard_map/all_to_all | solution.py:32
  126.7 3.2 fusion.36
  132.2 2.9 copy.122
  135.6 41.0 %all-to-all-done.1 = f32[32,2,128,128]{3,2,1,0:T(8,128)} async-done(((f32[32,2,128,128]{3,2,1,0:T(8,128)}), f32[32,2,128,128]{3,2,1,0:T(8,128)}, u32[]{:S(2)}, u32[]{:S(2)}) %all-to-all-start.1) | async-done | bytes 4194336 | tf_op jit(solution)/shard_map/all_to_all | solution.py:32
  176.5 4.6 %multiply_reduce_fusion.1 = (f32[128,32]{0,1:T(8,128)}, f32[128,32,128]{0,2,1:T(8,128)}) fusion(f32[128,32,128]{0,2,1:T(8,128)S(1)} %bitcast.198, f32[128,32]{0,1:T(8,128)S(1)} %copy.117, f32[32,2,128,128]{3,2,1,0:T(8,128)} %all-to-all-done.1, bf16[128,256]{1,0:T(8,128)(2,1)S(1)} %convolution_convert_fusion), kind=kOutput, calls=%fused_computation.33 | convolution fusion | flops 806875136 | bytes 6356992 | tf_op jit(solution)/shard_map/transpose(jvp(shp,sn->hpn))/dot_general | solution.py:57
  189.1 2.7 fusion.3
  196.7 3.1 copy.123
  203.7 4.8 %fusion.37 = f32[128,128]{1,0:T(8,128)S(1)} fusion(f32[32,2,128,128]{3,2,1,0:T(8,128)} %all-to-all-done.1, f32[128,32,128]{2,1,0:T(8,128)S(1)} %bitcast.206), kind=kOutput, calls=%fused_computation.50 | convolution fusion | flops 805306368 | bytes 4259840 | tf_op jit(solution)/shard_map/transpose(jvp(tn,hpn->thp))/dot_general | solution.py:60
  208.8 5.0 %fusion.40 = f32[128,128]{1,0:T(8,128)S(1)} fusion(f32[32,2,128,128]{3,2,1,0:T(8,128)} %all-to-all-done.1, f32[128,32,128]{2,1,0:T(8,128)S(1)} %bitcast.207), kind=kOutput, calls=%fused_computation.51 | convolution fusion | flops 805306368 | bytes 4259840 | tf_op jit(solution)/shard_map/transpose(jvp(shp,sn->hpn))/dot_general | solution.py:57
  213.9 2.7 convolution_bitcast_fusion
  216.7 5.6 %copy.125 = f32[4096,256]{1,0:T(8,128)} copy(f32[4096,256]{0,1:T(8,128)} %convolution_bitcast_fusion) | data formatting | bytes 8388608 | tf_op jit(solution)/shard_map/dot_general | solution.py:93
  223.9 2.6 pad_maximum_fusion
  226.5 72.1 %all_to_all.21 = f32[128,40,256]{2,1,0:T(8,128)} all-to-all(f32[128,40,256]{2,1,0:T(8,128)S(1)} %pad_maximum_fusion), channel_id=1, replica_groups=mesh['chain'=32,'dp'=4] {'chain','dp'}, dimensions={0} | all-to-all | bytes 10485760 | tf_op jit(solution)/shard_map/all_to_all | solution.py:104
  298.6 2.8 reduce_sum.104
  301.4 2.7 broadcast_in_dim.41
  304.1 5.1 %all-to-all-start.3 = ((f32[128,40,256]{2,1,0:T(8,128)}), f32[128,40,256]{2,1,0:T(8,128)}, u32[]{:S(2)}, u32[]{:S(2)}) async-start(f32[128,40,256]{2,1,0:T(8,128)} %broadcast_in_dim.41), calls=%async_computation.3 | async-start | bytes 10485760 | tf_op jit(solution)/shard_map/all_to_all | solution.py:107
  309.2 3.6 fusion.14
  315.1 58.1 %all-to-all-done.3 = f32[128,40,256]{2,1,0:T(8,128)} async-done(((f32[128,40,256]{2,1,0:T(8,128)}), f32[128,40,256]{2,1,0:T(8,128)}, u32[]{:S(2)}, u32[]{:S(2)}) %all-to-all-start.3) | async-done | bytes 5242912 | tf_op jit(solution)/shard_map/all_to_all | solution.py:107
  373.3 5.0 %slice.77 = f32[128,32,256]{2,1,0:T(8,128)} slice(f32[128,40,256]{2,1,0:T(8,128)} %all-to-all-done.3), slice={[0:128], [0:32], [0:256]} | slice | bytes 8388608 | tf_op jit(solution)/shard_map/slice | solution.py:108
  (100 shorter events, 44.4 us)
Async XLA Ops:
  0.6 6.3 %copy-start = (bf16[4096,256]{1,0:T(8,128)(2,1)S(1)}, bf16[4096,256]{1,0:T(8,128)(2,1)}, u32[]{:S(2)}) copy-start(bf16[4096,256]{1,0:T(8,128)(2,1)} %param.9) | copy-start | bytes 6291460
  6.9 1.9 copy-start.2
  99.0 1.6 copy-start.6
  106.5 20.1 %copy-start.3 = (f32[1,128,4096]{1,2,0:T(8,128)S(1)}, f32[1,128,4096]{1,2,0:T(8,128)}, u32[]{:S(2)}) copy-start(f32[1,128,4096]{1,2,0:T(8,128)} %copy.101) | copy-start | bytes 6291460
  106.5 70.0 %all-to-all-start.1 = ((f32[32,2,128,128]{3,2,1,0:T(8,128)}), f32[32,2,128,128]{3,2,1,0:T(8,128)}, u32[]{:S(2)}, u32[]{:S(2)}) async-start(f32[32,2,128,128]{3,2,1,0:T(8,128)} %pad_maximum_fusion.2), calls=%async_computation.1 | async-start | bytes 8388608 | tf_op jit(solution)/shard_map/all_to_all | solution.py:32
  126.3 3.5 copy-start.11
  126.5 3.3 copy-start.15
  126.6 3.2 copy-start.13
  191.9 2.6 copy-start.18
  191.9 2.6 copy-start.9
  191.9 2.6 copy-start.17
  196.7 3.1 copy-start.4
  202.1 1.6 copy-start.5
  208.7 5.2 %copy-start.7 = (bf16[1,128,4096]{2,1,0:T(8,128)(2,1)S(1)}, bf16[1,128,4096]{2,1,0:T(8,128)(2,1)}, u32[]{:S(2)}) copy-start(bf16[1,128,4096]{2,1,0:T(8,128)(2,1)} %param.8) | copy-start | bytes 3145732
  216.7 5.6 %copy-start.10 = (f32[32,128]{0,1:T(8,128)S(1)}, f32[32,128]{0,1:T(8,128)}, u32[]{:S(2)}) copy-start(f32[32,128]{0,1:T(8,128)} %get-tuple-element.41) | copy-start | bytes 49156
  216.7 7.1 %copy-start.19 = (f32[32]{0:T(128)S(1)}, f32[32]{0:T(128)}, u32[]{:S(2)}) copy-start(f32[32]{0:T(128)} %param.12) | copy-start | bytes 388
  304.1 5.1 %copy-start.8 = (f32[128,32,128]{0,2,1:T(8,128)S(1)}, f32[128,32,128]{0,2,1:T(8,128)}, u32[]{:S(2)}) copy-start(f32[128,32,128]{0,2,1:T(8,128)} %get-tuple-element.50) | copy-start | bytes 6291460
  304.1 5.1 %copy-start.12 = (f32[32,128]{1,0:T(8,128)S(1)}, f32[32,128]{1,0:T(8,128)}, u32[]{:S(2)}) copy-start(f32[32,128]{1,0:T(8,128)} %copy-done.11) | copy-start | bytes 49156
  304.1 5.1 %copy-start.14 = (f32[128,128]{0,1:T(8,128)S(1)}, f32[128,128]{0,1:T(8,128)}, u32[]{:S(2)}) copy-start(f32[128,128]{0,1:T(8,128)} %copy-done.13) | copy-start | bytes 196612
  304.1 5.1 %copy-start.16 = (pred[128,128]{0,1:T(8,128)(4,1)S(1)}, pred[128,128]{0,1:T(8,128)(4,1)}, u32[]{:S(2)}) copy-start(pred[128,128]{0,1:T(8,128)(4,1)} %copy-done.15) | copy-start | bytes 49156
  304.1 69.1 %all-to-all-start.3 = ((f32[128,40,256]{2,1,0:T(8,128)}), f32[128,40,256]{2,1,0:T(8,128)}, u32[]{:S(2)}, u32[]{:S(2)}) async-start(f32[128,40,256]{2,1,0:T(8,128)} %broadcast_in_dim.41), calls=%async_computation.3 | async-start | bytes 10485760 | tf_op jit(solution)/shard_map/all_to_all | solution.py:107
  373.3 6.1 %copy-start.1 = (bf16[4096,256]{1,0:T(8,128)(2,1)S(1)}, bf16[4096,256]{1,0:T(8,128)(2,1)}, u32[]{:S(2)}) copy-start(bf16[4096,256]{1,0:T(8,128)(2,1)} %param.9) | copy-start | bytes 6291460

commit v6 on v5

--- a/solution.py
+++ b/solution.py
@@ -18,7 +18,7 @@
         [jnp.concatenate([own_state, marks], axis=1), jnp.concatenate([back_term, marks], axis=1)], axis=1
     )
     sent = lax.all_to_all(both, "chain", 0, 0, tiled=True).reshape(count, per, 2, width + 8, state)
-    parts = sent[:, :, :, :width].reshape(count, per, 2, width * state)
+    parts = sent[:, :, :, :width]
     mine_logs = sent[:, :, 0, width, 0]
     edge = jnp.cumsum(mine_logs, axis=0) - mine_logs
     after = edge + mine_logs
@@ -26,8 +26,8 @@
     earlier = pos[None, :] < pos[:, None]
     fwd_w = jnp.exp(jnp.where(earlier[:, :, None], edge[:, None, :] - after[None, :, :], -jnp.inf))
     bwd_w = jnp.exp(jnp.where(earlier.T[:, :, None], edge[None, :, :] - after[:, None, :], -jnp.inf))
-    inc = jnp.einsum("djh,jhx->dhx", fwd_w, parts[:, :, 0], precision=HIGH)
-    out = jnp.einsum("djh,jhx->dhx", bwd_w, parts[:, :, 1], precision=HIGH)
+    inc = jnp.einsum("djh,jhpn->dhpn", fwd_w, parts[:, :, 0], precision=HIGH)
+    out = jnp.einsum("djh,jhpn->dhpn", bwd_w, parts[:, :, 1], precision=HIGH)
     res = jnp.stack([inc, out], axis=2).reshape(count * per, 2, width, state)
     back = lax.all_to_all(res, "chain", 0, 0, tiled=True)
     return back[:, 0], back[:, 1]

time: 378 us -> 347 us (0.918)
  starting transfers between devices: 24.5 us -> 10.1 us
  local copies, waits for them, and re-layouts: 61.2 us -> 48.3 us
    all_to_all x1, starting transfers between devices: 19.4 us -> 5 us  [exchange(): back = lax.all_to_all(res, 'chain', 0, 0, tiled=True)]
    slice x3 -> x0, local copies, waits for them, and re-layouts: 12.7 us -> none  [the longest x1 9.86 us: exchange(): inc = jnp.einsum('djh,jhx->dhx', fwd_w, parts[:, :, 0], precision=HIGH)]
    unnamed x47 -> x45, local copies, waits for them, and re-layouts: 10.3 us -> 6.95 us
  transfers between devices with their start and end apart: 2 -> 2, of which waited for: 2 -> 2; matrix products, arithmetic and copies ran while one was open for 4% -> 5% of each run, Pallas kernels for 0% -> 0%
where the time goes in v6:
time: 347 us; the launch traced here: 346 us
  blocking collectives  135 us (39%)
  waiting for transfers between devices  96.9 us (28%)
  local copies, waits for them, and re-layouts  48.3 us (14%)
  matrix products  38.2 us (11%)
  other arithmetic  16.3 us (5%)
  starting transfers between devices  10.1 us (3%)
    all_to_all x1, blocking collectives, per_device(): pieces = lax.all_to_all(parcel, axes, 0, 0, tiled=True)  72.1 us
    all_to_all x1, blocking collectives, exchange(): lax.all_to_all(both, 'chain', 0, 0, tiled=True)  63 us
    all_to_all x1, waiting for transfers between devices, per_device(): gathered = lax.all_to_all(spread, axes, 0, 0, tiled=True)  58.1 us
    all_to_all x1, waiting for transfers between devices, exchange(): back = lax.all_to_all(res, 'chain', 0, 0, tiled=True)  38.7 us
    dot_general x2, matrix products, block_forward(): jnp.einsum('shp,sn->hpn', inputs * tail[:, :, None], b_in, precision=HIGH)  8.79 us
    dot_general x2, matrix products, block_forward(): jnp.einsum('tn,hpn->thp', c_out, h_in, precision=HIGH)  7.66 us
    dot_general x2, matrix products, block_forward(): y_intra = jnp.einsum('hts,shp->thp', mixing, inputs, precision=HIGH)  7.4 us
    unnamed x45, local copies, waits for them, and re-layouts  6.95 us
  transfers between devices with their start and end apart: 2, of which 2 were waited for; matrix products, arithmetic and copies ran while one was open for 5% of the time, Pallas kernels for 0%

profile of v6, /device:TPU:1, one launch (start us, length us, event | category | flops | bytes accessed | tf_op | source)
XLA Modules:
  0.0 345.9 jit_solution(5326760374203816771)
XLA Ops:
  0.7 2.7 copy.111
  10.9 63.0 %all_to_all.20 = f32[32,2,136,128]{3,2,1,0:T(8,128)S(1)} all-to-all(f32[32,2,136,128]{3,2,1,0:T(8,128)S(1)} %copy.116), channel_id=1, replica_groups=mesh['chain'=32,'dp'=4] {'chain'}, dimensions={0} | all-to-all | bytes 8912896 | tf_op jit(solution)/shard_map/all_to_all | solution.py:20
  77.7 3.5 %fusion.24 = f32[32,1,1,128,128]{4,0,3,2,1:T(8,128)S(1)} fusion(f32[32,1,2,136,128]{4,0,3,2,1:T(8,128)} %bitcast.194, f32[32]{0:T(128)S(1)} %get-tuple-element.33, f32[32]{0:T(128)S(1)} %get-tuple-element.34), kind=kOutput, calls=%fused_computation.45 | convolution fusion | flops 201329664 | bytes 4194560 | tf_op jit(solution)/shard_map/djh,jhpn->dhpn/dot_general | solution.py:30
  81.2 3.5 %fusion.23 = f32[32,1,1,128,128]{4,0,3,2,1:T(8,128)S(1)} fusion(f32[32,1,2,136,128]{4,0,3,2,1:T(8,128)} %bitcast.195, f32[32]{0:T(128)S(1)} %get-tuple-element.33, f32[32]{0:T(128)S(1)} %get-tuple-element.34), kind=kOutput, calls=%fused_computation.44 | convolution fusion | flops 201329664 | bytes 4194560 | tf_op jit(solution)/shard_map/djh,jhpn->dhpn/dot_general | solution.py:29
  85.1 4.4 %copy.119 = f32[32,2,128,128]{3,2,1,0:T(8,128)} copy(f32[32,2,128,128]{3,0,2,1:T(8,128)S(1)} %maximum_bitcast_fusion) | data formatting | bytes 8388608 | tf_op jit(solution)/shard_map/reshape | solution.py:31
  89.6 5.0 %all-to-all-start.1 = ((f32[32,2,128,128]{3,2,1,0:T(8,128)}), f32[32,2,128,128]{3,2,1,0:T(8,128)}, u32[]{:S(2)}, u32[]{:S(2)}) async-start(f32[32,2,128,128]{3,2,1,0:T(8,128)} %copy.119), calls=%async_computation.1 | async-start | bytes 8388608 | tf_op jit(solution)/shard_map/all_to_all | solution.py:32
  95.3 3.8 %fusion.28 = (f32[32,128]{1,0:T(8,128)}, f32[32,128]{1,0:T(8,128)}, f32[128,128]{0,1:T(8,128)S(1)}) fusion(f32[128,128]{0,1:T(8,128)S(1)} %fusion.67, f32[32,128]{1,0:T(8,128)S(1)} %reduce_window_sum.41, pred[128,128]{0,1:T(8,128)(4,1)S(1)} %iota_compare_fusion, bf16[32,128,128]{2,1,0:T(8,128)(2,1)S(1)} %bitcast.198, f32[128,32,128]{0,2,1:T(8,128)S(1)} %bitcast.191, ...), kind=kOutput, calls=%fused_computation.47 | convolution fusion | flops 810524672 | bytes 3358720 | tf_op jit(solution)/shard_map/transpose(jvp(hts,shp->thp))/dot_general | solution.py:54
  102.8 2.9 copy.132
  106.2 38.7 %all-to-all-done.1 = f32[32,2,128,128]{3,2,1,0:T(8,128)} async-done(((f32[32,2,128,128]{3,2,1,0:T(8,128)}), f32[32,2,128,128]{3,2,1,0:T(8,128)}, u32[]{:S(2)}, u32[]{:S(2)}) %all-to-all-start.1) | async-done | bytes 4194336 | tf_op jit(solution)/shard_map/all_to_all | solution.py:32
  145.0 2.7 fusion.3
  148.4 4.0 %multiply_reduce_fusion.1 = (f32[128,32]{0,1:T(8,128)S(1)}, f32[128,32,128]{0,2,1:T(8,128)}) fusion(f32[128,32,128]{0,2,1:T(8,128)S(1)} %bitcast.192, f32[128,32]{0,1:T(8,128)S(1)} %copy.127, f32[32,2,128,128]{3,2,1,0:T(8,128)} %all-to-all-done.1, bf16[128,256]{1,0:T(8,128)(2,1)S(1)} %convolution_convert_fusion), kind=kOutput, calls=%fused_computation.32 | convolution fusion | flops 806875136 | bytes 6356992 | tf_op jit(solution)/shard_map/transpose(jvp(shp,sn->hpn))/dot_general | solution.py:57
  159.0 3.1 copy.133
  166.6 2.7 mul.146
  171.8 4.8 %fusion.32 = f32[128,128]{1,0:T(8,128)S(1)} fusion(f32[32,2,128,128]{3,2,1,0:T(8,128)} %all-to-all-done.1, f32[128,32,128]{2,1,0:T(8,128)S(1)} %bitcast.201), kind=kOutput, calls=%fused_computation.50 | convolution fusion | flops 805306368 | bytes 4259840 | tf_op jit(solution)/shard_map/transpose(jvp(shp,sn->hpn))/dot_general | solution.py:57
  176.8 5.0 %fusion.29 = f32[128,128]{1,0:T(8,128)S(1)} fusion(f32[32,2,128,128]{3,2,1,0:T(8,128)} %all-to-all-done.1, f32[128,32,128]{2,1,0:T(8,128)S(1)} %bitcast.202), kind=kOutput, calls=%fused_computation.49 | convolution fusion | flops 805306368 | bytes 4259840 | tf_op jit(solution)/shard_map/transpose(jvp(tn,hpn->thp))/dot_general | solution.py:60
  182.0 2.7 convolution_bitcast_fusion
  184.7 5.6 %copy.135 = f32[4096,256]{1,0:T(8,128)} copy(f32[4096,256]{0,1:T(8,128)} %convolution_bitcast_fusion) | data formatting | bytes 8388608 | tf_op jit(solution)/shard_map/dot_general | solution.py:93
  193.1 72.1 %all_to_all.21 = f32[128,40,256]{2,1,0:T(8,128)} all-to-all(f32[128,40,256]{2,1,0:T(8,128)S(1)} %pad_maximum_fusion), channel_id=1, replica_groups=mesh['chain'=32,'dp'=4] {'chain','dp'}, dimensions={0} | all-to-all | bytes 10485760 | tf_op jit(solution)/shard_map/all_to_all | solution.py:104
  265.1 2.8 reduce_sum.104
  267.9 2.7 broadcast_in_dim.41
  270.6 5.1 %all-to-all-start.3 = ((f32[128,40,256]{2,1,0:T(8,128)}), f32[128,40,256]{2,1,0:T(8,128)}, u32[]{:S(2)}, u32[]{:S(2)}) async-start(f32[128,40,256]{2,1,0:T(8,128)} %broadcast_in_dim.41), calls=%async_computation.3 | async-start | bytes 10485760 | tf_op jit(solution)/shard_map/all_to_all | solution.py:107
  275.8 3.6 %fusion.10 = bf16[128,32,128]{0,2,1:T(8,128)(2,1)} fusion(f32[128,32,128]{0,2,1:T(8,128)S(1)} %copy-done.7, bf16[32,128,128]{2,1,0:T(8,128)(2,1)S(1)} %bitcast.200, f32[128,32]{0,1:T(8,128)S(1)} %copy.127, f32[128,128]{0,1:T(8,128)S(1)} %copy-done.13, f32[32,128]{1,0:T(8,128)S(1)} %copy-done.11, f32[128,32]{0,1:T(8,128)S(1)} %copy.124, ...), kind=kOutput, calls=%fused_computation.26 | convolution fusion | flops 808976384 | bytes 4325376 | tf_op jit(solution)/shard_map/transpose(jvp(hts,shp->thp))/dot_general | solution.py:54
  281.7 58.1 %all-to-all-done.3 = f32[128,40,256]{2,1,0:T(8,128)} async-done(((f32[128,40,256]{2,1,0:T(8,128)}), f32[128,40,256]{2,1,0:T(8,128)}, u32[]{:S(2)}, u32[]{:S(2)}) %all-to-all-start.3) | async-done | bytes 5242912 | tf_op jit(solution)/shard_map/all_to_all | solution.py:107
  339.8 5.0 %slice.75 = f32[128,32,256]{2,1,0:T(8,128)} slice(f32[128,40,256]{2,1,0:T(8,128)} %all-to-all-done.3), slice={[0:128], [0:32], [0:256]} | slice | bytes 8388608 | tf_op jit(solution)/shard_map/slice | solution.py:108
  (97 shorter events, 37.3 us)
Async XLA Ops:
  0.6 5.0 %copy-start = (bf16[4096,256]{1,0:T(8,128)(2,1)S(1)}, bf16[4096,256]{1,0:T(8,128)(2,1)}, u32[]{:S(2)}) copy-start(bf16[4096,256]{1,0:T(8,128)(2,1)} %param.9) | copy-start | bytes 6291460
  0.6 2.8 copy-start.14
  0.7 2.9 copy-start.18
  5.6 1.9 copy-start.2
  75.3 2.0 copy-start.4
  89.5 5.7 %copy-start.3 = (f32[1,128,4096]{1,2,0:T(8,128)S(1)}, f32[1,128,4096]{1,2,0:T(8,128)}, u32[]{:S(2)}) copy-start(f32[1,128,4096]{1,2,0:T(8,128)} %copy.111) | copy-start | bytes 6291460
  89.6 55.4 %all-to-all-start.1 = ((f32[32,2,128,128]{3,2,1,0:T(8,128)}), f32[32,2,128,128]{3,2,1,0:T(8,128)}, u32[]{:S(2)}, u32[]{:S(2)}) async-start(f32[32,2,128,128]{3,2,1,0:T(8,128)} %copy.119), calls=%async_computation.1 | async-start | bytes 8388608 | tf_op jit(solution)/shard_map/all_to_all | solution.py:32
  95.0 4.1 %copy-start.10 = (f32[32,128]{1,0:T(8,128)}, f32[32,128]{1,0:T(8,128)S(1)}, u32[]{:S(2)}) copy-start(f32[32,128]{1,0:T(8,128)S(1)} %reduce_window_sum.41) | copy-start | bytes 49156
  95.1 3.9 %copy-start.15 = (pred[128,128]{0,1:T(8,128)(4,1)}, pred[128,128]{0,1:T(8,128)(4,1)S(1)}, u32[]{:S(2)}) copy-start(pred[128,128]{0,1:T(8,128)(4,1)S(1)} %iota_compare_fusion) | copy-start | bytes 49156
  95.3 3.8 %copy-start.12 = (f32[128,128]{0,1:T(8,128)}, f32[128,128]{0,1:T(8,128)S(1)}, u32[]{:S(2)}) copy-start(f32[128,128]{0,1:T(8,128)S(1)} %fusion.67) | copy-start | bytes 196612
  153.2 2.7 copy-start.8
  153.2 2.7 copy-start.9
  153.2 2.7 copy-start.17
  153.2 4.3 %copy-start.19 = (f32[32]{0:T(128)S(1)}, f32[32]{0:T(128)}, u32[]{:S(2)}) copy-start(f32[32]{0:T(128)} %param.12) | copy-start | bytes 388
  159.0 3.1 copy-start.5
  176.8 5.2 %copy-start.6 = (bf16[1,128,4096]{2,1,0:T(8,128)(2,1)S(1)}, bf16[1,128,4096]{2,1,0:T(8,128)(2,1)}, u32[]{:S(2)}) copy-start(bf16[1,128,4096]{2,1,0:T(8,128)(2,1)} %param.8) | copy-start | bytes 3145732
  270.6 5.1 %copy-start.7 = (f32[128,32,128]{0,2,1:T(8,128)S(1)}, f32[128,32,128]{0,2,1:T(8,128)}, u32[]{:S(2)}) copy-start(f32[128,32,128]{0,2,1:T(8,128)} %get-tuple-element.48) | copy-start | bytes 6291460
  270.6 5.1 %copy-start.11 = (f32[32,128]{1,0:T(8,128)S(1)}, f32[32,128]{1,0:T(8,128)}, u32[]{:S(2)}) copy-start(f32[32,128]{1,0:T(8,128)} %copy-done.10) | copy-start | bytes 49156
  270.6 5.1 %copy-start.13 = (f32[128,128]{0,1:T(8,128)S(1)}, f32[128,128]{0,1:T(8,128)}, u32[]{:S(2)}) copy-start(f32[128,128]{0,1:T(8,128)} %copy-done.12) | copy-start | bytes 196612
  270.6 5.1 %copy-start.16 = (pred[128,128]{0,1:T(8,128)(4,1)S(1)}, pred[128,128]{0,1:T(8,128)(4,1)}, u32[]{:S(2)}) copy-start(pred[128,128]{0,1:T(8,128)(4,1)} %copy-done.15) | copy-start | bytes 49156
  270.6 69.1 %all-to-all-start.3 = ((f32[128,40,256]{2,1,0:T(8,128)}), f32[128,40,256]{2,1,0:T(8,128)}, u32[]{:S(2)}, u32[]{:S(2)}) async-start(f32[128,40,256]{2,1,0:T(8,128)} %broadcast_in_dim.41), calls=%async_computation.3 | async-start | bytes 10485760 | tf_op jit(solution)/shard_map/all_to_all | solution.py:107
  339.8 6.1 %copy-start.1 = (bf16[4096,256]{1,0:T(8,128)(2,1)S(1)}, bf16[4096,256]{1,0:T(8,128)(2,1)}, u32[]{:S(2)}) copy-start(bf16[4096,256]{1,0:T(8,128)(2,1)} %param.9) | copy-start | bytes 6291460

commit v7 on v6

--- a/solution.py
+++ b/solution.py
@@ -103,10 +103,9 @@
     )
     pieces = lax.all_to_all(parcel, axes, 0, 0, tiled=True)
     mine_sum = jnp.sum(pieces, axis=0)
-    spread = jnp.broadcast_to(mine_sum[None], (total, chunk + 8, cols))
-    gathered = lax.all_to_all(spread, axes, 0, 0, tiled=True)
-    d_wbc = gathered[:, :chunk].reshape(rows, cols)
-    d_alog = gathered[0, chunk, :heads]
+    spread = jnp.broadcast_to(mine_sum[None, :chunk], (total, chunk, cols))
+    d_wbc = lax.all_to_all(spread, axes, 0, 0, tiled=True).reshape(rows, cols)
+    d_alog = mine_sum[chunk, :heads]
     return (d_x[None], d_wbc, d_alog)
 
 

time: 347 us -> 334 us (0.963)
  waiting for transfers between devices: 96.9 us -> 85.2 us
    all_to_all x1, waiting for transfers between devices: 58.1 us -> 46.5 us  [per_device(): d_wbc = lax.all_to_all(spread, axes, 0, 0, tiled=True).reshape(rows, cols)]
    slice x1, local copies, waits for them, and re-layouts: 4.96 us -> 0.01 us  [per_device(): spread = jnp.broadcast_to(mine_sum[None, :chunk], (total, chunk, cols))]
    unnamed x45 -> x46, local copies, waits for them, and re-layouts: 6.95 us -> 11.6 us
where the time goes in v7:
time: 334 us; the launch traced here: 333 us
  blocking collectives  135 us (40%)
  waiting for transfers between devices  85.2 us (26%)
  local copies, waits for them, and re-layouts  47.2 us (14%)
  matrix products  38.3 us (11%)
  other arithmetic  16.3 us (5%)
  starting transfers between devices  10.1 us (3%)
    all_to_all x1, blocking collectives, per_device(): pieces = lax.all_to_all(parcel, axes, 0, 0, tiled=True)  72.1 us
    all_to_all x1, blocking collectives, exchange(): lax.all_to_all(both, 'chain', 0, 0, tiled=True)  63 us
    all_to_all x1, waiting for transfers between devices, per_device(): d_wbc = lax.all_to_all(spread, axes, 0, 0, tiled=True).reshape(rows, cols)  46.5 us
    all_to_all x1, waiting for transfers between devices, exchange(): back = lax.all_to_all(res, 'chain', 0, 0, tiled=True)  38.7 us
    unnamed x46, local copies, waits for them, and re-layouts  11.6 us
    dot_general x2, matrix products, block_forward(): jnp.einsum('shp,sn->hpn', inputs * tail[:, :, None], b_in, precision=HIGH)  8.86 us
    dot_general x2, matrix products, block_forward(): jnp.einsum('tn,hpn->thp', c_out, h_in, precision=HIGH)  7.66 us
    dot_general x2, matrix products, block_forward(): y_intra = jnp.einsum('hts,shp->thp', mixing, inputs, precision=HIGH)  7.43 us
  transfers between devices with their start and end apart: 2, of which 2 were waited for; matrix products, arithmetic and copies ran while one was open for 5% of the time, Pallas kernels for 0%

profile of v7, /device:TPU:1, one launch (start us, length us, event | category | flops | bytes accessed | tf_op | source)
XLA Modules:
  0.0 333.3 jit_solution(2154666607851957741)
XLA Ops:
  0.7 2.7 copy.111
  10.9 63.0 %all_to_all.20 = f32[32,2,136,128]{3,2,1,0:T(8,128)S(1)} all-to-all(f32[32,2,136,128]{3,2,1,0:T(8,128)S(1)} %copy.116), channel_id=1, replica_groups=mesh['chain'=32,'dp'=4] {'chain'}, dimensions={0} | all-to-all | bytes 8912896 | tf_op jit(solution)/shard_map/all_to_all | solution.py:20
  77.7 3.5 %fusion.24 = f32[32,1,1,128,128]{4,0,3,2,1:T(8,128)S(1)} fusion(f32[32,1,2,136,128]{4,0,3,2,1:T(8,128)} %bitcast.194, f32[32]{0:T(128)S(1)} %get-tuple-element.33, f32[32]{0:T(128)S(1)} %get-tuple-element.34), kind=kOutput, calls=%fused_computation.45 | convolution fusion | flops 201329664 | bytes 4194560 | tf_op jit(solution)/shard_map/djh,jhpn->dhpn/dot_general | solution.py:30
  81.2 3.5 %fusion.23 = f32[32,1,1,128,128]{4,0,3,2,1:T(8,128)S(1)} fusion(f32[32,1,2,136,128]{4,0,3,2,1:T(8,128)} %bitcast.195, f32[32]{0:T(128)S(1)} %get-tuple-element.33, f32[32]{0:T(128)S(1)} %get-tuple-element.34), kind=kOutput, calls=%fused_computation.44 | convolution fusion | flops 201329664 | bytes 4194560 | tf_op jit(solution)/shard_map/djh,jhpn->dhpn/dot_general | solution.py:29
  85.1 4.4 %copy.119 = f32[32,2,128,128]{3,2,1,0:T(8,128)} copy(f32[32,2,128,128]{3,0,2,1:T(8,128)S(1)} %maximum_bitcast_fusion) | data formatting | bytes 8388608 | tf_op jit(solution)/shard_map/reshape | solution.py:31
  89.6 5.0 %all-to-all-start.1 = ((f32[32,2,128,128]{3,2,1,0:T(8,128)}), f32[32,2,128,128]{3,2,1,0:T(8,128)}, u32[]{:S(2)}, u32[]{:S(2)}) async-start(f32[32,2,128,128]{3,2,1,0:T(8,128)} %copy.119), calls=%async_computation.1 | async-start | bytes 8388608 | tf_op jit(solution)/shard_map/all_to_all | solution.py:32
  95.3 3.8 %fusion.28 = (f32[32,128]{1,0:T(8,128)}, f32[32,128]{1,0:T(8,128)}, f32[128,128]{0,1:T(8,128)S(1)}) fusion(f32[128,128]{0,1:T(8,128)S(1)} %fusion.67, f32[32,128]{1,0:T(8,128)S(1)} %reduce_window_sum.41, pred[128,128]{0,1:T(8,128)(4,1)S(1)} %iota_compare_fusion, bf16[32,128,128]{2,1,0:T(8,128)(2,1)S(1)} %bitcast.198, f32[128,32,128]{0,2,1:T(8,128)S(1)} %bitcast.191, ...), kind=kOutput, calls=%fused_computation.47 | convolution fusion | flops 810524672 | bytes 3358720 | tf_op jit(solution)/shard_map/transpose(jvp(hts,shp->thp))/dot_general | solution.py:54
  102.8 2.9 copy.132
  106.2 38.7 %all-to-all-done.1 = f32[32,2,128,128]{3,2,1,0:T(8,128)} async-done(((f32[32,2,128,128]{3,2,1,0:T(8,128)}), f32[32,2,128,128]{3,2,1,0:T(8,128)}, u32[]{:S(2)}, u32[]{:S(2)}) %all-to-all-start.1) | async-done | bytes 4194336 | tf_op jit(solution)/shard_map/all_to_all | solution.py:32
  145.0 2.7 fusion.3
  148.4 4.1 %multiply_reduce_fusion.1 = (f32[128,32]{0,1:T(8,128)S(1)}, f32[128,32,128]{0,2,1:T(8,128)}) fusion(f32[128,32,128]{0,2,1:T(8,128)S(1)} %bitcast.192, f32[128,32]{0,1:T(8,128)S(1)} %copy.127, f32[32,2,128,128]{3,2,1,0:T(8,128)} %all-to-all-done.1, bf16[128,256]{1,0:T(8,128)(2,1)S(1)} %convolution_convert_fusion), kind=kOutput, calls=%fused_computation.32 | convolution fusion | flops 806875136 | bytes 6356992 | tf_op jit(solution)/shard_map/transpose(jvp(shp,sn->hpn))/dot_general | solution.py:57
  159.0 3.1 copy.133
  166.7 2.8 mul.146
  171.9 4.8 %fusion.32 = f32[128,128]{1,0:T(8,128)S(1)} fusion(f32[32,2,128,128]{3,2,1,0:T(8,128)} %all-to-all-done.1, f32[128,32,128]{2,1,0:T(8,128)S(1)} %bitcast.201), kind=kOutput, calls=%fused_computation.50 | convolution fusion | flops 805306368 | bytes 4259840 | tf_op jit(solution)/shard_map/transpose(jvp(shp,sn->hpn))/dot_general | solution.py:57
  176.9 5.0 %fusion.29 = f32[128,128]{1,0:T(8,128)S(1)} fusion(f32[32,2,128,128]{3,2,1,0:T(8,128)} %all-to-all-done.1, f32[128,32,128]{2,1,0:T(8,128)S(1)} %bitcast.202), kind=kOutput, calls=%fused_computation.49 | convolution fusion | flops 805306368 | bytes 4259840 | tf_op jit(solution)/shard_map/transpose(jvp(tn,hpn->thp))/dot_general | solution.py:60
  182.1 2.7 convolution_bitcast_fusion
  184.9 5.6 %copy.135 = f32[4096,256]{1,0:T(8,128)} copy(f32[4096,256]{0,1:T(8,128)} %convolution_bitcast_fusion) | data formatting | bytes 8388608 | tf_op jit(solution)/shard_map/dot_general | solution.py:93
  190.5 2.6 pad_maximum_fusion
  193.2 72.1 %all_to_all.21 = f32[128,40,256]{2,1,0:T(8,128)} all-to-all(f32[128,40,256]{2,1,0:T(8,128)S(1)} %pad_maximum_fusion), channel_id=1, replica_groups=mesh['chain'=32,'dp'=4] {'chain','dp'}, dimensions={0} | all-to-all | bytes 10485760 | tf_op jit(solution)/shard_map/all_to_all | solution.py:104
  265.3 2.8 reduce_sum.104
  270.6 5.1 %all-to-all-start.3 = ((f32[128,32,256]{2,1,0:T(8,128)}), f32[128,32,256]{2,1,0:T(8,128)}, u32[]{:S(2)}, u32[]{:S(2)}) async-start(f32[128,32,256]{2,1,0:T(8,128)} %broadcast_in_dim.41), calls=%async_computation.3 | async-start | bytes 8388608 | tf_op jit(solution)/shard_map/all_to_all | solution.py:107
  275.8 3.7 %fusion.10 = bf16[128,32,128]{0,2,1:T(8,128)(2,1)} fusion(f32[128,32,128]{0,2,1:T(8,128)S(1)} %copy-done.7, bf16[32,128,128]{2,1,0:T(8,128)(2,1)S(1)} %bitcast.200, f32[128,32]{0,1:T(8,128)S(1)} %copy.127, f32[128,128]{0,1:T(8,128)S(1)} %copy-done.13, f32[32,128]{1,0:T(8,128)S(1)} %copy-done.11, f32[128,32]{0,1:T(8,128)S(1)} %copy.124, ...), kind=kOutput, calls=%fused_computation.26 | convolution fusion | flops 808976384 | bytes 4325376 | tf_op jit(solution)/shard_map/transpose(jvp(hts,shp->thp))/dot_general | solution.py:54
  282.2 46.5 %all-to-all-done.3 = f32[128,32,256]{2,1,0:T(8,128)} async-done(((f32[128,32,256]{2,1,0:T(8,128)}), f32[128,32,256]{2,1,0:T(8,128)}, u32[]{:S(2)}, u32[]{:S(2)}) %all-to-all-start.3) | async-done | bytes 4194336 | tf_op jit(solution)/shard_map/all_to_all | solution.py:107
  328.7 4.6 %copy.161 = f32[4096,256]{1,0:T(8,128)} copy(f32[4096,256]{1,0:T(8,128)} %bitcast.46) | data formatting | bytes 8388608
  (98 shorter events, 36.5 us)
Async XLA Ops:
  0.6 5.0 %copy-start = (bf16[4096,256]{1,0:T(8,128)(2,1)S(1)}, bf16[4096,256]{1,0:T(8,128)(2,1)}, u32[]{:S(2)}) copy-start(bf16[4096,256]{1,0:T(8,128)(2,1)} %param.9) | copy-start | bytes 6291460
  0.6 2.8 copy-start.14
  0.7 2.9 copy-start.18
  5.6 1.9 copy-start.2
  75.3 2.0 copy-start.4
  89.5 5.7 %copy-start.3 = (f32[1,128,4096]{1,2,0:T(8,128)S(1)}, f32[1,128,4096]{1,2,0:T(8,128)}, u32[]{:S(2)}) copy-start(f32[1,128,4096]{1,2,0:T(8,128)} %copy.111) | copy-start | bytes 6291460
  89.6 55.4 %all-to-all-start.1 = ((f32[32,2,128,128]{3,2,1,0:T(8,128)}), f32[32,2,128,128]{3,2,1,0:T(8,128)}, u32[]{:S(2)}, u32[]{:S(2)}) async-start(f32[32,2,128,128]{3,2,1,0:T(8,128)} %copy.119), calls=%async_computation.1 | async-start | bytes 8388608 | tf_op jit(solution)/shard_map/all_to_all | solution.py:32
  95.0 4.1 %copy-start.10 = (f32[32,128]{1,0:T(8,128)}, f32[32,128]{1,0:T(8,128)S(1)}, u32[]{:S(2)}) copy-start(f32[32,128]{1,0:T(8,128)S(1)} %reduce_window_sum.41) | copy-start | bytes 49156
  95.1 3.9 %copy-start.15 = (pred[128,128]{0,1:T(8,128)(4,1)}, pred[128,128]{0,1:T(8,128)(4,1)S(1)}, u32[]{:S(2)}) copy-start(pred[128,128]{0,1:T(8,128)(4,1)S(1)} %iota_compare_fusion) | copy-start | bytes 49156
  95.3 3.8 %copy-start.12 = (f32[128,128]{0,1:T(8,128)}, f32[128,128]{0,1:T(8,128)S(1)}, u32[]{:S(2)}) copy-start(f32[128,128]{0,1:T(8,128)S(1)} %fusion.67) | copy-start | bytes 196612
  153.2 2.7 copy-start.8
  153.2 2.7 copy-start.9
  153.3 2.7 copy-start.17
  153.3 4.3 %copy-start.19 = (f32[32]{0:T(128)S(1)}, f32[32]{0:T(128)}, u32[]{:S(2)}) copy-start(f32[32]{0:T(128)} %param.12) | copy-start | bytes 388
  159.0 3.1 copy-start.5
  176.9 5.2 %copy-start.6 = (bf16[1,128,4096]{2,1,0:T(8,128)(2,1)S(1)}, bf16[1,128,4096]{2,1,0:T(8,128)(2,1)}, u32[]{:S(2)}) copy-start(bf16[1,128,4096]{2,1,0:T(8,128)(2,1)} %param.8) | copy-start | bytes 3145732
  270.6 5.1 %copy-start.7 = (f32[128,32,128]{0,2,1:T(8,128)S(1)}, f32[128,32,128]{0,2,1:T(8,128)}, u32[]{:S(2)}) copy-start(f32[128,32,128]{0,2,1:T(8,128)} %get-tuple-element.48) | copy-start | bytes 6291460
  270.6 5.1 %copy-start.11 = (f32[32,128]{1,0:T(8,128)S(1)}, f32[32,128]{1,0:T(8,128)}, u32[]{:S(2)}) copy-start(f32[32,128]{1,0:T(8,128)} %copy-done.10) | copy-start | bytes 49156
  270.6 5.1 %copy-start.13 = (f32[128,128]{0,1:T(8,128)S(1)}, f32[128,128]{0,1:T(8,128)}, u32[]{:S(2)}) copy-start(f32[128,128]{0,1:T(8,128)} %copy-done.12) | copy-start | bytes 196612
  270.6 5.1 %copy-start.16 = (pred[128,128]{0,1:T(8,128)(4,1)S(1)}, pred[128,128]{0,1:T(8,128)(4,1)}, u32[]{:S(2)}) copy-start(pred[128,128]{0,1:T(8,128)(4,1)} %copy-done.15) | copy-start | bytes 49156
  270.6 58.1 %all-to-all-start.3 = ((f32[128,32,256]{2,1,0:T(8,128)}), f32[128,32,256]{2,1,0:T(8,128)}, u32[]{:S(2)}, u32[]{:S(2)}) async-start(f32[128,32,256]{2,1,0:T(8,128)} %broadcast_in_dim.41), calls=%async_computation.3 | async-start | bytes 8388608 | tf_op jit(solution)/shard_map/all_to_all | solution.py:107
  328.7 4.6 %copy-start.1 = (bf16[4096,256]{1,0:T(8,128)(2,1)S(1)}, bf16[4096,256]{1,0:T(8,128)(2,1)}, u32[]{:S(2)}) copy-start(bf16[4096,256]{1,0:T(8,128)(2,1)} %param.9) | copy-start | bytes 6291460

commit v8 on v7

--- a/solution.py
+++ b/solution.py
@@ -1,23 +1,24 @@
 import jax
 import jax.numpy as jnp
 from jax import lax
-from jax.sharding import PartitionSpec as P
+from jax.sharding import Mesh, PartitionSpec as P
 
 GROUP = 128
+CHAIN = ("cz", "core")
 
 
 HIGH = lax.Precision.HIGHEST
 
 
 def exchange(log_total, own_state, back_term):
-    count, mine = (lax.axis_size("chain"), lax.axis_index("chain"))
+    count = lax.axis_size(CHAIN)
     heads, width, state = own_state.shape
     per = heads // count
     marks = jnp.broadcast_to(log_total[:, None, None], (heads, 8, state))
     both = jnp.stack(
         [jnp.concatenate([own_state, marks], axis=1), jnp.concatenate([back_term, marks], axis=1)], axis=1
     )
-    sent = lax.all_to_all(both, "chain", 0, 0, tiled=True).reshape(count, per, 2, width + 8, state)
+    sent = lax.all_to_all(both, CHAIN, 0, 0, tiled=True).reshape(count, per, 2, width + 8, state)
     parts = sent[:, :, :, :width]
     mine_logs = sent[:, :, 0, width, 0]
     edge = jnp.cumsum(mine_logs, axis=0) - mine_logs
@@ -29,7 +30,7 @@
     inc = jnp.einsum("djh,jhpn->dhpn", fwd_w, parts[:, :, 0], precision=HIGH)
     out = jnp.einsum("djh,jhpn->dhpn", bwd_w, parts[:, :, 1], precision=HIGH)
     res = jnp.stack([inc, out], axis=2).reshape(count * per, 2, width, state)
-    back = lax.all_to_all(res, "chain", 0, 0, tiled=True)
+    back = lax.all_to_all(res, CHAIN, 0, 0, tiled=True)
     return back[:, 0], back[:, 1]
 
 
@@ -93,34 +94,41 @@
     d_weight = lax.dot_general(
         tokens_here, d_bc, (((0,), (0,)), ((), ())), preferred_element_type=jnp.float32
     )
-    axes = ("chain", "dp")
+    rows, cols = d_weight.shape
+    half = rows // 2
+    core = lax.axis_index("core")
+    rate_rows = jnp.zeros((8, cols), jnp.float32).at[0, :heads].set(d_rate)
+    halves = d_weight.reshape(2, half, cols)
+    keep = jnp.concatenate([lax.dynamic_index_in_dim(halves, core, 0, keepdims=False), rate_rows], axis=0)
+    give = jnp.concatenate([lax.dynamic_index_in_dim(halves, 1 - core, 0, keepdims=False), rate_rows], axis=0)
+    paired = keep + lax.ppermute(give, "core", [(0, 1), (1, 0)])
+    axes = ("cz", "dp")
     total = lax.axis_size(axes)
-    rows, cols = d_weight.shape
-    chunk = rows // total
-    rate_rows = jnp.zeros((8, cols), jnp.float32).at[0, :heads].set(d_rate)
+    chunk = half // total
     parcel = jnp.concatenate(
-        [d_weight.reshape(total, chunk, cols), jnp.broadcast_to(rate_rows[None], (total, 8, cols))], axis=1
+        [paired[:half].reshape(total, chunk, cols), jnp.broadcast_to(paired[None, half:], (total, 8, cols))], axis=1
     )
     pieces = lax.all_to_all(parcel, axes, 0, 0, tiled=True)
     mine_sum = jnp.sum(pieces, axis=0)
     spread = jnp.broadcast_to(mine_sum[None, :chunk], (total, chunk, cols))
-    d_wbc = lax.all_to_all(spread, axes, 0, 0, tiled=True).reshape(rows, cols)
+    own_half = lax.all_to_all(spread, axes, 0, 0, tiled=True).reshape(half, cols)
+    other_half = lax.ppermute(own_half, "core", [(0, 1), (1, 0)])
+    first = core == 0
+    d_wbc = jnp.concatenate(
+        [jnp.where(first, own_half, other_half), jnp.where(first, other_half, own_half)], axis=0
+    )
     d_alog = mine_sum[chunk, :heads]
     return (d_x[None], d_wbc, d_alog)
 
 
 def solution(mesh):
+    rows, dp = mesh.devices.shape
+    split = Mesh(mesh.devices.reshape(rows // 2, 2, dp), ("cz", "core", "dp"))
+    blocks = P("dp", CHAIN, None)
     return jax.shard_map(
         per_device,
-        mesh=mesh,
-        in_specs=(
-            P("dp", "chain", None),
-            P(),
-            P("dp", "chain", None),
-            P("dp", "chain", None),
-            P(),
-            P("dp", "chain", None),
-        ),
-        out_specs=(P("dp", "chain", None), P(), P()),
+        mesh=split,
+        in_specs=(blocks, P(), blocks, blocks, P(), blocks),
+        out_specs=(blocks, P(), P()),
         check_vma=False,
     )

time: 334 us -> 317 us (0.949); the launches traced: 333 us -> 312 us
  waiting for transfers between devices: 85.2 us -> 38.9 us
  local copies, waits for them, and re-layouts: 47.2 us -> 61.1 us
  other arithmetic: 16.3 us -> 22.7 us
    all_to_all x2 -> x1, waiting for transfers between devices: 85.2 us -> 38.7 us  [exchange(): back = lax.all_to_all(res, CHAIN, 0, 0, tiled=True)]
    all_to_all x1 -> x2, blocking collectives: 63 us -> 96.5 us  [the longest x1 63.6 us: exchange(): lax.all_to_all(both, CHAIN, 0, 0, tiled=True)]
    all_to_all x1, blocking collectives: 72.1 us -> 40.1 us  [per_device(): pieces = lax.all_to_all(parcel, axes, 0, 0, tiled=True)]
    dynamic_slice x0 -> x3, local copies, waits for them, and re-layouts: none -> 19.2 us  [the longest x2 13.1 us: per_device(): lax.dynamic_index_in_dim(halves, core, 0, keepdims=False)]
    ppermute x0 -> x2, starting transfers between devices: none -> 7.07 us  [the longest x1 3.71 us: per_device(): paired = keep + lax.ppermute(give, 'core', [(0, 1), (1, 0)])]
    reshape x0 -> x1, local copies, waits for them, and re-layouts: none -> 6.8 us  [per_device(): halves = d_weight.reshape(2, half, cols)]
    dot_general x1 -> x0, local copies, waits for them, and re-layouts: 5.6 us -> none  [per_device(): lax.dot_general(tokens_here, d_bc, (((0,), (0,)), ((), ())), preferred_el...]
    all_to_all x2 -> x1, starting transfers between devices: 10.1 us -> 5.08 us  [exchange(): back = lax.all_to_all(res, CHAIN, 0, 0, tiled=True)]
  transfers between devices with their start and end apart: 2 -> 3, of which waited for: 2 -> 2; matrix products, arithmetic and copies ran while one was open for 5% -> 7% of each run, Pallas kernels for 0% -> 0%
where the time goes in v8:
time: 317 us; the launch traced here: 312 us
  blocking collectives  137 us (43%)
  local copies, waits for them, and re-layouts  61.1 us (19%)
  matrix products  39.5 us (12%)
  waiting for transfers between devices  38.9 us (12%)
  other arithmetic  22.7 us (7%)
  starting transfers between devices  12.1 us (4%)
    all_to_all x1, blocking collectives, exchange(): lax.all_to_all(both, CHAIN, 0, 0, tiled=True)  63.6 us
    all_to_all x1, blocking collectives, per_device(): pieces = lax.all_to_all(parcel, axes, 0, 0, tiled=True)  40.1 us
    all_to_all x1, waiting for transfers between devices, exchange(): back = lax.all_to_all(res, CHAIN, 0, 0, tiled=True)  38.7 us
    all_to_all x1, blocking collectives, per_device(): lax.all_to_all(spread, axes, 0, 0, tiled=True).reshape(half, cols)  32.9 us
    dynamic_slice x2, local copies, waits for them, and re-layouts, per_device(): lax.dynamic_index_in_dim(halves, core, 0, keepdims=False)  13.1 us
    dot_general x2, matrix products, block_forward(): jnp.einsum('shp,sn->hpn', inputs * tail[:, :, None], b_in, precision=HIGH)  8.82 us
    dot_general x2, matrix products, block_forward(): y_intra = jnp.einsum('hts,shp->thp', mixing, inputs, precision=HIGH)  8.61 us
    dot_general x2, matrix products, block_forward(): jnp.einsum('tn,hpn->thp', c_out, h_in, precision=HIGH)  7.66 us
  transfers between devices with their start and end apart: 3, of which 2 were waited for; matrix products, arithmetic and copies ran while one was open for 7% of the time, Pallas kernels for 0%

profile of v8, /device:TPU:1, one launch (start us, length us, event | category | flops | bytes accessed | tf_op | source)
XLA Modules:
  0.0 312.3 jit_solution(13400655210665668207)
XLA Ops:
  10.9 63.6 %all_to_all.20 = f32[32,2,136,128]{3,2,1,0:T(8,128)S(1)} all-to-all(f32[32,2,136,128]{3,2,1,0:T(8,128)S(1)} %copy.120), channel_id=1, replica_groups=mesh['cz'=16,'core'=2,'dp'=4] {'cz','core'}, dimensions={0} | all-to-all | bytes 8912896 | tf_op jit(solution)/shard_map/all_to_all | solution.py:21
  78.2 3.5 %fusion.27 = f32[32,1,1,128,128]{4,0,3,2,1:T(8,128)S(1)} fusion(f32[32,1,2,136,128]{4,0,3,2,1:T(8,128)} %bitcast.200, f32[32]{0:T(128)S(1)} %get-tuple-element.33, f32[32]{0:T(128)S(1)} %get-tuple-element.34), kind=kOutput, calls=%fused_computation.51 | convolution fusion | flops 201329664 | bytes 4194560 | tf_op jit(solution)/shard_map/djh,jhpn->dhpn/dot_general | solution.py:31
  81.7 3.5 %fusion.26 = f32[32,1,1,128,128]{4,0,3,2,1:T(8,128)S(1)} fusion(f32[32,1,2,136,128]{4,0,3,2,1:T(8,128)} %bitcast.201, f32[32]{0:T(128)S(1)} %get-tuple-element.33, f32[32]{0:T(128)S(1)} %get-tuple-element.34), kind=kOutput, calls=%fused_computation.50 | convolution fusion | flops 201329664 | bytes 4194560 | tf_op jit(solution)/shard_map/djh,jhpn->dhpn/dot_general | solution.py:30
  85.6 4.4 %copy.123 = f32[32,2,128,128]{3,2,1,0:T(8,128)} copy(f32[32,2,128,128]{3,0,2,1:T(8,128)S(1)} %maximum_bitcast_fusion) | data formatting | bytes 8388608 | tf_op jit(solution)/shard_map/reshape | solution.py:32
  90.1 5.1 %all-to-all-start.1 = ((f32[32,2,128,128]{3,2,1,0:T(8,128)}), f32[32,2,128,128]{3,2,1,0:T(8,128)}, u32[]{:S(2)}, u32[]{:S(2)}) async-start(f32[32,2,128,128]{3,2,1,0:T(8,128)} %copy.123), calls=%async_computation.1 | async-start | bytes 8388608 | tf_op jit(solution)/shard_map/all_to_all | solution.py:33
  95.9 3.8 %fusion.31 = (f32[32,128]{1,0:T(8,128)}, f32[32,128]{1,0:T(8,128)}, f32[128,128]{0,1:T(8,128)S(1)}) fusion(f32[128,128]{0,1:T(8,128)S(1)} %fusion.70, f32[32,128]{1,0:T(8,128)S(1)} %reduce_window_sum.41, pred[128,128]{0,1:T(8,128)(4,1)S(1)} %iota_compare_fusion.1, bf16[32,128,128]{2,1,0:T(8,128)(2,1)S(1)} %bitcast.203, f32[128,32,128]{0,2,1:T(8,128)S(1)} %bitcast.197, ...), kind=kOutput, calls=%fused_computation.53 | convolution fusion | flops 810524672 | bytes 3358720 | tf_op jit(solution)/shard_map/transpose(jvp(hts,shp->thp))/dot_general | solution.py:55
  103.4 2.9 copy.136
  106.8 38.7 %all-to-all-done.1 = f32[32,2,128,128]{3,2,1,0:T(8,128)} async-done(((f32[32,2,128,128]{3,2,1,0:T(8,128)}), f32[32,2,128,128]{3,2,1,0:T(8,128)}, u32[]{:S(2)}, u32[]{:S(2)}) %all-to-all-start.1) | async-done | bytes 4194336 | tf_op jit(solution)/shard_map/all_to_all | solution.py:33
  149.0 4.0 %multiply_reduce_fusion.1 = (f32[128,32]{0,1:T(8,128)S(1)}, f32[128,32,128]{0,2,1:T(8,128)}) fusion(f32[128,32,128]{0,2,1:T(8,128)S(1)} %bitcast.198, f32[128,32]{0,1:T(8,128)S(1)} %copy.131, f32[32,2,128,128]{3,2,1,0:T(8,128)} %all-to-all-done.1, bf16[128,256]{1,0:T(8,128)(2,1)S(1)} %convolution_convert_fusion), kind=kOutput, calls=%fused_computation.38 | convolution fusion | flops 806875136 | bytes 6356992 | tf_op jit(solution)/shard_map/transpose(jvp(shp,sn->hpn))/dot_general | solution.py:58
  159.6 3.1 copy.137
  167.3 2.9 mul.146
  172.6 4.8 %fusion.35 = f32[128,128]{1,0:T(8,128)S(1)} fusion(f32[32,2,128,128]{3,2,1,0:T(8,128)} %all-to-all-done.1, f32[128,32,128]{2,1,0:T(8,128)S(1)} %bitcast.207), kind=kOutput, calls=%fused_computation.56 | convolution fusion | flops 805306368 | bytes 4259840 | tf_op jit(solution)/shard_map/transpose(jvp(shp,sn->hpn))/dot_general | solution.py:58
  177.7 5.0 %fusion.32 = f32[128,128]{1,0:T(8,128)S(1)} fusion(f32[32,2,128,128]{3,2,1,0:T(8,128)} %all-to-all-done.1, f32[128,32,128]{2,1,0:T(8,128)S(1)} %bitcast.208), kind=kOutput, calls=%fused_computation.55 | convolution fusion | flops 805306368 | bytes 4259840 | tf_op jit(solution)/shard_map/transpose(jvp(tn,hpn->thp))/dot_general | solution.py:61
  182.9 2.7 convolution_bitcast_fusion
  185.6 6.8 %reshape.408 = f32[2,2048,256]{1,0,2:T(2,128)} reshape(f32[4096,256]{0,1:T(8,128)} %convolution_bitcast_fusion) | data formatting | bytes 8388608 | tf_op jit(solution)/shard_map/reshape | solution.py:101
  192.4 9.1 %constant_dynamic-slice_fusion.1 = (f32[1,2048,256]{1,0,2:T(1,128)S(1)}, f32[1,2048,256]{1,0,2:T(1,128)}) fusion(f32[2,2048,256]{1,0,2:T(2,128)} %reshape.408, s32[]{:T(128)S(6)} %select_n.71, s32[]{:T(128)S(6)} %select_n.73), kind=kLoop, calls=%fused_computation.135 | loop fusion | bytes 8388616 | tf_op jit(solution)/shard_map/jit(dynamic_index_in_dim)/dynamic_slice | solution.py:102
  201.5 6.1 %copy.146 = f32[1,2048,256]{2,1,0:T(8,128)} copy(f32[1,2048,256]{1,0,2:T(1,128)} %get-tuple-element.40) | data formatting | bytes 4194304 | tf_op jit(solution)/shard_map/jit(dynamic_index_in_dim)/dynamic_slice | solution.py:103
  207.6 3.0 fusion.3
  210.7 3.7 %collective-permute-start = (f32[2056,256]{1,0:T(8,128)}, f32[2056,256]{1,0:T(8,128)}, u32[]{:S(2)}, u32[]{:S(2)}) collective-permute-start(f32[2056,256]{1,0:T(8,128)} %fusion.3), channel_id=1, source_target_pairs={{0,4},{4,0},{1,5},{5,1},{2,6},{6,2},{3,7},{7,3},{8,12},{12,8},{9,1... | collective-permute-start | bytes 6316040 | tf_op jit(solution)/shard_map/ppermute | solution.py:104
  214.4 4.0 %copy.139 = f32[1,2048,256]{2,1,0:T(8,128)} copy(f32[1,2048,256]{1,0,2:T(1,128)S(1)} %get-tuple-element.39) | data formatting | bytes 4194304 | tf_op jit(solution)/shard_map/jit(dynamic_index_in_dim)/dynamic_slice | solution.py:102
  221.5 40.1 %all_to_all.21 = f32[64,40,256]{2,1,0:T(8,128)} all-to-all(f32[64,40,256]{2,1,0:T(8,128)S(1)} %pad_maximum_fusion.4), channel_id=1, replica_groups=mesh['cz'=16,'core'=2,'dp'=4] {'cz','dp'}, dimensions={0} | all-to-all | bytes 5242880 | tf_op jit(solution)/shard_map/all_to_all | solution.py:111
  263.8 32.9 %all_to_all.22 = f32[64,32,256]{2,1,0:T(8,128)} all-to-all(f32[64,32,256]{2,1,0:T(8,128)S(1)} %broadcast_in_dim.38), channel_id=1, replica_groups=mesh['cz'=16,'core'=2,'dp'=4] {'cz','dp'}, dimensions={0} | all-to-all | bytes 4194304 | tf_op jit(solution)/shard_map/all_to_all | solution.py:114
  296.7 3.4 %collective-permute-start.1 = (f32[2048,256]{1,0:T(8,128)}, f32[2048,256]{1,0:T(8,128)S(1)}, u32[]{:S(2)}, u32[]{:S(2)}) collective-permute-start(f32[2048,256]{1,0:T(8,128)} %bitcast.48), channel_id=1, source_target_pairs={{0,4},{4,0},{1,5},{5,1},{2,6},{6,2},{3,7},{7,3},{8,12},{12,8},{9,1... | collective-permute-start | bytes 6291464 | tf_op jit(solution)/shard_map/ppermute | solution.py:115
  300.1 4.9 %fusion.13 = bf16[128,32,128]{0,2,1:T(8,128)(2,1)} fusion(f32[128,32,128]{0,2,1:T(8,128)} %get-tuple-element.52, bf16[32,128,128]{2,1,0:T(8,128)(2,1)S(1)} %bitcast.205, f32[128,32]{0,1:T(8,128)S(1)} %copy.131, f32[128,128]{0,1:T(8,128)S(1)} %copy-done.12, f32[32,128]{1,0:T(8,128)S(1)} %copy-done.10, f32[128,32]{0,1:T(8,128)S(1)} %copy.128, ...), kind=kOutput, calls=%fused_computation.32 | convolution fusion | flops 808976384 | bytes 4325376 | tf_op jit(solution)/shard_map/transpose(jvp(hts,shp->thp))/dot_general | solution.py:55
  (106 shorter events, 48.9 us)
Async XLA Ops:
  0.6 5.0 %copy-start = (bf16[4096,256]{1,0:T(8,128)(2,1)S(1)}, bf16[4096,256]{1,0:T(8,128)(2,1)}, u32[]{:S(2)}) copy-start(bf16[4096,256]{1,0:T(8,128)(2,1)} %param.9) | copy-start | bytes 6291460
  0.6 2.8 copy-start.13
  0.7 2.9 copy-start.17
  5.6 1.9 copy-start.2
  75.9 2.0 copy-start.4
  90.1 5.8 %copy-start.3 = (f32[1,128,4096]{1,2,0:T(8,128)S(1)}, f32[1,128,4096]{1,2,0:T(8,128)}, u32[]{:S(2)}) copy-start(f32[1,128,4096]{1,2,0:T(8,128)} %copy.115) | copy-start | bytes 6291460
  90.1 55.5 %all-to-all-start.1 = ((f32[32,2,128,128]{3,2,1,0:T(8,128)}), f32[32,2,128,128]{3,2,1,0:T(8,128)}, u32[]{:S(2)}, u32[]{:S(2)}) async-start(f32[32,2,128,128]{3,2,1,0:T(8,128)} %copy.123), calls=%async_computation.1 | async-start | bytes 8388608 | tf_op jit(solution)/shard_map/all_to_all | solution.py:33
  95.6 4.1 %copy-start.9 = (f32[32,128]{1,0:T(8,128)}, f32[32,128]{1,0:T(8,128)S(1)}, u32[]{:S(2)}) copy-start(f32[32,128]{1,0:T(8,128)S(1)} %reduce_window_sum.41) | copy-start | bytes 49156
  95.7 3.9 %copy-start.14 = (pred[128,128]{0,1:T(8,128)(4,1)}, pred[128,128]{0,1:T(8,128)(4,1)S(1)}, u32[]{:S(2)}) copy-start(pred[128,128]{0,1:T(8,128)(4,1)S(1)} %iota_compare_fusion.1) | copy-start | bytes 49156
  95.9 3.8 %copy-start.11 = (f32[128,128]{0,1:T(8,128)}, f32[128,128]{0,1:T(8,128)S(1)}, u32[]{:S(2)}) copy-start(f32[128,128]{0,1:T(8,128)S(1)} %fusion.70) | copy-start | bytes 196612
  153.8 2.7 copy-start.7
  153.8 2.7 copy-start.8
  153.8 2.7 copy-start.16
  153.8 4.3 %copy-start.18 = (f32[32]{0:T(128)S(1)}, f32[32]{0:T(128)}, u32[]{:S(2)}) copy-start(f32[32]{0:T(128)} %param.12) | copy-start | bytes 388
  159.6 3.1 copy-start.5
  177.6 5.2 %copy-start.6 = (bf16[1,128,4096]{2,1,0:T(8,128)(2,1)S(1)}, bf16[1,128,4096]{2,1,0:T(8,128)(2,1)}, u32[]{:S(2)}) copy-start(bf16[1,128,4096]{2,1,0:T(8,128)(2,1)} %param.8) | copy-start | bytes 3145732
  210.7 7.9 %collective-permute-start = (f32[2056,256]{1,0:T(8,128)}, f32[2056,256]{1,0:T(8,128)}, u32[]{:S(2)}, u32[]{:S(2)}) collective-permute-start(f32[2056,256]{1,0:T(8,128)} %fusion.3), channel_id=1, source_target_pairs={{0,4},{4,0},{1,5},{5,1},{2,6},{6,2},{3,7},{7,3},{8,12},{12,8},{9,1... | collective-permute-start | bytes 6316040 | tf_op jit(solution)/shard_map/ppermute | solution.py:104
  263.8 36.3 %copy-start.10 = (f32[32,128]{1,0:T(8,128)S(1)}, f32[32,128]{1,0:T(8,128)}, u32[]{:S(2)}) copy-start(f32[32,128]{1,0:T(8,128)} %copy-done.9) | copy-start | bytes 49156
  263.8 36.3 %copy-start.12 = (f32[128,128]{0,1:T(8,128)S(1)}, f32[128,128]{0,1:T(8,128)}, u32[]{:S(2)}) copy-start(f32[128,128]{0,1:T(8,128)} %copy-done.11) | copy-start | bytes 196612
  263.8 36.3 %copy-start.15 = (pred[128,128]{0,1:T(8,128)(4,1)S(1)}, pred[128,128]{0,1:T(8,128)(4,1)}, u32[]{:S(2)}) copy-start(pred[128,128]{0,1:T(8,128)(4,1)} %copy-done.14) | copy-start | bytes 49156
  296.7 11.0 %collective-permute-start.1 = (f32[2048,256]{1,0:T(8,128)}, f32[2048,256]{1,0:T(8,128)S(1)}, u32[]{:S(2)}, u32[]{:S(2)}) collective-permute-start(f32[2048,256]{1,0:T(8,128)} %bitcast.48), channel_id=1, source_target_pairs={{0,4},{4,0},{1,5},{5,1},{2,6},{6,2},{3,7},{7,3},{8,12},{12,8},{9,1... | collective-permute-start | bytes 6291464 | tf_op jit(solution)/shard_map/ppermute | solution.py:115
  309.6 2.4 copy-start.1

commit v9 on v8

--- a/solution.py
+++ b/solution.py
@@ -91,29 +91,28 @@
 
     _, pull_all = jax.vjp(whole_block, bc, channels, a_log)
     d_bc, d_x, d_rate = pull_all((upstream, outgoing_grad))
-    d_weight = lax.dot_general(
-        tokens_here, d_bc, (((0,), (0,)), ((), ())), preferred_element_type=jnp.float32
-    )
-    rows, cols = d_weight.shape
+    rows, cols = tokens_here.shape[1], d_bc.shape[1]
     half = rows // 2
-    core = lax.axis_index("core")
+    first = lax.axis_index("core") == 0
+    top, bottom = tokens_here[:, :half], tokens_here[:, half:]
+    dims = (((0,), (0,)), ((), ()))
+    keep = lax.dot_general(jnp.where(first, top, bottom), d_bc, dims, preferred_element_type=jnp.float32)
+    give = lax.dot_general(jnp.where(first, bottom, top), d_bc, dims, preferred_element_type=jnp.float32)
     rate_rows = jnp.zeros((8, cols), jnp.float32).at[0, :heads].set(d_rate)
-    halves = d_weight.reshape(2, half, cols)
-    keep = jnp.concatenate([lax.dynamic_index_in_dim(halves, core, 0, keepdims=False), rate_rows], axis=0)
-    give = jnp.concatenate([lax.dynamic_index_in_dim(halves, 1 - core, 0, keepdims=False), rate_rows], axis=0)
-    paired = keep + lax.ppermute(give, "core", [(0, 1), (1, 0)])
+    swap = [(0, 1), (1, 0)]
+    paired = keep + lax.ppermute(give, "core", swap)
+    rate_pair = rate_rows + lax.ppermute(rate_rows, "core", swap)
     axes = ("cz", "dp")
     total = lax.axis_size(axes)
     chunk = half // total
     parcel = jnp.concatenate(
-        [paired[:half].reshape(total, chunk, cols), jnp.broadcast_to(paired[None, half:], (total, 8, cols))], axis=1
+        [paired.reshape(total, chunk, cols), jnp.broadcast_to(rate_pair[None], (total, 8, cols))], axis=1
     )
     pieces = lax.all_to_all(parcel, axes, 0, 0, tiled=True)
     mine_sum = jnp.sum(pieces, axis=0)
     spread = jnp.broadcast_to(mine_sum[None, :chunk], (total, chunk, cols))
     own_half = lax.all_to_all(spread, axes, 0, 0, tiled=True).reshape(half, cols)
-    other_half = lax.ppermute(own_half, "core", [(0, 1), (1, 0)])
-    first = core == 0
+    other_half = lax.ppermute(own_half, "core", swap)
     d_wbc = jnp.concatenate(
         [jnp.where(first, own_half, other_half), jnp.where(first, other_half, own_half)], axis=0
     )

time: 317 us -> 288 us (0.909)
  local copies, waits for them, and re-layouts: 61.1 us -> 33.8 us
  other arithmetic: 22.7 us -> 16.6 us
  waiting for transfers between devices: 38.9 us -> 43.2 us
    dynamic_slice x3 -> x0, local copies, waits for them, and re-layouts: 19.2 us -> none  [the longest x2 13.1 us: per_device(): lax.dynamic_index_in_dim(halves, core, 0, keepdims=False)]
    reshape x1 -> x0, local copies, waits for them, and re-layouts: 6.8 us -> none  [per_device(): halves = d_weight.reshape(2, half, cols)]
    ppermute x2 -> x3, starting transfers between devices: 7.07 us -> 7.16 us  [the longest x1 3.72 us: per_device(): paired = keep + lax.ppermute(give, 'core', swap)]
    unnamed x43 -> x53, local copies, waits for them, and re-layouts: 7.07 us -> 7.09 us
  transfers between devices with their start and end apart: 3 -> 4, of which waited for: 2 -> 2; matrix products, arithmetic and copies ran while one was open for 7% -> 6% of each run, Pallas kernels for 0% -> 0%
where the time goes in v9:
time: 288 us; the launch traced here: 283 us
  blocking collectives  137 us (48%)
  waiting for transfers between devices  43.2 us (15%)
  matrix products  39.2 us (14%)
  local copies, waits for them, and re-layouts  33.8 us (12%)
  other arithmetic  16.6 us (6%)
  starting transfers between devices  12.2 us (4%)
    all_to_all x1, blocking collectives, exchange(): lax.all_to_all(both, CHAIN, 0, 0, tiled=True)  63.6 us
    all_to_all x1, waiting for transfers between devices, exchange(): back = lax.all_to_all(res, CHAIN, 0, 0, tiled=True)  40.6 us
    all_to_all x1, blocking collectives, per_device(): pieces = lax.all_to_all(parcel, axes, 0, 0, tiled=True)  40.4 us
    all_to_all x1, blocking collectives, per_device(): lax.all_to_all(spread, axes, 0, 0, tiled=True).reshape(half, cols)  32.9 us
    dot_general x2, matrix products, block_forward(): jnp.einsum('shp,sn->hpn', inputs * tail[:, :, None], b_in, precision=HIGH)  8.81 us
    dot_general x2, matrix products, block_forward(): jnp.einsum('tn,hpn->thp', c_out, h_in, precision=HIGH)  7.66 us
    unnamed x53, local copies, waits for them, and re-layouts  7.09 us
    dot_general x2, matrix products, block_forward(): y_intra = jnp.einsum('hts,shp->thp', mixing, inputs, precision=HIGH)  6.83 us
  transfers between devices with their start and end apart: 4, of which 2 were waited for; matrix products, arithmetic and copies ran while one was open for 6% of the time, Pallas kernels for 0%

profile of v9, /device:TPU:1, one launch (start us, length us, event | category | flops | bytes accessed | tf_op | source)
XLA Modules:
  0.0 283.3 jit_solution(10420781364015679473)
XLA Ops:
  0.7 2.7 copy.115
  10.9 63.6 %all_to_all.20 = f32[32,2,136,128]{3,2,1,0:T(8,128)S(1)} all-to-all(f32[32,2,136,128]{3,2,1,0:T(8,128)S(1)} %copy.120), channel_id=1, replica_groups=mesh['cz'=16,'core'=2,'dp'=4] {'cz','core'}, dimensions={0} | all-to-all | bytes 8912896 | tf_op jit(solution)/shard_map/all_to_all | solution.py:21
  78.2 3.5 %fusion.24 = f32[32,1,1,128,128]{4,0,3,2,1:T(8,128)S(1)} fusion(f32[32,1,2,136,128]{4,0,3,2,1:T(8,128)} %bitcast.192, f32[32]{0:T(128)S(1)} %get-tuple-element.33, f32[32]{0:T(128)S(1)} %get-tuple-element.34), kind=kOutput, calls=%fused_computation.46 | convolution fusion | flops 201329664 | bytes 4194560 | tf_op jit(solution)/shard_map/djh,jhpn->dhpn/dot_general | solution.py:31
  81.7 3.5 %fusion.23 = f32[32,1,1,128,128]{4,0,3,2,1:T(8,128)S(1)} fusion(f32[32,1,2,136,128]{4,0,3,2,1:T(8,128)} %bitcast.193, f32[32]{0:T(128)S(1)} %get-tuple-element.33, f32[32]{0:T(128)S(1)} %get-tuple-element.34), kind=kOutput, calls=%fused_computation.45 | convolution fusion | flops 201329664 | bytes 4194560 | tf_op jit(solution)/shard_map/djh,jhpn->dhpn/dot_general | solution.py:30
  85.6 4.4 %copy.123 = f32[32,2,128,128]{3,2,1,0:T(8,128)} copy(f32[32,2,128,128]{3,0,2,1:T(8,128)S(1)} %maximum_bitcast_fusion) | data formatting | bytes 8388608 | tf_op jit(solution)/shard_map/reshape | solution.py:32
  90.1 5.1 %all-to-all-start.1 = ((f32[32,2,128,128]{3,2,1,0:T(8,128)}), f32[32,2,128,128]{3,2,1,0:T(8,128)}, u32[]{:S(2)}, u32[]{:S(2)}) async-start(f32[32,2,128,128]{3,2,1,0:T(8,128)} %copy.123), calls=%async_computation.1 | async-start | bytes 8388608 | tf_op jit(solution)/shard_map/all_to_all | solution.py:33
  95.9 3.2 %fusion.28 = (f32[32,128]{1,0:T(8,128)S(1)}, f32[32,128]{1,0:T(8,128)S(1)}, f32[128,128]{0,1:T(8,128)S(1)}) fusion(f32[128,128]{0,1:T(8,128)S(1)} %fusion.71, f32[32,128]{1,0:T(8,128)S(1)} %reduce_window_sum.41, pred[128,128]{0,1:T(8,128)(4,1)S(1)} %iota_compare_fusion, bf16[32,128,128]{2,1,0:T(8,128)(2,1)S(1)} %bitcast.195, ...), kind=kOutput, calls=%fused_computation.48 | convolution fusion | flops 810524672 | bytes 3358720 | tf_op jit(solution)/shard_map/transpose(jvp(hts,shp->thp))/dot_general | solution.py:55
  102.0 2.9 %copy.136 = f32[1,128,4096]{2,1,0:T(8,128)} copy(f32[1,128,4096]{1,2,0:T(8,128)} %bitcast.201) | data formatting | bytes 4194304 | tf_op jit(solution)/shard_map/transpose(jvp())/mul | solution.py:46
  104.9 40.6 %all-to-all-done.1 = f32[32,2,128,128]{3,2,1,0:T(8,128)} async-done(((f32[32,2,128,128]{3,2,1,0:T(8,128)}), f32[32,2,128,128]{3,2,1,0:T(8,128)}, u32[]{:S(2)}, u32[]{:S(2)}) %all-to-all-start.1) | async-done | bytes 4194336 | tf_op jit(solution)/shard_map/all_to_all | solution.py:33
  145.6 2.7 fusion.3
  149.0 4.0 %multiply_reduce_fusion.1 = (f32[128,32]{0,1:T(8,128)S(1)}, f32[128,32,128]{0,2,1:T(8,128)}) fusion(f32[128,32,128]{0,2,1:T(8,128)S(1)} %bitcast.190, f32[128,32]{0,1:T(8,128)S(1)} %copy.131, f32[32,2,128,128]{3,2,1,0:T(8,128)} %all-to-all-done.1, bf16[128,256]{1,0:T(8,128)(2,1)S(1)} %convolution_convert_fusion), kind=kOutput, calls=%fused_computation.33 | convolution fusion | flops 806875136 | bytes 6356992 | tf_op jit(solution)/shard_map/transpose(jvp(shp,sn->hpn))/dot_general | solution.py:58
  153.2 2.6 multiply_reduce_fusion
  157.5 3.1 %copy.137 = f32[1,128,4096]{2,1,0:T(8,128)} copy(f32[1,128,4096]{1,2,0:T(8,128)} %bitcast.202) | data formatting | bytes 4194304 | tf_op jit(solution)/shard_map/transpose(jvp())/mul | solution.py:58
  165.1 2.9 %mul.146 = f32[1,128,4096]{2,1,0:T(8,128)} reshape(f32[128,32,128]{2,1,0:T(8,128)} %mul.145) | data formatting | bytes 4194304 | tf_op jit(solution)/shard_map/transpose(jvp())/mul | solution.py:61
  170.5 4.8 %fusion.32 = f32[128,128]{1,0:T(8,128)S(1)} fusion(f32[32,2,128,128]{3,2,1,0:T(8,128)} %all-to-all-done.1, f32[128,32,128]{2,1,0:T(8,128)S(1)} %bitcast.199), kind=kOutput, calls=%fused_computation.51 | convolution fusion | flops 805306368 | bytes 4259840 | tf_op jit(solution)/shard_map/transpose(jvp(shp,sn->hpn))/dot_general | solution.py:58
  175.5 5.0 %fusion.29 = f32[128,128]{1,0:T(8,128)S(1)} fusion(f32[32,2,128,128]{3,2,1,0:T(8,128)} %all-to-all-done.1, f32[128,32,128]{2,1,0:T(8,128)S(1)} %bitcast.200), kind=kOutput, calls=%fused_computation.50 | convolution fusion | flops 805306368 | bytes 4259840 | tf_op jit(solution)/shard_map/transpose(jvp(tn,hpn->thp))/dot_general | solution.py:61
  182.6 3.7 %collective-permute-start = (f32[2048,256]{1,0:T(8,128)}, f32[2048,256]{1,0:T(8,128)}, u32[]{:S(2)}, u32[]{:S(2)}) collective-permute-start(f32[2048,256]{1,0:T(8,128)} %fusion.45), channel_id=1, source_target_pairs={{0,4},{4,0},{1,5},{5,1},{2,6},{6,2},{3,7},{7,3},{8,12},{12,8},{9,1... | collective-permute-start | bytes 6291464 | tf_op jit(solution)/shard_map/ppermute | solution.py:103
  188.0 2.5 collective-permute-done.1
  190.6 2.4 convolution_add_fusion
  193.4 40.4 %all_to_all.21 = f32[64,40,256]{2,1,0:T(8,128)} all-to-all(f32[64,40,256]{2,1,0:T(8,128)S(1)} %pad_maximum_fusion.4), channel_id=1, replica_groups=mesh['cz'=16,'core'=2,'dp'=4] {'cz','dp'}, dimensions={0} | all-to-all | bytes 5242880 | tf_op jit(solution)/shard_map/all_to_all | solution.py:111
  235.9 32.9 %all_to_all.22 = f32[64,32,256]{2,1,0:T(8,128)} all-to-all(f32[64,32,256]{2,1,0:T(8,128)S(1)} %broadcast_in_dim.38), channel_id=1, replica_groups=mesh['cz'=16,'core'=2,'dp'=4] {'cz','dp'}, dimensions={0} | all-to-all | bytes 4194304 | tf_op jit(solution)/shard_map/all_to_all | solution.py:114
  268.9 3.4 %collective-permute-start.2 = (f32[2048,256]{1,0:T(8,128)}, f32[2048,256]{1,0:T(8,128)S(1)}, u32[]{:S(2)}, u32[]{:S(2)}) collective-permute-start(f32[2048,256]{1,0:T(8,128)} %bitcast.45), channel_id=1, source_target_pairs={{0,4},{4,0},{1,5},{5,1},{2,6},{6,2},{3,7},{7,3},{8,12},{12,8},{9,1... | collective-permute-start | bytes 6291464 | tf_op jit(solution)/shard_map/ppermute | solution.py:115
  272.3 3.7 %fusion.10 = bf16[128,32,128]{0,2,1:T(8,128)(2,1)} fusion(f32[128,32,128]{0,2,1:T(8,128)S(1)} %copy-done.7, bf16[32,128,128]{2,1,0:T(8,128)(2,1)S(1)} %bitcast.197, f32[128,32]{0,1:T(8,128)S(1)} %copy.131, f32[128,128]{0,1:T(8,128)S(1)} %copy-done.16, f32[32,128]{1,0:T(8,128)S(1)} %copy-done.14, f32[128,32]{0,1:T(8,128)S(1)} %copy-done.12, ...), kind=kOutput, calls=%fused_computation.27 | convolution fusion | flops 808976384 | bytes 4325376 | tf_op jit(solution)/shard_map/transpose(jvp(hts,shp->thp))/dot_general | solution.py:55
  280.6 2.3 pad_maximum_fusion.1
  (114 shorter events, 36.0 us)
Async XLA Ops:
  0.6 5.0 %copy-start = (bf16[4096,256]{1,0:T(8,128)(2,1)S(1)}, bf16[4096,256]{1,0:T(8,128)(2,1)}, u32[]{:S(2)}) copy-start(bf16[4096,256]{1,0:T(8,128)(2,1)} %param.9) | copy-start | bytes 6291460
  0.6 2.8 copy-start.17
  0.7 2.9 %copy-start.22 = (f32[32]{0:T(128)S(1)}, f32[32]{0:T(128)}, u32[]{:S(2)}) copy-start(f32[32]{0:T(128)} %param.12) | copy-start | bytes 388
  90.1 5.8 %copy-start.3 = (f32[1,128,4096]{1,2,0:T(8,128)S(1)}, f32[1,128,4096]{1,2,0:T(8,128)}, u32[]{:S(2)}) copy-start(f32[1,128,4096]{1,2,0:T(8,128)} %copy.115) | copy-start | bytes 6291460
  90.1 55.5 %all-to-all-start.1 = ((f32[32,2,128,128]{3,2,1,0:T(8,128)}), f32[32,2,128,128]{3,2,1,0:T(8,128)}, u32[]{:S(2)}, u32[]{:S(2)}) async-start(f32[32,2,128,128]{3,2,1,0:T(8,128)} %copy.123), calls=%async_computation.1 | async-start | bytes 8388608 | tf_op jit(solution)/shard_map/all_to_all | solution.py:33
  95.6 3.5 %copy-start.13 = (f32[32,128]{1,0:T(8,128)}, f32[32,128]{1,0:T(8,128)S(1)}, u32[]{:S(2)}) copy-start(f32[32,128]{1,0:T(8,128)S(1)} %reduce_window_sum.41) | copy-start | bytes 49156
  95.7 3.3 %copy-start.18 = (pred[128,128]{0,1:T(8,128)(4,1)}, pred[128,128]{0,1:T(8,128)(4,1)S(1)}, u32[]{:S(2)}) copy-start(pred[128,128]{0,1:T(8,128)(4,1)S(1)} %iota_compare_fusion) | copy-start | bytes 49156
  95.9 3.2 %copy-start.15 = (f32[128,128]{0,1:T(8,128)}, f32[128,128]{0,1:T(8,128)S(1)}, u32[]{:S(2)}) copy-start(f32[128,128]{0,1:T(8,128)S(1)} %fusion.71) | copy-start | bytes 196612
  104.9 48.2 %copy-start.20 = (f32[32]{0:T(128)}, f32[32]{0:T(128)S(1)}, u32[]{:S(2)}) copy-start(f32[32]{0:T(128)S(1)} %slice_bitcast_fusion.23) | copy-start | bytes 388
  153.1 2.7 copy-start.8
  153.1 2.7 copy-start.9
  153.2 2.7 copy-start.10
  156.0 4.6 %copy-start.11 = (f32[128,32]{0,1:T(8,128)}, f32[128,32]{0,1:T(8,128)S(1)}, u32[]{:S(2)}) copy-start(f32[128,32]{0,1:T(8,128)S(1)} %copy.128) | copy-start | bytes 49156
  157.5 3.1 %copy-start.5 = (f32[1,128,4096]{2,1,0:T(8,128)S(1)}, f32[1,128,4096]{2,1,0:T(8,128)}, u32[]{:S(2)}) copy-start(f32[1,128,4096]{2,1,0:T(8,128)} %copy.136) | copy-start | bytes 6291460
  175.5 5.2 %copy-start.6 = (bf16[1,128,4096]{2,1,0:T(8,128)(2,1)S(1)}, bf16[1,128,4096]{2,1,0:T(8,128)(2,1)}, u32[]{:S(2)}) copy-start(bf16[1,128,4096]{2,1,0:T(8,128)(2,1)} %param.8) | copy-start | bytes 3145732
  180.5 7.3 %copy-start.23 = (f32[32]{0:T(128)S(1)}, f32[32]{0:T(128)}, u32[]{:S(2)}) copy-start(f32[32]{0:T(128)} %param.12) | copy-start | bytes 388
  182.6 8.0 %collective-permute-start = (f32[2048,256]{1,0:T(8,128)}, f32[2048,256]{1,0:T(8,128)}, u32[]{:S(2)}, u32[]{:S(2)}) collective-permute-start(f32[2048,256]{1,0:T(8,128)} %fusion.45), channel_id=1, source_target_pairs={{0,4},{4,0},{1,5},{5,1},{2,6},{6,2},{3,7},{7,3},{8,12},{12,8},{9,1... | collective-permute-start | bytes 6291464 | tf_op jit(solution)/shard_map/ppermute | solution.py:103
  187.9 2.6 collective-permute-start.1
  235.9 36.3 %copy-start.7 = (f32[128,32,128]{0,2,1:T(8,128)S(1)}, f32[128,32,128]{0,2,1:T(8,128)}, u32[]{:S(2)}) copy-start(f32[128,32,128]{0,2,1:T(8,128)} %get-tuple-element.50) | copy-start | bytes 6291460
  235.9 36.3 %copy-start.12 = (f32[128,32]{0,1:T(8,128)S(1)}, f32[128,32]{0,1:T(8,128)}, u32[]{:S(2)}) copy-start(f32[128,32]{0,1:T(8,128)} %copy-done.11) | copy-start | bytes 49156
  235.9 36.3 %copy-start.14 = (f32[32,128]{1,0:T(8,128)S(1)}, f32[32,128]{1,0:T(8,128)}, u32[]{:S(2)}) copy-start(f32[32,128]{1,0:T(8,128)} %copy-done.13) | copy-start | bytes 49156
  235.9 36.3 %copy-start.16 = (f32[128,128]{0,1:T(8,128)S(1)}, f32[128,128]{0,1:T(8,128)}, u32[]{:S(2)}) copy-start(f32[128,128]{0,1:T(8,128)} %copy-done.15) | copy-start | bytes 196612
  235.9 36.3 %copy-start.19 = (pred[128,128]{0,1:T(8,128)(4,1)S(1)}, pred[128,128]{0,1:T(8,128)(4,1)}, u32[]{:S(2)}) copy-start(pred[128,128]{0,1:T(8,128)(4,1)} %copy-done.18) | copy-start | bytes 49156
  268.9 9.8 %collective-permute-start.2 = (f32[2048,256]{1,0:T(8,128)}, f32[2048,256]{1,0:T(8,128)S(1)}, u32[]{:S(2)}, u32[]{:S(2)}) collective-permute-start(f32[2048,256]{1,0:T(8,128)} %bitcast.45), channel_id=1, source_target_pairs={{0,4},{4,0},{1,5},{5,1},{2,6},{6,2},{3,7},{7,3},{8,12},{12,8},{9,1... | collective-permute-start | bytes 6291464 | tf_op jit(solution)/shard_map/ppermute | solution.py:115
  (4 other events, 9.1 us)

commit v10 on v9

--- a/solution.py
+++ b/solution.py
@@ -11,27 +11,36 @@
 
 
 def exchange(log_total, own_state, back_term):
-    count = lax.axis_size(CHAIN)
     heads, width, state = own_state.shape
+    first = lax.axis_index("core") == 0
+    swap = [(0, 1), (1, 0)]
+
+    def marked(value, logs):
+        return jnp.concatenate([value, jnp.broadcast_to(logs[:, None, None], (heads, 8, state))], axis=1)
+
+    got = lax.ppermute(marked(jnp.where(first, own_state, back_term), log_total), "core", swap)
+    partner = got[:, :width]
+    partner_log = got[:, width, 0]
+    pair_log = log_total + partner_log
+    mine = jnp.where(first, back_term, own_state)
+    combined = mine + jnp.exp(log_total)[:, None, None] * partner
+    count = lax.axis_size("cz")
     per = heads // count
-    marks = jnp.broadcast_to(log_total[:, None, None], (heads, 8, state))
-    both = jnp.stack(
-        [jnp.concatenate([own_state, marks], axis=1), jnp.concatenate([back_term, marks], axis=1)], axis=1
-    )
-    sent = lax.all_to_all(both, CHAIN, 0, 0, tiled=True).reshape(count, per, 2, width + 8, state)
-    parts = sent[:, :, :, :width]
-    mine_logs = sent[:, :, 0, width, 0]
-    edge = jnp.cumsum(mine_logs, axis=0) - mine_logs
-    after = edge + mine_logs
+    sent = lax.all_to_all(marked(combined, pair_log), "cz", 0, 0, tiled=True).reshape(count, per, width + 8, state)
+    parts = sent[:, :, :width]
+    chip_logs = sent[:, :, width, 0]
+    edge = jnp.cumsum(chip_logs, axis=0) - chip_logs
+    after = edge + chip_logs
     pos = jnp.arange(count, dtype=jnp.int32)
     earlier = pos[None, :] < pos[:, None]
     fwd_w = jnp.exp(jnp.where(earlier[:, :, None], edge[:, None, :] - after[None, :, :], -jnp.inf))
     bwd_w = jnp.exp(jnp.where(earlier.T[:, :, None], edge[None, :, :] - after[:, None, :], -jnp.inf))
-    inc = jnp.einsum("djh,jhpn->dhpn", fwd_w, parts[:, :, 0], precision=HIGH)
-    out = jnp.einsum("djh,jhpn->dhpn", bwd_w, parts[:, :, 1], precision=HIGH)
-    res = jnp.stack([inc, out], axis=2).reshape(count * per, 2, width, state)
-    back = lax.all_to_all(res, CHAIN, 0, 0, tiled=True)
-    return back[:, 0], back[:, 1]
+    weight = jnp.where(first, bwd_w, fwd_w)
+    res = jnp.einsum("djh,jhpn->dhpn", weight, parts, precision=HIGH).reshape(count * per, width, state)
+    back = lax.all_to_all(res, "cz", 0, 0, tiled=True)
+    other = lax.ppermute(back, "core", swap)
+    fixed = jnp.exp(partner_log)[:, None, None] * back + partner
+    return jnp.where(first, other, fixed), jnp.where(first, fixed, other)
 
 
 def block_forward(bc, x, dt_raw, a_log, h_in):

time: 288 us -> 243 us (0.84); the launches traced: 283 us -> 242 us
  blocking collectives: 137 us -> 105 us
  local copies, waits for them, and re-layouts: 33.8 us -> 20.1 us
  other arithmetic: 16.6 us -> 23.2 us
  starting transfers between devices: 12.2 us -> 15.6 us
    all_to_all x1, blocking collectives: 63.6 us -> 30.4 us  [exchange(): back = lax.all_to_all(res, 'cz', 0, 0, tiled=True)]
    mul x6 -> x0, local copies, waits for them, and re-layouts: 13.9 us -> none  [the longest x2 4.88 us: block_forward(): jnp.einsum('tn,hpn->thp', c_out, h_in, precision=HIGH)]
    all_to_all x1, waiting for transfers between devices: 40.6 us -> 34.3 us  [exchange(): lax.all_to_all(marked(combined, pair_log), 'cz', 0, 0, tiled=True)]
    reshape x1 -> x0, local copies, waits for them, and re-layouts: 4.44 us -> none  [exchange(): res = jnp.stack([inc, out], axis=2).reshape(count * per, 2, width, state)]
    unnamed x2 -> x0, other arithmetic: 4.3 us -> none
    ppermute x0 -> x2, waiting for transfers between devices: none -> 4.22 us  [the longest x1 4.22 us: exchange(): lax.ppermute(marked(jnp.where(first, own_state, back_term), log_total), '...]
    slice x0 -> x2, local copies, waits for them, and re-layouts: none -> 4.05 us  [the longest x1 3.14 us: exchange(): parts = sent[:, :, :width]]
    ppermute x0 -> x2, starting transfers between devices: none -> 3.73 us  [the longest x1 2.35 us: exchange(): other = lax.ppermute(back, 'core', swap)]
  transfers between devices with their start and end apart: 4 -> 6, of which waited for: 2 -> 3; matrix products, arithmetic and copies ran while one was open for 6% -> 7% of each run, Pallas kernels for 0% -> 0%
where the time goes in v10:
time: 243 us; the launch traced here: 242 us
  blocking collectives  105 us (43%)
  waiting for transfers between devices  40.7 us (17%)
  matrix products  37.3 us (15%)
  other arithmetic  23.2 us (10%)
  local copies, waits for them, and re-layouts  20.1 us (8%)
  starting transfers between devices  15.6 us (6%)
    all_to_all x1, blocking collectives, per_device(): pieces = lax.all_to_all(parcel, axes, 0, 0, tiled=True)  41.2 us
    all_to_all x1, waiting for transfers between devices, exchange(): lax.all_to_all(marked(combined, pair_log), 'cz', 0, 0, tiled=True)  34.3 us
    all_to_all x1, blocking collectives, per_device(): lax.all_to_all(spread, axes, 0, 0, tiled=True).reshape(half, cols)  32.9 us
    all_to_all x1, blocking collectives, exchange(): back = lax.all_to_all(res, 'cz', 0, 0, tiled=True)  30.4 us
    dot_general x2, matrix products, block_forward(): jnp.einsum('shp,sn->hpn', inputs * tail[:, :, None], b_in, precision=HIGH)  8.61 us
    all_to_all x1, starting transfers between devices, exchange(): lax.all_to_all(marked(combined, pair_log), 'cz', 0, 0, tiled=True)  7.75 us
    dot_general x2, matrix products, block_forward(): y_intra = jnp.einsum('hts,shp->thp', mixing, inputs, precision=HIGH)  7.65 us
    dot_general x2, matrix products, block_forward(): jnp.einsum('tn,hpn->thp', c_out, h_in, precision=HIGH)  5.29 us
  transfers between devices with their start and end apart: 6, of which 3 were waited for; matrix products, arithmetic and copies ran while one was open for 7% of the time, Pallas kernels for 0%

profile of v10, /device:TPU:1, one launch (start us, length us, event | category | flops | bytes accessed | tf_op | source)
XLA Modules:
  0.0 242.4 jit_solution(11221519265475479663)
XLA Ops:
  0.7 2.7 %copy.121 = f32[1,128,4096]{1,2,0:T(8,128)} copy(bf16[1,128,4096]{2,1,0:T(8,128)(2,1)} %param.10) | data formatting | bytes 3145728 | tf_op jit(solution)/shard_map/convert_element_type | solution.py:92
  9.4 2.4 %broadcast_select_fusion.4 = (f32[32,128,128]{2,1,0:T(8,128)S(1)}, f32[32,128,128]{2,1,0:T(8,128)}) fusion(f32[32,128,128]{2,1,0:T(8,128)S(1)} %fusion, pred[]{:T(512)S(6)} %eq.4, bf16[128,256]{1,0:T(8,128)(2,1)S(1)} %convolution_convert_fusion, f32[128,32,128]{0,2,1:T(8,128)S(1)} %bitcast.141, f32[128,32]{0,1:T(8,128)S(1)} %copy.123), kind=kOutput, calls=%fused_computation.60 | convolution fusion | flops 806354944 | bytes 8437761 | tf_op jit(solution)/shard_map/thp,tn->hpn/dot_general | solution.py:93
  14.9 4.2 %collective-permute-done = f32[32,136,128]{2,1,0:T(8,128)} collective-permute-done((f32[32,136,128]{2,1,0:T(8,128)}, f32[32,136,128]{2,1,0:T(8,128)}, u32[]{:S(2)}, u32[]{:S(2)}) %collective-permute-start) | collective-permute-done | bytes 2228256 | tf_op jit(solution)/shard_map/ppermute | solution.py:21
  20.9 2.6 %multiply_add_fusion.1 = f32[32,128,128]{2,1,0:T(8,128)S(1)} fusion(f32[32,128,128]{2,1,0:T(8,128)} %copy-done.4, f32[32,128,128]{2,1,0:T(8,128)} %get-tuple-element.53, f32[32,136,128]{2,1,0:T(8,128)} %collective-permute-done, f32[32]{0:T(128)S(1)} %fusion.106, pred[]{:T(512)S(6)} %eq.4), kind=kLoop, calls=%fused_computation.29 | loop fusion | flops 1572864 | bytes 8388737 | tf_op jit(solution)/shard_map/add | solution.py:26
  25.1 7.8 %all-to-all-start = ((f32[32,136,128]{2,1,0:T(8,128)}), f32[32,136,128]{2,1,0:T(8,128)}, u32[]{:S(2)}, u32[]{:S(2)}) async-start(f32[32,136,128]{2,1,0:T(8,128)} %pad_maximum_fusion.3), calls=%async_computation | async-start | bytes 4456448 | tf_op jit(solution)/shard_map/all_to_all | solution.py:29
  32.9 34.3 %all-to-all-done = f32[32,136,128]{2,1,0:T(8,128)} async-done(((f32[32,136,128]{2,1,0:T(8,128)}), f32[32,136,128]{2,1,0:T(8,128)}, u32[]{:S(2)}, u32[]{:S(2)}) %all-to-all-start) | async-done | bytes 2228256 | tf_op jit(solution)/shard_map/all_to_all | solution.py:29
  67.1 3.1 %slice.73 = f32[16,2,128,128]{3,2,1,0:T(8,128)} slice(f32[16,2,136,128]{3,2,1,0:T(8,128)} %bitcast.8), slice={[0:16], [0:2], [0:128], [0:128]} | slice | bytes 4194304 | tf_op jit(solution)/shard_map/slice | solution.py:30
  71.6 4.7 %fusion.19 = f32[16,2,128,128]{3,0,2,1:T(8,128)S(1)} fusion(f32[16,2,128,128]{3,2,1,0:T(8,128)} %slice.73, f32[16,2]{0,1:T(2,128)S(1)} %copy.133, f32[16,2]{0,1:T(2,128)S(1)} %copy.131, pred[16,16]{1,0:T(8,128)(4,1)S(1)} %get-tuple-element.56, pred[16,16]{1,0:T(8,128)(4,1)S(1)} %get-tuple-element.57, pred[]{:T(512)S(6)} %eq.4), kind=kOutput, calls=%fused_computation.35 | convolution fusion | flops 100665856 | bytes 4195073 | tf_op jit(solution)/shard_map/djh,jhpn->dhpn/dot_general | solution.py:39
  76.9 30.4 %all_to_all.20 = f32[32,128,128]{2,1,0:T(8,128)} all-to-all(f32[32,128,128]{2,1,0:T(8,128)S(1)} %bitcast.151), channel_id=1, replica_groups=mesh['cz'=16,'core'=2,'dp'=4] {'cz'}, dimensions={0} | all-to-all | bytes 4194304 | tf_op jit(solution)/shard_map/all_to_all | solution.py:40
  107.4 2.3 collective-permute-start.1
  110.4 4.0 %fusion.23 = (f32[32,128]{1,0:T(8,128)}, f32[32,128]{1,0:T(8,128)S(1)}, f32[128,128]{0,1:T(8,128)}) fusion(f32[128,128]{0,1:T(8,128)S(1)} %fusion.77, f32[32,128]{1,0:T(8,128)S(1)} %reduce_window_sum.46, pred[128,128]{0,1:T(8,128)(4,1)S(1)} %iota_compare_fusion, bf16[32,128,128]{2,1,0:T(8,128)(2,1)S(1)} %bitcast.146, f32[128,32,128]{0,2,1:T(8,128)S(1)} %bitcast.142, ...), kind=kOutput, calls=%fused_computation.37 | convolution fusion | flops 810524672 | bytes 3358720 | tf_op jit(solution)/shard_map/transpose(jvp(hts,shp->thp))/dot_general | solution.py:64
  118.7 4.0 %multiply_reduce_fusion = (f32[32]{0:T(128)}, f32[32,128,128]{2,1,0:T(8,128)S(1)}, f32[32,128,128]{2,1,0:T(8,128)S(1)}) fusion(f32[32,128,128]{2,1,0:T(8,128)} %collective-permute-done.1, f32[32,136,128]{2,1,0:T(8,128)} %collective-permute-done, f32[32,128,128]{2,1,0:T(8,128)} %all_to_all.20, f32[32]{0:T(128)} %get-tuple-element.30, pred[]{:T(512)S(6)} %eq.4), kind=kLoop, calls=%fused_computation.21 | loop fusion | flops 3145696 | bytes 10486017 | tf_op jit(solution)/shard_map/transpose(jvp())/reduce_sum | solution.py:68
  122.7 3.3 %multiply_reduce_fusion.1 = (f32[128,32]{0,1:T(8,128)}, f32[128,32,128]{0,2,1:T(8,128)}) fusion(f32[128,32,128]{0,2,1:T(8,128)S(1)} %bitcast.143, f32[128,32]{0,1:T(8,128)S(1)} %copy.143, f32[32,128,128]{2,1,0:T(8,128)S(1)} %get-tuple-element.37, bf16[128,256]{1,0:T(8,128)(2,1)S(1)} %convolution_convert_fusion), kind=kOutput, calls=%fused_computation.22 | convolution fusion | flops 806875136 | bytes 6356992 | tf_op jit(solution)/shard_map/transpose(jvp(shp,sn->hpn))/dot_general | solution.py:67
  135.2 5.3 %fusion.33 = bf16[128,128]{1,0:T(8,128)(2,1)S(1)} fusion(f32[128,128]{1,0:T(8,128)S(1)} %fusion.75, f32[32,128,128]{2,1,0:T(8,128)} %copy-done.3, f32[128,32,128]{0,2,1:T(8,128)S(1)} %bitcast.144, f32[128,32]{0,1:T(8,128)S(1)} %copy.143, f32[128,32]{0,1:T(8,128)S(1)} %copy.140), kind=kOutput, calls=%fused_computation.44 | convolution fusion | flops 806387712 | bytes 4325376 | tf_op jit(solution)/shard_map/transpose(jvp(shp,sn->hpn))/dot_general | solution.py:67
  140.6 3.6 %fusion.32 = bf16[128,128]{1,0:T(8,128)(2,1)S(1)} fusion(f32[128,128]{1,0:T(8,128)S(1)} %copy-done.10, f32[32,128,128]{2,1,0:T(8,128)S(1)} %copy-done.6, bf16[128,32,128]{0,2,1:T(8,128)(2,1)S(1)} %bitcast.148, f32[128,32]{0,1:T(8,128)S(1)} %copy.145), kind=kOutput, calls=%fused_computation.43 | convolution fusion | flops 806387712 | bytes 3260416 | tf_op jit(solution)/shard_map/transpose(jvp(tn,hpn->thp))/dot_general | solution.py:70
  147.1 2.2 collective-permute-done.3
  149.4 2.4 convolution_add_fusion
  152.2 41.2 %all_to_all.21 = f32[64,40,256]{2,1,0:T(8,128)} all-to-all(f32[64,40,256]{2,1,0:T(8,128)S(1)} %pad_maximum_fusion.1), channel_id=1, replica_groups=mesh['cz'=16,'core'=2,'dp'=4] {'cz','dp'}, dimensions={0} | all-to-all | bytes 5242880 | tf_op jit(solution)/shard_map/all_to_all | solution.py:120
  193.3 1.9 reduce_sum.104
  195.6 32.9 %all_to_all.22 = f32[64,32,256]{2,1,0:T(8,128)} all-to-all(f32[64,32,256]{2,1,0:T(8,128)S(1)} %broadcast_in_dim.56), channel_id=1, replica_groups=mesh['cz'=16,'core'=2,'dp'=4] {'cz','dp'}, dimensions={0} | all-to-all | bytes 4194304 | tf_op jit(solution)/shard_map/all_to_all | solution.py:123
  228.4 3.2 %collective-permute-start.4 = (f32[2048,256]{1,0:T(8,128)}, f32[2048,256]{1,0:T(8,128)S(1)}, u32[]{:S(2)}, u32[]{:S(2)}) collective-permute-start(f32[2048,256]{1,0:T(8,128)} %bitcast.32), channel_id=1, source_target_pairs={{0,4},{4,0},{1,5},{5,1},{2,6},{6,2},{3,7},{7,3},{8,12},{12,8},{9,1... | collective-permute-start | bytes 6291464 | tf_op jit(solution)/shard_map/ppermute | solution.py:124
  231.7 3.7 %fusion.9 = bf16[128,32,128]{0,2,1:T(8,128)(2,1)} fusion(f32[128,32,128]{0,2,1:T(8,128)S(1)} %copy-done.8, f32[128,32]{0,1:T(8,128)S(1)} %copy.143, bf16[32,128,128]{2,1,0:T(8,128)(2,1)S(1)} %bitcast.149, f32[128,128]{0,1:T(8,128)S(1)} %copy-done.14, f32[32,128]{1,0:T(8,128)S(1)} %copy-done.12, f32[128,32]{0,1:T(8,128)S(1)} %copy.140, ...), kind=kOutput, calls=%fused_computation.20 | convolution fusion | flops 808976384 | bytes 4325376 | tf_op jit(solution)/shard_map/transpose(jvp(hts,shp->thp))/dot_general | solution.py:64
  235.3 2.3 copy.155
  240.0 2.3 pad_maximum_fusion
  (113 shorter events, 34.6 us)
Async XLA Ops:
  0.6 5.4 %copy-start = (bf16[4096,256]{1,0:T(8,128)(2,1)S(1)}, bf16[4096,256]{1,0:T(8,128)(2,1)}, u32[]{:S(2)}) copy-start(bf16[4096,256]{1,0:T(8,128)(2,1)} %param.9) | copy-start | bytes 6291460
  0.6 2.7 %copy-start.15 = (f32[1,128,32]{1,2,0:T(8,128)S(1)}, f32[1,128,32]{1,2,0:T(8,128)}, u32[]{:S(2)}) copy-start(f32[1,128,32]{1,2,0:T(8,128)} %param.11) | copy-start | bytes 49156
  0.7 2.8 %copy-start.21 = (f32[32]{0:T(128)S(1)}, f32[32]{0:T(128)}, u32[]{:S(2)}) copy-start(f32[32]{0:T(128)} %param.12) | copy-start | bytes 388
  9.0 2.9 %copy-start.4 = (f32[32,128,128]{2,1,0:T(8,128)}, f32[32,128,128]{2,1,0:T(8,128)S(1)}, u32[]{:S(2)}) copy-start(f32[32,128,128]{2,1,0:T(8,128)S(1)} %fusion) | copy-start | bytes 6291460
  9.4 2.5 %copy-start.19 = (f32[32]{0:T(128)S(1)}, f32[32]{0:T(128)}, u32[]{:S(2)}) copy-start(f32[32]{0:T(128)} %copy-done.18) | copy-start | bytes 388
  11.9 2.9 %copy-start.20 = (f32[32,1,1]{0,2,1:T(1,128)S(1)}, f32[32,1,1]{0,2,1:T(1,128)}, u32[]{:S(2)}) copy-start(f32[32,1,1]{0,2,1:T(1,128)} %get-tuple-element.48) | copy-start | bytes 388
  13.5 5.7 %collective-permute-start = (f32[32,136,128]{2,1,0:T(8,128)}, f32[32,136,128]{2,1,0:T(8,128)}, u32[]{:S(2)}, u32[]{:S(2)}) collective-permute-start(f32[32,136,128]{2,1,0:T(8,128)} %pad_maximum_fusion.2), channel_id=1, source_target_pairs={{0,4},{4,0},{1,5},{5,1},{2,6},{6,2},{3,7},{7,3},{8,12},{12,8},{9,1... | collective-permute-start | bytes 6684680 | tf_op jit(solution)/shard_map/ppermute | solution.py:21
  25.1 42.0 %all-to-all-start = ((f32[32,136,128]{2,1,0:T(8,128)}), f32[32,136,128]{2,1,0:T(8,128)}, u32[]{:S(2)}, u32[]{:S(2)}) async-start(f32[32,136,128]{2,1,0:T(8,128)} %pad_maximum_fusion.3), calls=%async_computation | async-start | bytes 4456448 | tf_op jit(solution)/shard_map/all_to_all | solution.py:29
  107.4 11.3 %collective-permute-start.1 = (f32[32,128,128]{2,1,0:T(8,128)}, f32[32,128,128]{2,1,0:T(8,128)}, u32[]{:S(2)}, u32[]{:S(2)}) collective-permute-start(f32[32,128,128]{2,1,0:T(8,128)} %all_to_all.20), channel_id=1, source_target_pairs={{0,4},{4,0},{1,5},{5,1},{2,6},{6,2},{3,7},{7,3},{8,12},{12,8},{9,1... | collective-permute-start | bytes 6291464 | tf_op jit(solution)/shard_map/ppermute | solution.py:41
  110.2 4.3 %copy-start.11 = (f32[32,128]{1,0:T(8,128)}, f32[32,128]{1,0:T(8,128)S(1)}, u32[]{:S(2)}) copy-start(f32[32,128]{1,0:T(8,128)S(1)} %reduce_window_sum.46) | copy-start | bytes 49156
  110.3 4.1 %copy-start.16 = (pred[128,128]{0,1:T(8,128)(4,1)}, pred[128,128]{0,1:T(8,128)(4,1)S(1)}, u32[]{:S(2)}) copy-start(pred[128,128]{0,1:T(8,128)(4,1)S(1)} %iota_compare_fusion) | copy-start | bytes 49156
  110.4 4.0 %copy-start.13 = (f32[128,128]{0,1:T(8,128)}, f32[128,128]{0,1:T(8,128)S(1)}, u32[]{:S(2)}) copy-start(f32[128,128]{0,1:T(8,128)S(1)} %fusion.77) | copy-start | bytes 196612
  122.7 3.3 %copy-start.3 = (f32[32,128,128]{2,1,0:T(8,128)}, f32[32,128,128]{2,1,0:T(8,128)S(1)}, u32[]{:S(2)}) copy-start(f32[32,128,128]{2,1,0:T(8,128)S(1)} %get-tuple-element.37) | copy-start | bytes 6291460
  122.7 3.3 %copy-start.5 = (f32[32,128,128]{2,1,0:T(8,128)}, f32[32,128,128]{2,1,0:T(8,128)S(1)}, u32[]{:S(2)}) copy-start(f32[32,128,128]{2,1,0:T(8,128)S(1)} %get-tuple-element.36) | copy-start | bytes 6291460
  135.2 5.3 %copy-start.6 = (f32[32,128,128]{2,1,0:T(8,128)S(1)}, f32[32,128,128]{2,1,0:T(8,128)}, u32[]{:S(2)}) copy-start(f32[32,128,128]{2,1,0:T(8,128)} %copy-done.5) | copy-start | bytes 6291460
  135.2 5.3 %copy-start.10 = (f32[128,128]{1,0:T(8,128)S(1)}, f32[128,128]{1,0:T(8,128)}, u32[]{:S(2)}) copy-start(f32[128,128]{1,0:T(8,128)} %fusion.82) | copy-start | bytes 196612
  140.6 3.6 %copy-start.7 = (bf16[1,128,4096]{2,1,0:T(8,128)(2,1)S(1)}, bf16[1,128,4096]{2,1,0:T(8,128)(2,1)}, u32[]{:S(2)}) copy-start(bf16[1,128,4096]{2,1,0:T(8,128)(2,1)} %param.8) | copy-start | bytes 3145732
  144.7 4.7 %collective-permute-start.2 = (f32[2048,256]{1,0:T(8,128)S(1)}, f32[2048,256]{1,0:T(8,128)}, u32[]{:S(2)}, u32[]{:S(2)}) collective-permute-start(f32[2048,256]{1,0:T(8,128)S(1)} %fusion.49), channel_id=1, source_target_pairs={{0,4},{4,0},{1,5},{5,1},{2,6},{6,2},{3,7},{7,3},{8,12},{12,8},{9,1... | collective-permute-start | bytes 6291464 | tf_op jit(solution)/shard_map/ppermute | solution.py:112
  146.5 2.7 %collective-permute-start.3 = (f32[8,256]{1,0:T(8,128)S(1)}, f32[8,256]{1,0:T(8,128)S(1)}, u32[]{:S(2)}, u32[]{:S(2)}) collective-permute-start(f32[8,256]{1,0:T(8,128)S(1)} %scatter.7), channel_id=1, source_target_pairs={{0,4},{4,0},{1,5},{5,1},{2,6},{6,2},{3,7},{7,3},{8,12},{12,8},{9,1... | collective-permute-start | bytes 24584 | tf_op jit(solution)/shard_map/ppermute | solution.py:113
  195.5 36.1 %copy-start.8 = (f32[128,32,128]{0,2,1:T(8,128)S(1)}, f32[128,32,128]{0,2,1:T(8,128)}, u32[]{:S(2)}) copy-start(f32[128,32,128]{0,2,1:T(8,128)} %get-tuple-element.55) | copy-start | bytes 6291460
  195.5 36.1 %copy-start.12 = (f32[32,128]{1,0:T(8,128)S(1)}, f32[32,128]{1,0:T(8,128)}, u32[]{:S(2)}) copy-start(f32[32,128]{1,0:T(8,128)} %copy-done.11) | copy-start | bytes 49156
  195.5 36.1 %copy-start.14 = (f32[128,128]{0,1:T(8,128)S(1)}, f32[128,128]{0,1:T(8,128)}, u32[]{:S(2)}) copy-start(f32[128,128]{0,1:T(8,128)} %copy-done.13) | copy-start | bytes 196612
  195.5 36.1 %copy-start.17 = (pred[128,128]{0,1:T(8,128)(4,1)S(1)}, pred[128,128]{0,1:T(8,128)(4,1)}, u32[]{:S(2)}) copy-start(pred[128,128]{0,1:T(8,128)(4,1)} %copy-done.16) | copy-start | bytes 49156
  228.4 9.7 %collective-permute-start.4 = (f32[2048,256]{1,0:T(8,128)}, f32[2048,256]{1,0:T(8,128)S(1)}, u32[]{:S(2)}, u32[]{:S(2)}) collective-permute-start(f32[2048,256]{1,0:T(8,128)} %bitcast.32), channel_id=1, source_target_pairs={{0,4},{4,0},{1,5},{5,1},{2,6},{6,2},{3,7},{7,3},{8,12},{12,8},{9,1... | collective-permute-start | bytes 6291464 | tf_op jit(solution)/shard_map/ppermute | solution.py:124
  (5 other events, 8.9 us)

commit v11 on v10

--- a/solution.py
+++ b/solution.py
@@ -111,21 +111,27 @@
     swap = [(0, 1), (1, 0)]
     paired = keep + lax.ppermute(give, "core", swap)
     rate_pair = rate_rows + lax.ppermute(rate_rows, "core", swap)
-    axes = ("cz", "dp")
-    total = lax.axis_size(axes)
-    chunk = half // total
-    parcel = jnp.concatenate(
-        [paired.reshape(total, chunk, cols), jnp.broadcast_to(rate_pair[None], (total, 8, cols))], axis=1
-    )
-    pieces = lax.all_to_all(parcel, axes, 0, 0, tiled=True)
-    mine_sum = jnp.sum(pieces, axis=0)
-    spread = jnp.broadcast_to(mine_sum[None, :chunk], (total, chunk, cols))
-    own_half = lax.all_to_all(spread, axes, 0, 0, tiled=True).reshape(half, cols)
+    level = []
+    block = paired
+    extra = rate_pair
+    for axis in ("dp", "cz"):
+        total = lax.axis_size(axis)
+        chunk = block.shape[0] // total
+        parcel = jnp.concatenate(
+            [block.reshape(total, chunk, cols), jnp.broadcast_to(extra[None], (total, 8, cols))], axis=1
+        )
+        summed = jnp.sum(lax.all_to_all(parcel, axis, 0, 0, tiled=True), axis=0)
+        level.append((axis, total, chunk))
+        block, extra = summed[:chunk], summed[chunk:]
+    d_alog = extra[0, :heads]
+    for axis, total, chunk in level[::-1]:
+        block = lax.all_to_all(jnp.broadcast_to(block[None], (total, chunk, cols)), axis, 0, 0, tiled=True)
+        block = block.reshape(total * chunk, cols)
+    own_half = block
     other_half = lax.ppermute(own_half, "core", swap)
     d_wbc = jnp.concatenate(
         [jnp.where(first, own_half, other_half), jnp.where(first, other_half, own_half)], axis=0
     )
-    d_alog = mine_sum[chunk, :heads]
     return (d_x[None], d_wbc, d_alog)
 
 

time: 243 us -> 253 us (1.041)
  blocking collectives: 105 us -> 113 us
    all_to_all x2 -> x4, blocking collectives: 74.1 us -> 82.3 us  [the longest x2 44.5 us: per_device(): summed = jnp.sum(lax.all_to_all(parcel, axis, 0, 0, tiled=True), axis=0)]
where the time goes in v11:
time: 253 us; the launch traced here: 252 us
  blocking collectives  113 us (45%)
  waiting for transfers between devices  40.7 us (16%)
  matrix products  37.3 us (15%)
  other arithmetic  23.1 us (9%)
  local copies, waits for them, and re-layouts  20.1 us (8%)
  starting transfers between devices  17 us (7%)
    all_to_all x2, blocking collectives, per_device(): summed = jnp.sum(lax.all_to_all(parcel, axis, 0, 0, tiled=True), axis=0)  44.5 us
    all_to_all x2, blocking collectives, per_device(): lax.all_to_all(jnp.broadcast_to(block[None], (total, chunk, cols)), axis,...  37.8 us
    all_to_all x1, waiting for transfers between devices, exchange(): lax.all_to_all(marked(combined, pair_log), 'cz', 0, 0, tiled=True)  34.3 us
    all_to_all x1, blocking collectives, exchange(): back = lax.all_to_all(res, 'cz', 0, 0, tiled=True)  30.4 us
    dot_general x2, matrix products, block_forward(): jnp.einsum('shp,sn->hpn', inputs * tail[:, :, None], b_in, precision=HIGH)  8.61 us
    all_to_all x1, starting transfers between devices, exchange(): lax.all_to_all(marked(combined, pair_log), 'cz', 0, 0, tiled=True)  7.75 us
    dot_general x2, matrix products, block_forward(): y_intra = jnp.einsum('hts,shp->thp', mixing, inputs, precision=HIGH)  7.66 us
    dot_general x2, matrix products, block_forward(): jnp.einsum('tn,hpn->thp', c_out, h_in, precision=HIGH)  5.29 us
  transfers between devices with their start and end apart: 6, of which 3 were waited for; matrix products, arithmetic and copies ran while one was open for 7% of the time, Pallas kernels for 0%

profile of v11, /device:TPU:1, one launch (start us, length us, event | category | flops | bytes accessed | tf_op | source)
XLA Modules:
  0.0 252.0 jit_solution(18257564906205464221)
XLA Ops:
  0.7 2.7 %copy.148 = f32[1,128,4096]{1,2,0:T(8,128)} copy(bf16[1,128,4096]{2,1,0:T(8,128)(2,1)} %param.10) | data formatting | bytes 3145728 | tf_op jit(solution)/shard_map/convert_element_type | solution.py:92
  9.4 2.4 broadcast_select_fusion.4
  14.9 4.2 %collective-permute-done = f32[32,136,128]{2,1,0:T(8,128)} collective-permute-done((f32[32,136,128]{2,1,0:T(8,128)}, f32[32,136,128]{2,1,0:T(8,128)}, u32[]{:S(2)}, u32[]{:S(2)}) %collective-permute-start) | collective-permute-done | bytes 2228256 | tf_op jit(solution)/shard_map/ppermute | solution.py:21
  20.9 2.6 %multiply_add_fusion.1 = f32[32,128,128]{2,1,0:T(8,128)S(1)} fusion(f32[32,128,128]{2,1,0:T(8,128)} %copy-done.4, f32[32,128,128]{2,1,0:T(8,128)} %get-tuple-element.56, f32[32,136,128]{2,1,0:T(8,128)} %collective-permute-done, f32[32]{0:T(128)S(1)} %fusion.106, pred[]{:T(512)S(6)} %eq.4), kind=kLoop, calls=%fused_computation.29 | loop fusion | flops 1572864 | bytes 8388737 | tf_op jit(solution)/shard_map/add | solution.py:26
  25.1 7.8 %all-to-all-start = ((f32[32,136,128]{2,1,0:T(8,128)}), f32[32,136,128]{2,1,0:T(8,128)}, u32[]{:S(2)}, u32[]{:S(2)}) async-start(f32[32,136,128]{2,1,0:T(8,128)} %pad_maximum_fusion.2), calls=%async_computation | async-start | bytes 4456448 | tf_op jit(solution)/shard_map/all_to_all | solution.py:29
  32.9 34.3 %all-to-all-done = f32[32,136,128]{2,1,0:T(8,128)} async-done(((f32[32,136,128]{2,1,0:T(8,128)}), f32[32,136,128]{2,1,0:T(8,128)}, u32[]{:S(2)}, u32[]{:S(2)}) %all-to-all-start) | async-done | bytes 2228256 | tf_op jit(solution)/shard_map/all_to_all | solution.py:29
  67.1 3.1 %slice.83 = f32[16,2,128,128]{3,2,1,0:T(8,128)} slice(f32[16,2,136,128]{3,2,1,0:T(8,128)} %bitcast.8), slice={[0:16], [0:2], [0:128], [0:128]} | slice | bytes 4194304 | tf_op jit(solution)/shard_map/slice | solution.py:30
  71.6 4.7 %fusion.19 = f32[16,2,128,128]{3,0,2,1:T(8,128)S(1)} fusion(f32[16,2,128,128]{3,2,1,0:T(8,128)} %slice.83, f32[16,2]{0,1:T(2,128)S(1)} %copy.160, f32[16,2]{0,1:T(2,128)S(1)} %copy.158, pred[16,16]{1,0:T(8,128)(4,1)S(1)} %get-tuple-element.59, pred[16,16]{1,0:T(8,128)(4,1)S(1)} %get-tuple-element.60, pred[]{:T(512)S(6)} %eq.4), kind=kOutput, calls=%fused_computation.35 | convolution fusion | flops 100665856 | bytes 4195073 | tf_op jit(solution)/shard_map/djh,jhpn->dhpn/dot_general | solution.py:39
  76.9 30.4 %all_to_all.30 = f32[32,128,128]{2,1,0:T(8,128)} all-to-all(f32[32,128,128]{2,1,0:T(8,128)S(1)} %bitcast.153), channel_id=1, replica_groups=mesh['cz'=16,'core'=2,'dp'=4] {'cz'}, dimensions={0} | all-to-all | bytes 4194304 | tf_op jit(solution)/shard_map/all_to_all | solution.py:40
  107.4 2.3 collective-permute-start.1
  110.4 4.0 %fusion.23 = (f32[32,128]{1,0:T(8,128)}, f32[32,128]{1,0:T(8,128)S(1)}, f32[128,128]{0,1:T(8,128)}) fusion(f32[128,128]{0,1:T(8,128)S(1)} %fusion.77, f32[32,128]{1,0:T(8,128)S(1)} %reduce_window_sum.46, pred[128,128]{0,1:T(8,128)(4,1)S(1)} %iota_compare_fusion, bf16[32,128,128]{2,1,0:T(8,128)(2,1)S(1)} %bitcast.148, f32[128,32,128]{0,2,1:T(8,128)S(1)} %bitcast.144, ...), kind=kOutput, calls=%fused_computation.37 | convolution fusion | flops 810524672 | bytes 3358720 | tf_op jit(solution)/shard_map/transpose(jvp(hts,shp->thp))/dot_general | solution.py:64
  118.7 4.0 %multiply_reduce_fusion = (f32[32]{0:T(128)}, f32[32,128,128]{2,1,0:T(8,128)S(1)}, f32[32,128,128]{2,1,0:T(8,128)S(1)}) fusion(f32[32,128,128]{2,1,0:T(8,128)} %collective-permute-done.1, f32[32,136,128]{2,1,0:T(8,128)} %collective-permute-done, f32[32,128,128]{2,1,0:T(8,128)} %all_to_all.30, f32[32]{0:T(128)} %get-tuple-element.33, pred[]{:T(512)S(6)} %eq.4), kind=kLoop, calls=%fused_computation.21 | loop fusion | flops 3145696 | bytes 10486017 | tf_op jit(solution)/shard_map/transpose(jvp())/reduce_sum | solution.py:68
  122.7 3.3 %multiply_reduce_fusion.1 = (f32[128,32]{0,1:T(8,128)}, f32[128,32,128]{0,2,1:T(8,128)}) fusion(f32[128,32,128]{0,2,1:T(8,128)S(1)} %bitcast.145, f32[128,32]{0,1:T(8,128)S(1)} %copy.170, f32[32,128,128]{2,1,0:T(8,128)S(1)} %get-tuple-element.40, bf16[128,256]{1,0:T(8,128)(2,1)S(1)} %convolution_convert_fusion), kind=kOutput, calls=%fused_computation.22 | convolution fusion | flops 806875136 | bytes 6356992 | tf_op jit(solution)/shard_map/transpose(jvp(shp,sn->hpn))/dot_general | solution.py:67
  135.2 5.3 %fusion.33 = bf16[128,128]{1,0:T(8,128)(2,1)S(1)} fusion(f32[128,128]{1,0:T(8,128)S(1)} %fusion.75, f32[32,128,128]{2,1,0:T(8,128)} %copy-done.3, f32[128,32,128]{0,2,1:T(8,128)S(1)} %bitcast.146, f32[128,32]{0,1:T(8,128)S(1)} %copy.170, f32[128,32]{0,1:T(8,128)S(1)} %copy.167), kind=kOutput, calls=%fused_computation.44 | convolution fusion | flops 806387712 | bytes 4325376 | tf_op jit(solution)/shard_map/transpose(jvp(shp,sn->hpn))/dot_general | solution.py:67
  140.6 3.6 %fusion.32 = bf16[128,128]{1,0:T(8,128)(2,1)S(1)} fusion(f32[128,128]{1,0:T(8,128)S(1)} %copy-done.10, f32[32,128,128]{2,1,0:T(8,128)S(1)} %copy-done.6, bf16[128,32,128]{0,2,1:T(8,128)(2,1)S(1)} %bitcast.150, f32[128,32]{0,1:T(8,128)S(1)} %copy.172), kind=kOutput, calls=%fused_computation.43 | convolution fusion | flops 806387712 | bytes 3260416 | tf_op jit(solution)/shard_map/transpose(jvp(tn,hpn->thp))/dot_general | solution.py:70
  149.4 2.4 convolution_add_fusion
  152.0 30.4 %all_to_all.31 = f32[4,520,256]{2,1,0:T(8,128)} all-to-all(f32[4,520,256]{2,1,0:T(8,128)S(1)} %pad_maximum_fusion.3), channel_id=1, replica_groups=mesh['cz'=16,'core'=2,'dp'=4] {'dp'}, dimensions={0} | all-to-all | bytes 4259840 | tf_op jit(solution)/shard_map/all_to_all | solution.py:123
  184.4 14.1 %all_to_all.32 = f32[16,40,256]{2,1,0:T(8,128)S(1)} all-to-all(f32[16,40,256]{2,1,0:T(8,128)S(1)} %pad_maximum_fusion.4), channel_id=1, replica_groups=mesh['cz'=16,'core'=2,'dp'=4] {'cz'}, dimensions={0} | all-to-all | bytes 1310720 | tf_op jit(solution)/shard_map/all_to_all | solution.py:123
  198.6 11.9 %all_to_all.33 = f32[16,32,256]{2,1,0:T(8,128)S(1)} all-to-all(f32[16,32,256]{2,1,0:T(8,128)S(1)} %broadcast_in_dim.63), channel_id=1, replica_groups=mesh['cz'=16,'core'=2,'dp'=4] {'cz'}, dimensions={0} | all-to-all | bytes 1048576 | tf_op jit(solution)/shard_map/all_to_all | solution.py:128
  210.6 26.0 %all_to_all.34 = f32[4,512,256]{2,1,0:T(8,128)} all-to-all(f32[4,512,256]{2,1,0:T(8,128)S(1)} %broadcast_in_dim.65), channel_id=1, replica_groups=mesh['cz'=16,'core'=2,'dp'=4] {'dp'}, dimensions={0} | all-to-all | bytes 4194304 | tf_op jit(solution)/shard_map/all_to_all | solution.py:128
  236.6 4.7 %collective-permute-start.4 = (f32[2048,256]{1,0:T(8,128)}, f32[2048,256]{1,0:T(8,128)S(1)}, u32[]{:S(2)}, u32[]{:S(2)}) collective-permute-start(f32[2048,256]{1,0:T(8,128)} %bitcast.34), channel_id=1, source_target_pairs={{0,4},{4,0},{1,5},{5,1},{2,6},{6,2},{3,7},{7,3},{8,12},{12,8},{9,1... | collective-permute-start | bytes 6291464 | tf_op jit(solution)/shard_map/ppermute | solution.py:131
  241.3 3.7 %fusion.9 = bf16[128,32,128]{0,2,1:T(8,128)(2,1)} fusion(f32[128,32,128]{0,2,1:T(8,128)S(1)} %copy-done.8, f32[128,32]{0,1:T(8,128)S(1)} %copy.170, bf16[32,128,128]{2,1,0:T(8,128)(2,1)S(1)} %bitcast.151, f32[128,128]{0,1:T(8,128)S(1)} %copy-done.14, f32[32,128]{1,0:T(8,128)S(1)} %copy-done.12, f32[128,32]{0,1:T(8,128)S(1)} %copy.167, ...), kind=kOutput, calls=%fused_computation.20 | convolution fusion | flops 808976384 | bytes 4325376 | tf_op jit(solution)/shard_map/transpose(jvp(hts,shp->thp))/dot_general | solution.py:64
  245.0 2.3 copy.182
  249.6 2.3 pad_maximum_fusion
  (121 shorter events, 38.6 us)
Async XLA Ops:
  0.6 5.4 %copy-start = (bf16[4096,256]{1,0:T(8,128)(2,1)S(1)}, bf16[4096,256]{1,0:T(8,128)(2,1)}, u32[]{:S(2)}) copy-start(bf16[4096,256]{1,0:T(8,128)(2,1)} %param.9) | copy-start | bytes 6291460
  0.6 2.7 %copy-start.15 = (f32[1,128,32]{1,2,0:T(8,128)S(1)}, f32[1,128,32]{1,2,0:T(8,128)}, u32[]{:S(2)}) copy-start(f32[1,128,32]{1,2,0:T(8,128)} %param.11) | copy-start | bytes 49156
  0.7 2.8 %copy-start.21 = (f32[32]{0:T(128)S(1)}, f32[32]{0:T(128)}, u32[]{:S(2)}) copy-start(f32[32]{0:T(128)} %param.12) | copy-start | bytes 388
  9.0 2.9 %copy-start.4 = (f32[32,128,128]{2,1,0:T(8,128)}, f32[32,128,128]{2,1,0:T(8,128)S(1)}, u32[]{:S(2)}) copy-start(f32[32,128,128]{2,1,0:T(8,128)S(1)} %fusion) | copy-start | bytes 6291460
  9.4 2.5 copy-start.19
  11.9 2.9 %copy-start.20 = (f32[32,1,1]{0,2,1:T(1,128)S(1)}, f32[32,1,1]{0,2,1:T(1,128)}, u32[]{:S(2)}) copy-start(f32[32,1,1]{0,2,1:T(1,128)} %get-tuple-element.51) | copy-start | bytes 388
  13.5 5.7 %collective-permute-start = (f32[32,136,128]{2,1,0:T(8,128)}, f32[32,136,128]{2,1,0:T(8,128)}, u32[]{:S(2)}, u32[]{:S(2)}) collective-permute-start(f32[32,136,128]{2,1,0:T(8,128)} %pad_maximum_fusion.1), channel_id=1, source_target_pairs={{0,4},{4,0},{1,5},{5,1},{2,6},{6,2},{3,7},{7,3},{8,12},{12,8},{9,1... | collective-permute-start | bytes 6684680 | tf_op jit(solution)/shard_map/ppermute | solution.py:21
  25.1 42.0 %all-to-all-start = ((f32[32,136,128]{2,1,0:T(8,128)}), f32[32,136,128]{2,1,0:T(8,128)}, u32[]{:S(2)}, u32[]{:S(2)}) async-start(f32[32,136,128]{2,1,0:T(8,128)} %pad_maximum_fusion.2), calls=%async_computation | async-start | bytes 4456448 | tf_op jit(solution)/shard_map/all_to_all | solution.py:29
  107.4 11.3 %collective-permute-start.1 = (f32[32,128,128]{2,1,0:T(8,128)}, f32[32,128,128]{2,1,0:T(8,128)}, u32[]{:S(2)}, u32[]{:S(2)}) collective-permute-start(f32[32,128,128]{2,1,0:T(8,128)} %all_to_all.30), channel_id=1, source_target_pairs={{0,4},{4,0},{1,5},{5,1},{2,6},{6,2},{3,7},{7,3},{8,12},{12,8},{9,1... | collective-permute-start | bytes 6291464 | tf_op jit(solution)/shard_map/ppermute | solution.py:41
  110.2 4.3 %copy-start.11 = (f32[32,128]{1,0:T(8,128)}, f32[32,128]{1,0:T(8,128)S(1)}, u32[]{:S(2)}) copy-start(f32[32,128]{1,0:T(8,128)S(1)} %reduce_window_sum.46) | copy-start | bytes 49156
  110.3 4.1 %copy-start.16 = (pred[128,128]{0,1:T(8,128)(4,1)}, pred[128,128]{0,1:T(8,128)(4,1)S(1)}, u32[]{:S(2)}) copy-start(pred[128,128]{0,1:T(8,128)(4,1)S(1)} %iota_compare_fusion) | copy-start | bytes 49156
  110.4 4.0 %copy-start.13 = (f32[128,128]{0,1:T(8,128)}, f32[128,128]{0,1:T(8,128)S(1)}, u32[]{:S(2)}) copy-start(f32[128,128]{0,1:T(8,128)S(1)} %fusion.77) | copy-start | bytes 196612
  122.7 3.3 %copy-start.3 = (f32[32,128,128]{2,1,0:T(8,128)}, f32[32,128,128]{2,1,0:T(8,128)S(1)}, u32[]{:S(2)}) copy-start(f32[32,128,128]{2,1,0:T(8,128)S(1)} %get-tuple-element.40) | copy-start | bytes 6291460
  122.7 3.3 %copy-start.5 = (f32[32,128,128]{2,1,0:T(8,128)}, f32[32,128,128]{2,1,0:T(8,128)S(1)}, u32[]{:S(2)}) copy-start(f32[32,128,128]{2,1,0:T(8,128)S(1)} %get-tuple-element.39) | copy-start | bytes 6291460
  135.2 5.3 %copy-start.6 = (f32[32,128,128]{2,1,0:T(8,128)S(1)}, f32[32,128,128]{2,1,0:T(8,128)}, u32[]{:S(2)}) copy-start(f32[32,128,128]{2,1,0:T(8,128)} %copy-done.5) | copy-start | bytes 6291460
  135.2 5.3 %copy-start.10 = (f32[128,128]{1,0:T(8,128)S(1)}, f32[128,128]{1,0:T(8,128)}, u32[]{:S(2)}) copy-start(f32[128,128]{1,0:T(8,128)} %fusion.82) | copy-start | bytes 196612
  140.6 3.6 %copy-start.7 = (bf16[1,128,4096]{2,1,0:T(8,128)(2,1)S(1)}, bf16[1,128,4096]{2,1,0:T(8,128)(2,1)}, u32[]{:S(2)}) copy-start(bf16[1,128,4096]{2,1,0:T(8,128)(2,1)} %param.8) | copy-start | bytes 3145732
  144.7 4.7 %collective-permute-start.2 = (f32[2048,256]{1,0:T(8,128)S(1)}, f32[2048,256]{1,0:T(8,128)}, u32[]{:S(2)}, u32[]{:S(2)}) collective-permute-start(f32[2048,256]{1,0:T(8,128)S(1)} %fusion.49), channel_id=1, source_target_pairs={{0,4},{4,0},{1,5},{5,1},{2,6},{6,2},{3,7},{7,3},{8,12},{12,8},{9,1... | collective-permute-start | bytes 6291464 | tf_op jit(solution)/shard_map/ppermute | solution.py:112
  146.5 2.7 %collective-permute-start.3 = (f32[8,256]{1,0:T(8,128)S(1)}, f32[8,256]{1,0:T(8,128)S(1)}, u32[]{:S(2)}, u32[]{:S(2)}) collective-permute-start(f32[8,256]{1,0:T(8,128)S(1)} %scatter.7), channel_id=1, source_target_pairs={{0,4},{4,0},{1,5},{5,1},{2,6},{6,2},{3,7},{7,3},{8,12},{12,8},{9,1... | collective-permute-start | bytes 24584 | tf_op jit(solution)/shard_map/ppermute | solution.py:113
  210.6 30.7 %copy-start.8 = (f32[128,32,128]{0,2,1:T(8,128)S(1)}, f32[128,32,128]{0,2,1:T(8,128)}, u32[]{:S(2)}) copy-start(f32[128,32,128]{0,2,1:T(8,128)} %get-tuple-element.58) | copy-start | bytes 6291460
  210.6 30.7 %copy-start.12 = (f32[32,128]{1,0:T(8,128)S(1)}, f32[32,128]{1,0:T(8,128)}, u32[]{:S(2)}) copy-start(f32[32,128]{1,0:T(8,128)} %copy-done.11) | copy-start | bytes 49156
  210.6 30.7 %copy-start.14 = (f32[128,128]{0,1:T(8,128)S(1)}, f32[128,128]{0,1:T(8,128)}, u32[]{:S(2)}) copy-start(f32[128,128]{0,1:T(8,128)} %copy-done.13) | copy-start | bytes 196612
  210.6 30.7 %copy-start.17 = (pred[128,128]{0,1:T(8,128)(4,1)S(1)}, pred[128,128]{0,1:T(8,128)(4,1)}, u32[]{:S(2)}) copy-start(pred[128,128]{0,1:T(8,128)(4,1)} %copy-done.16) | copy-start | bytes 49156
  236.6 11.1 %collective-permute-start.4 = (f32[2048,256]{1,0:T(8,128)}, f32[2048,256]{1,0:T(8,128)S(1)}, u32[]{:S(2)}, u32[]{:S(2)}) collective-permute-start(f32[2048,256]{1,0:T(8,128)} %bitcast.34), channel_id=1, source_target_pairs={{0,4},{4,0},{1,5},{5,1},{2,6},{6,2},{3,7},{7,3},{8,12},{12,8},{9,1... | collective-permute-start | bytes 6291464 | tf_op jit(solution)/shard_map/ppermute | solution.py:131
  (5 other events, 8.9 us)

commit v12 on v10

--- a/solution.py
+++ b/solution.py
@@ -7,7 +7,7 @@
 CHAIN = ("cz", "core")
 
 
-HIGH = lax.Precision.HIGHEST
+HIGH = lax.Precision.HIGH
 
 
 def exchange(log_total, own_state, back_term):

time: 243 us -> 236 us (0.971)
  matrix products: 37.3 us -> 29.8 us
where the time goes in v12:
time: 236 us; the launch traced here: 235 us
  blocking collectives  105 us (44%)
  waiting for transfers between devices  40.7 us (17%)
  matrix products  29.8 us (13%)
  other arithmetic  23.2 us (10%)
  local copies, waits for them, and re-layouts  20.8 us (9%)
  starting transfers between devices  15.1 us (6%)
    all_to_all x1, blocking collectives, per_device(): pieces = lax.all_to_all(parcel, axes, 0, 0, tiled=True)  41.2 us
    all_to_all x1, waiting for transfers between devices, exchange(): lax.all_to_all(marked(combined, pair_log), 'cz', 0, 0, tiled=True)  34.3 us
    all_to_all x1, blocking collectives, per_device(): lax.all_to_all(spread, axes, 0, 0, tiled=True).reshape(half, cols)  32.9 us
    all_to_all x1, blocking collectives, exchange(): back = lax.all_to_all(res, 'cz', 0, 0, tiled=True)  30.4 us
    all_to_all x1, starting transfers between devices, exchange(): lax.all_to_all(marked(combined, pair_log), 'cz', 0, 0, tiled=True)  7.75 us
    dot_general x2, matrix products, block_forward(): jnp.einsum('shp,sn->hpn', inputs * tail[:, :, None], b_in, precision=HIGH)  6.76 us
    dot_general x2, matrix products, block_forward(): y_intra = jnp.einsum('hts,shp->thp', mixing, inputs, precision=HIGH)  6.01 us
    unnamed x50, local copies, waits for them, and re-layouts  5.37 us
  transfers between devices with their start and end apart: 6, of which 3 were waited for; matrix products, arithmetic and copies ran while one was open for 7% of the time, Pallas kernels for 0%

profile of v12, /device:TPU:1, one launch (start us, length us, event | category | flops | bytes accessed | tf_op | source)
XLA Modules:
  0.0 235.1 jit_solution(1682395082517661288)
XLA Ops:
  0.7 2.7 %copy.121 = f32[1,128,4096]{1,2,0:T(8,128)} copy(bf16[1,128,4096]{2,1,0:T(8,128)(2,1)} %param.10) | data formatting | bytes 3145728 | tf_op jit(solution)/shard_map/convert_element_type | solution.py:92
  9.4 2.0 broadcast_select_fusion.4
  14.5 4.2 %collective-permute-done = f32[32,136,128]{2,1,0:T(8,128)} collective-permute-done((f32[32,136,128]{2,1,0:T(8,128)}, f32[32,136,128]{2,1,0:T(8,128)}, u32[]{:S(2)}, u32[]{:S(2)}) %collective-permute-start) | collective-permute-done | bytes 2228256 | tf_op jit(solution)/shard_map/ppermute | solution.py:21
  20.5 2.6 %multiply_add_fusion.1 = f32[32,128,128]{2,1,0:T(8,128)S(1)} fusion(f32[32,128,128]{2,1,0:T(8,128)} %copy-done.4, f32[32,128,128]{2,1,0:T(8,128)} %get-tuple-element.53, f32[32,136,128]{2,1,0:T(8,128)} %collective-permute-done, f32[32]{0:T(128)S(1)} %fusion.106, pred[]{:T(512)S(6)} %eq.4), kind=kLoop, calls=%fused_computation.29 | loop fusion | flops 1572864 | bytes 8388737 | tf_op jit(solution)/shard_map/add | solution.py:26
  24.7 7.8 %all-to-all-start = ((f32[32,136,128]{2,1,0:T(8,128)}), f32[32,136,128]{2,1,0:T(8,128)}, u32[]{:S(2)}, u32[]{:S(2)}) async-start(f32[32,136,128]{2,1,0:T(8,128)} %pad_maximum_fusion.3), calls=%async_computation | async-start | bytes 4456448 | tf_op jit(solution)/shard_map/all_to_all | solution.py:29
  32.4 34.3 %all-to-all-done = f32[32,136,128]{2,1,0:T(8,128)} async-done(((f32[32,136,128]{2,1,0:T(8,128)}), f32[32,136,128]{2,1,0:T(8,128)}, u32[]{:S(2)}, u32[]{:S(2)}) %all-to-all-start) | async-done | bytes 2228256 | tf_op jit(solution)/shard_map/all_to_all | solution.py:29
  66.7 3.1 %slice.73 = f32[16,2,128,128]{3,2,1,0:T(8,128)} slice(f32[16,2,136,128]{3,2,1,0:T(8,128)} %bitcast.8), slice={[0:16], [0:2], [0:128], [0:128]} | slice | bytes 4194304 | tf_op jit(solution)/shard_map/slice | solution.py:30
  71.1 3.5 %fusion.19 = f32[16,2,128,128]{3,0,2,1:T(8,128)S(1)} fusion(f32[16,2,128,128]{3,2,1,0:T(8,128)} %slice.73, f32[16,2]{0,1:T(2,128)S(1)} %copy.133, f32[16,2]{0,1:T(2,128)S(1)} %copy.131, pred[16,16]{1,0:T(8,128)(4,1)S(1)} %get-tuple-element.56, pred[16,16]{1,0:T(8,128)(4,1)S(1)} %get-tuple-element.57, pred[]{:T(512)S(6)} %eq.4), kind=kOutput, calls=%fused_computation.35 | convolution fusion | flops 50334208 | bytes 4195073 | tf_op jit(solution)/shard_map/djh,jhpn->dhpn/dot_general | solution.py:39
  75.4 30.4 %all_to_all.20 = f32[32,128,128]{2,1,0:T(8,128)} all-to-all(f32[32,128,128]{2,1,0:T(8,128)S(1)} %bitcast.151), channel_id=1, replica_groups=mesh['cz'=16,'core'=2,'dp'=4] {'cz'}, dimensions={0} | all-to-all | bytes 4194304 | tf_op jit(solution)/shard_map/all_to_all | solution.py:40
  105.8 2.3 collective-permute-start.1
  108.9 3.3 %fusion.23 = (f32[32,128]{1,0:T(8,128)}, f32[32,128]{1,0:T(8,128)S(1)}, f32[128,128]{0,1:T(8,128)}) fusion(f32[128,128]{0,1:T(8,128)S(1)} %fusion.77, f32[32,128]{1,0:T(8,128)S(1)} %reduce_window_sum.46, pred[128,128]{0,1:T(8,128)(4,1)S(1)} %iota_compare_fusion, bf16[32,128,128]{2,1,0:T(8,128)(2,1)S(1)} %bitcast.146, f32[128,32,128]{0,2,1:T(8,128)S(1)} %bitcast.142, ...), kind=kOutput, calls=%fused_computation.37 | convolution fusion | flops 407871488 | bytes 3358720 | tf_op jit(solution)/shard_map/transpose(jvp(hts,shp->thp))/dot_general | solution.py:64
  116.3 4.0 %multiply_reduce_fusion = (f32[32]{0:T(128)}, f32[32,128,128]{2,1,0:T(8,128)S(1)}, f32[32,128,128]{2,1,0:T(8,128)S(1)}) fusion(f32[32,128,128]{2,1,0:T(8,128)} %collective-permute-done.1, f32[32,136,128]{2,1,0:T(8,128)} %collective-permute-done, f32[32,128,128]{2,1,0:T(8,128)} %all_to_all.20, f32[32]{0:T(128)} %get-tuple-element.30, pred[]{:T(512)S(6)} %eq.4), kind=kLoop, calls=%fused_computation.21 | loop fusion | flops 3145696 | bytes 10486017 | tf_op jit(solution)/shard_map/transpose(jvp())/reduce_sum | solution.py:68
  120.3 3.2 %multiply_reduce_fusion.1 = (f32[128,32]{0,1:T(8,128)}, f32[128,32,128]{0,2,1:T(8,128)}) fusion(f32[128,32,128]{0,2,1:T(8,128)S(1)} %bitcast.143, f32[128,32]{0,1:T(8,128)S(1)} %copy.143, f32[32,128,128]{2,1,0:T(8,128)S(1)} %get-tuple-element.37, bf16[128,256]{1,0:T(8,128)(2,1)S(1)} %convolution_convert_fusion), kind=kOutput, calls=%fused_computation.22 | convolution fusion | flops 404221952 | bytes 6356992 | tf_op jit(solution)/shard_map/transpose(jvp(shp,sn->hpn))/dot_general | solution.py:67
  132.5 3.6 %fusion.33 = bf16[128,128]{1,0:T(8,128)(2,1)S(1)} fusion(f32[128,128]{1,0:T(8,128)S(1)} %fusion.75, f32[32,128,128]{2,1,0:T(8,128)} %copy-done.3, f32[128,32,128]{0,2,1:T(8,128)S(1)} %bitcast.144, f32[128,32]{0,1:T(8,128)S(1)} %copy.143, f32[128,32]{0,1:T(8,128)S(1)} %copy.140), kind=kOutput, calls=%fused_computation.44 | convolution fusion | flops 403734528 | bytes 4325376 | tf_op jit(solution)/shard_map/transpose(jvp(shp,sn->hpn))/dot_general | solution.py:67
  136.1 1.9 fusion.32
  140.7 2.2 collective-permute-done.3
  143.1 2.4 %convolution_add_fusion = f32[2048,256]{1,0:T(8,128)S(1)} fusion(f32[2048,256]{1,0:T(8,128)} %collective-permute-done.2, pred[]{:T(512)S(6)} %eq.4, bf16[128,4096]{1,0:T(8,128)(2,1)} %bitcast.152, bf16[128,128]{1,0:T(8,128)(2,1)S(1)} %fusion.33, bf16[128,128]{1,0:T(8,128)(2,1)S(1)} %fusion.32), kind=kOutput, calls=%fused_computation.4 | convolution fusion | flops 135135232 | bytes 5308417 | tf_op jit(solution)/shard_map/dot_general | solution.py:108
  145.8 41.2 %all_to_all.21 = f32[64,40,256]{2,1,0:T(8,128)} all-to-all(f32[64,40,256]{2,1,0:T(8,128)S(1)} %pad_maximum_fusion.1), channel_id=1, replica_groups=mesh['cz'=16,'core'=2,'dp'=4] {'cz','dp'}, dimensions={0} | all-to-all | bytes 5242880 | tf_op jit(solution)/shard_map/all_to_all | solution.py:120
  187.0 1.9 reduce_sum.104
  189.2 32.9 %all_to_all.22 = f32[64,32,256]{2,1,0:T(8,128)} all-to-all(f32[64,32,256]{2,1,0:T(8,128)S(1)} %broadcast_in_dim.56), channel_id=1, replica_groups=mesh['cz'=16,'core'=2,'dp'=4] {'cz','dp'}, dimensions={0} | all-to-all | bytes 4194304 | tf_op jit(solution)/shard_map/all_to_all | solution.py:123
  222.1 3.2 %collective-permute-start.4 = (f32[2048,256]{1,0:T(8,128)}, f32[2048,256]{1,0:T(8,128)S(1)}, u32[]{:S(2)}, u32[]{:S(2)}) collective-permute-start(f32[2048,256]{1,0:T(8,128)} %bitcast.32), channel_id=1, source_target_pairs={{0,4},{4,0},{1,5},{5,1},{2,6},{6,2},{3,7},{7,3},{8,12},{12,8},{9,1... | collective-permute-start | bytes 6291464 | tf_op jit(solution)/shard_map/ppermute | solution.py:124
  225.3 2.7 %fusion.9 = bf16[128,32,128]{0,2,1:T(8,128)(2,1)} fusion(f32[128,32,128]{0,2,1:T(8,128)S(1)} %copy-done.8, f32[128,32]{0,1:T(8,128)S(1)} %copy.143, bf16[32,128,128]{2,1,0:T(8,128)(2,1)S(1)} %bitcast.149, f32[128,128]{0,1:T(8,128)S(1)} %copy-done.14, f32[32,128]{1,0:T(8,128)S(1)} %copy-done.12, f32[128,32]{0,1:T(8,128)S(1)} %copy.140, ...), kind=kOutput, calls=%fused_computation.20 | convolution fusion | flops 406323200 | bytes 4325376 | tf_op jit(solution)/shard_map/transpose(jvp(hts,shp->thp))/dot_general | solution.py:64
  228.1 2.3 copy.155
  232.7 2.3 pad_maximum_fusion
  (113 shorter events, 34.1 us)
Async XLA Ops:
  0.6 5.4 %copy-start = (bf16[4096,256]{1,0:T(8,128)(2,1)S(1)}, bf16[4096,256]{1,0:T(8,128)(2,1)}, u32[]{:S(2)}) copy-start(bf16[4096,256]{1,0:T(8,128)(2,1)} %param.9) | copy-start | bytes 6291460
  0.6 2.7 %copy-start.15 = (f32[1,128,32]{1,2,0:T(8,128)S(1)}, f32[1,128,32]{1,2,0:T(8,128)}, u32[]{:S(2)}) copy-start(f32[1,128,32]{1,2,0:T(8,128)} %param.11) | copy-start | bytes 49156
  0.7 2.8 %copy-start.21 = (f32[32]{0:T(128)S(1)}, f32[32]{0:T(128)}, u32[]{:S(2)}) copy-start(f32[32]{0:T(128)} %param.12) | copy-start | bytes 388
  8.5 2.9 %copy-start.4 = (f32[32,128,128]{2,1,0:T(8,128)}, f32[32,128,128]{2,1,0:T(8,128)S(1)}, u32[]{:S(2)}) copy-start(f32[32,128,128]{2,1,0:T(8,128)S(1)} %fusion) | copy-start | bytes 6291460
  11.5 2.9 %copy-start.20 = (f32[32,1,1]{0,2,1:T(1,128)S(1)}, f32[32,1,1]{0,2,1:T(1,128)}, u32[]{:S(2)}) copy-start(f32[32,1,1]{0,2,1:T(1,128)} %get-tuple-element.48) | copy-start | bytes 388
  13.0 5.7 %collective-permute-start = (f32[32,136,128]{2,1,0:T(8,128)}, f32[32,136,128]{2,1,0:T(8,128)}, u32[]{:S(2)}, u32[]{:S(2)}) collective-permute-start(f32[32,136,128]{2,1,0:T(8,128)} %pad_maximum_fusion.2), channel_id=1, source_target_pairs={{0,4},{4,0},{1,5},{5,1},{2,6},{6,2},{3,7},{7,3},{8,12},{12,8},{9,1... | collective-permute-start | bytes 6684680 | tf_op jit(solution)/shard_map/ppermute | solution.py:21
  24.7 42.0 %all-to-all-start = ((f32[32,136,128]{2,1,0:T(8,128)}), f32[32,136,128]{2,1,0:T(8,128)}, u32[]{:S(2)}, u32[]{:S(2)}) async-start(f32[32,136,128]{2,1,0:T(8,128)} %pad_maximum_fusion.3), calls=%async_computation | async-start | bytes 4456448 | tf_op jit(solution)/shard_map/all_to_all | solution.py:29
  105.8 10.5 %collective-permute-start.1 = (f32[32,128,128]{2,1,0:T(8,128)}, f32[32,128,128]{2,1,0:T(8,128)}, u32[]{:S(2)}, u32[]{:S(2)}) collective-permute-start(f32[32,128,128]{2,1,0:T(8,128)} %all_to_all.20), channel_id=1, source_target_pairs={{0,4},{4,0},{1,5},{5,1},{2,6},{6,2},{3,7},{7,3},{8,12},{12,8},{9,1... | collective-permute-start | bytes 6291464 | tf_op jit(solution)/shard_map/ppermute | solution.py:41
  108.6 3.5 %copy-start.11 = (f32[32,128]{1,0:T(8,128)}, f32[32,128]{1,0:T(8,128)S(1)}, u32[]{:S(2)}) copy-start(f32[32,128]{1,0:T(8,128)S(1)} %reduce_window_sum.46) | copy-start | bytes 49156
  108.7 3.4 %copy-start.16 = (pred[128,128]{0,1:T(8,128)(4,1)}, pred[128,128]{0,1:T(8,128)(4,1)S(1)}, u32[]{:S(2)}) copy-start(pred[128,128]{0,1:T(8,128)(4,1)S(1)} %iota_compare_fusion) | copy-start | bytes 49156
  108.9 3.3 %copy-start.13 = (f32[128,128]{0,1:T(8,128)}, f32[128,128]{0,1:T(8,128)S(1)}, u32[]{:S(2)}) copy-start(f32[128,128]{0,1:T(8,128)S(1)} %fusion.77) | copy-start | bytes 196612
  120.3 3.2 %copy-start.3 = (f32[32,128,128]{2,1,0:T(8,128)}, f32[32,128,128]{2,1,0:T(8,128)S(1)}, u32[]{:S(2)}) copy-start(f32[32,128,128]{2,1,0:T(8,128)S(1)} %get-tuple-element.37) | copy-start | bytes 6291460
  120.3 3.2 %copy-start.5 = (f32[32,128,128]{2,1,0:T(8,128)}, f32[32,128,128]{2,1,0:T(8,128)S(1)}, u32[]{:S(2)}) copy-start(f32[32,128,128]{2,1,0:T(8,128)S(1)} %get-tuple-element.36) | copy-start | bytes 6291460
  132.5 3.6 %copy-start.6 = (f32[32,128,128]{2,1,0:T(8,128)S(1)}, f32[32,128,128]{2,1,0:T(8,128)}, u32[]{:S(2)}) copy-start(f32[32,128,128]{2,1,0:T(8,128)} %copy-done.5) | copy-start | bytes 6291460
  132.5 3.6 %copy-start.10 = (f32[128,128]{1,0:T(8,128)S(1)}, f32[128,128]{1,0:T(8,128)}, u32[]{:S(2)}) copy-start(f32[128,128]{1,0:T(8,128)} %fusion.82) | copy-start | bytes 196612
  138.0 2.3 copy-start.22
  138.6 4.5 %collective-permute-start.2 = (f32[2048,256]{1,0:T(8,128)S(1)}, f32[2048,256]{1,0:T(8,128)}, u32[]{:S(2)}, u32[]{:S(2)}) collective-permute-start(f32[2048,256]{1,0:T(8,128)S(1)} %fusion.49), channel_id=1, source_target_pairs={{0,4},{4,0},{1,5},{5,1},{2,6},{6,2},{3,7},{7,3},{8,12},{12,8},{9,1... | collective-permute-start | bytes 6291464 | tf_op jit(solution)/shard_map/ppermute | solution.py:112
  140.4 2.5 %collective-permute-start.3 = (f32[8,256]{1,0:T(8,128)S(1)}, f32[8,256]{1,0:T(8,128)S(1)}, u32[]{:S(2)}, u32[]{:S(2)}) collective-permute-start(f32[8,256]{1,0:T(8,128)S(1)} %scatter.7), channel_id=1, source_target_pairs={{0,4},{4,0},{1,5},{5,1},{2,6},{6,2},{3,7},{7,3},{8,12},{12,8},{9,1... | collective-permute-start | bytes 24584 | tf_op jit(solution)/shard_map/ppermute | solution.py:113
  189.2 36.1 %copy-start.8 = (f32[128,32,128]{0,2,1:T(8,128)S(1)}, f32[128,32,128]{0,2,1:T(8,128)}, u32[]{:S(2)}) copy-start(f32[128,32,128]{0,2,1:T(8,128)} %get-tuple-element.55) | copy-start | bytes 6291460
  189.2 36.1 %copy-start.12 = (f32[32,128]{1,0:T(8,128)S(1)}, f32[32,128]{1,0:T(8,128)}, u32[]{:S(2)}) copy-start(f32[32,128]{1,0:T(8,128)} %copy-done.11) | copy-start | bytes 49156
  189.2 36.1 %copy-start.14 = (f32[128,128]{0,1:T(8,128)S(1)}, f32[128,128]{0,1:T(8,128)}, u32[]{:S(2)}) copy-start(f32[128,128]{0,1:T(8,128)} %copy-done.13) | copy-start | bytes 196612
  189.2 36.1 %copy-start.17 = (pred[128,128]{0,1:T(8,128)(4,1)S(1)}, pred[128,128]{0,1:T(8,128)(4,1)}, u32[]{:S(2)}) copy-start(pred[128,128]{0,1:T(8,128)(4,1)} %copy-done.16) | copy-start | bytes 49156
  222.1 8.7 %collective-permute-start.4 = (f32[2048,256]{1,0:T(8,128)}, f32[2048,256]{1,0:T(8,128)S(1)}, u32[]{:S(2)}, u32[]{:S(2)}) collective-permute-start(f32[2048,256]{1,0:T(8,128)} %bitcast.32), channel_id=1, source_target_pairs={{0,4},{4,0},{1,5},{5,1},{2,6},{6,2},{3,7},{7,3},{8,12},{12,8},{9,1... | collective-permute-start | bytes 6291464 | tf_op jit(solution)/shard_map/ppermute | solution.py:124
  232.7 2.4 %copy-start.1 = (bf16[4096,256]{1,0:T(8,128)(2,1)S(1)}, bf16[4096,256]{1,0:T(8,128)(2,1)}, u32[]{:S(2)}) copy-start(bf16[4096,256]{1,0:T(8,128)(2,1)} %param.9) | copy-start | bytes 6291460
  (5 other events, 8.1 us)

commit v13 on v12

--- a/solution.py
+++ b/solution.py
@@ -27,7 +27,6 @@
     count = lax.axis_size("cz")
     per = heads // count
     sent = lax.all_to_all(marked(combined, pair_log), "cz", 0, 0, tiled=True).reshape(count, per, width + 8, state)
-    parts = sent[:, :, :width]
     chip_logs = sent[:, :, width, 0]
     edge = jnp.cumsum(chip_logs, axis=0) - chip_logs
     after = edge + chip_logs
@@ -36,10 +35,10 @@
     fwd_w = jnp.exp(jnp.where(earlier[:, :, None], edge[:, None, :] - after[None, :, :], -jnp.inf))
     bwd_w = jnp.exp(jnp.where(earlier.T[:, :, None], edge[None, :, :] - after[:, None, :], -jnp.inf))
     weight = jnp.where(first, bwd_w, fwd_w)
-    res = jnp.einsum("djh,jhpn->dhpn", weight, parts, precision=HIGH).reshape(count * per, width, state)
+    res = jnp.einsum("djh,jhpn->dhpn", weight, sent, precision=HIGH).reshape(count * per, width + 8, state)
     back = lax.all_to_all(res, "cz", 0, 0, tiled=True)
-    other = lax.ppermute(back, "core", swap)
-    fixed = jnp.exp(partner_log)[:, None, None] * back + partner
+    other = lax.ppermute(back, "core", swap)[:, :width]
+    fixed = jnp.exp(partner_log)[:, None, None] * back[:, :width] + partner
     return jnp.where(first, other, fixed), jnp.where(first, fixed, other)
 
 

time: 236 us -> 234 us (level)
  local copies, waits for them, and re-layouts: 20.8 us -> 17.7 us
    slice x1 -> x0, local copies, waits for them, and re-layouts: 3.14 us -> none  [exchange(): parts = sent[:, :, :width]]
where the time goes in v13:
time: 234 us; the launch traced here: 233 us
  blocking collectives  106 us (45%)
  waiting for transfers between devices  40.7 us (17%)
  matrix products  29.3 us (13%)
  other arithmetic  23.2 us (10%)
  local copies, waits for them, and re-layouts  17.7 us (8%)
  starting transfers between devices  15.3 us (7%)
    all_to_all x1, blocking collectives, per_device(): pieces = lax.all_to_all(parcel, axes, 0, 0, tiled=True)  41.5 us
    all_to_all x1, waiting for transfers between devices, exchange(): lax.all_to_all(marked(combined, pair_log), 'cz', 0, 0, tiled=True)  34.3 us
    all_to_all x1, blocking collectives, per_device(): lax.all_to_all(spread, axes, 0, 0, tiled=True).reshape(half, cols)  32.9 us
    all_to_all x1, blocking collectives, exchange(): back = lax.all_to_all(res, 'cz', 0, 0, tiled=True)  31.8 us
    all_to_all x1, starting transfers between devices, exchange(): lax.all_to_all(marked(combined, pair_log), 'cz', 0, 0, tiled=True)  7.75 us
    dot_general x2, matrix products, block_forward(): jnp.einsum('shp,sn->hpn', inputs * tail[:, :, None], b_in, precision=HIGH)  6.76 us
    dot_general x2, matrix products, block_forward(): y_intra = jnp.einsum('hts,shp->thp', mixing, inputs, precision=HIGH)  6.01 us
    unnamed x50, local copies, waits for them, and re-layouts  5.37 us
  transfers between devices with their start and end apart: 6, of which 3 were waited for; matrix products, arithmetic and copies ran while one was open for 7% of the time, Pallas kernels for 0%

profile of v13, /device:TPU:1, one launch (start us, length us, event | category | flops | bytes accessed | tf_op | source)
XLA Modules:
  0.0 233.3 jit_solution(8007362347494252508)
XLA Ops:
  0.7 2.7 %copy.121 = f32[1,128,4096]{1,2,0:T(8,128)} copy(bf16[1,128,4096]{2,1,0:T(8,128)(2,1)} %param.10) | data formatting | bytes 3145728 | tf_op jit(solution)/shard_map/convert_element_type | solution.py:91
  9.4 2.0 broadcast_select_fusion.2
  14.5 4.2 %collective-permute-done = f32[32,136,128]{2,1,0:T(8,128)} collective-permute-done((f32[32,136,128]{2,1,0:T(8,128)}, f32[32,136,128]{2,1,0:T(8,128)}, u32[]{:S(2)}, u32[]{:S(2)}) %collective-permute-start) | collective-permute-done | bytes 2228256 | tf_op jit(solution)/shard_map/ppermute | solution.py:21
  20.5 2.6 %multiply_add_fusion = f32[32,128,128]{2,1,0:T(8,128)S(1)} fusion(f32[32,128,128]{2,1,0:T(8,128)} %copy-done.4, f32[32,128,128]{2,1,0:T(8,128)} %get-tuple-element.53, f32[32,136,128]{2,1,0:T(8,128)} %collective-permute-done, f32[32]{0:T(128)S(1)} %fusion.107, pred[]{:T(512)S(6)} %eq.4), kind=kLoop, calls=%fused_computation.30 | loop fusion | flops 1572864 | bytes 8388737 | tf_op jit(solution)/shard_map/add | solution.py:26
  24.7 7.8 %all-to-all-start = ((f32[32,136,128]{2,1,0:T(8,128)}), f32[32,136,128]{2,1,0:T(8,128)}, u32[]{:S(2)}, u32[]{:S(2)}) async-start(f32[32,136,128]{2,1,0:T(8,128)} %pad_maximum_fusion.3), calls=%async_computation | async-start | bytes 4456448 | tf_op jit(solution)/shard_map/all_to_all | solution.py:29
  32.4 34.3 %all-to-all-done = f32[32,136,128]{2,1,0:T(8,128)} async-done(((f32[32,136,128]{2,1,0:T(8,128)}), f32[32,136,128]{2,1,0:T(8,128)}, u32[]{:S(2)}, u32[]{:S(2)}) %all-to-all-start) | async-done | bytes 2228256 | tf_op jit(solution)/shard_map/all_to_all | solution.py:29
  68.0 3.1 %fusion.20 = f32[16,2,136,128]{3,0,2,1:T(8,128)S(1)} fusion(f32[16,2,136,128]{3,2,1,0:T(8,128)} %bitcast.8, f32[16,2]{0,1:T(2,128)S(1)} %copy.132, f32[16,2]{0,1:T(2,128)S(1)} %copy.130, pred[16,16]{1,0:T(8,128)(4,1)S(1)} %get-tuple-element.56, pred[16,16]{1,0:T(8,128)(4,1)S(1)} %get-tuple-element.57, pred[]{:T(512)S(6)} %eq.4), kind=kOutput, calls=%fused_computation.38 | convolution fusion | flops 53479936 | bytes 4457217 | tf_op jit(solution)/shard_map/djh,jhpn->dhpn/dot_general | solution.py:38
  71.8 31.8 %all_to_all.20 = f32[32,136,128]{2,1,0:T(8,128)} all-to-all(f32[32,136,128]{2,1,0:T(8,128)S(1)} %bitcast.150), channel_id=1, replica_groups=mesh['cz'=16,'core'=2,'dp'=4] {'cz'}, dimensions={0} | all-to-all | bytes 4456448 | tf_op jit(solution)/shard_map/all_to_all | solution.py:39
  103.6 2.5 %collective-permute-start.1 = (f32[32,136,128]{2,1,0:T(8,128)}, f32[32,136,128]{2,1,0:T(8,128)}, u32[]{:S(2)}, u32[]{:S(2)}) collective-permute-start(f32[32,136,128]{2,1,0:T(8,128)} %all_to_all.20), channel_id=1, source_target_pairs={{0,4},{4,0},{1,5},{5,1},{2,6},{6,2},{3,7},{7,3},{8,12},{12,8},{9,1... | collective-permute-start | bytes 6684680 | tf_op jit(solution)/shard_map/ppermute | solution.py:40
  106.8 3.3 %fusion.24 = (f32[32,128]{1,0:T(8,128)}, f32[32,128]{1,0:T(8,128)S(1)}, f32[128,128]{0,1:T(8,128)}) fusion(f32[128,128]{0,1:T(8,128)S(1)} %fusion.78, f32[32,128]{1,0:T(8,128)S(1)} %reduce_window_sum.46, pred[128,128]{0,1:T(8,128)(4,1)S(1)} %iota_compare_fusion, bf16[32,128,128]{2,1,0:T(8,128)(2,1)S(1)} %bitcast.146, f32[128,32,128]{0,2,1:T(8,128)S(1)} %bitcast.142, ...), kind=kOutput, calls=%fused_computation.40 | convolution fusion | flops 407871488 | bytes 3358720 | tf_op jit(solution)/shard_map/transpose(jvp(hts,shp->thp))/dot_general | solution.py:63
  114.2 4.1 %multiply_reduce_fusion = (f32[32]{0:T(128)}, f32[32,128,128]{2,1,0:T(8,128)S(1)}, f32[32,128,128]{2,1,0:T(8,128)S(1)}) fusion(f32[32,136,128]{2,1,0:T(8,128)} %collective-permute-done, f32[32,136,128]{2,1,0:T(8,128)} %all_to_all.20, f32[32]{0:T(128)} %get-tuple-element.30, f32[32,136,128]{2,1,0:T(8,128)} %collective-permute-done.1, pred[]{:T(512)S(6)} %eq.4), kind=kLoop, calls=%fused_computation.23 | loop fusion | flops 3145696 | bytes 10486017 | tf_op jit(solution)/shard_map/transpose(jvp())/reduce_sum | solution.py:67
  118.3 3.2 %multiply_reduce_fusion.1 = (f32[128,32]{0,1:T(8,128)}, f32[128,32,128]{0,2,1:T(8,128)}) fusion(f32[128,32,128]{0,2,1:T(8,128)S(1)} %bitcast.143, f32[128,32]{0,1:T(8,128)S(1)} %copy.143, f32[32,128,128]{2,1,0:T(8,128)S(1)} %get-tuple-element.37, bf16[128,256]{1,0:T(8,128)(2,1)S(1)} %convolution_convert_fusion), kind=kOutput, calls=%fused_computation.24 | convolution fusion | flops 404221952 | bytes 6356992 | tf_op jit(solution)/shard_map/transpose(jvp(shp,sn->hpn))/dot_general | solution.py:66
  130.4 3.6 %fusion.34 = bf16[128,128]{1,0:T(8,128)(2,1)S(1)} fusion(f32[128,128]{1,0:T(8,128)S(1)} %fusion.76, f32[32,128,128]{2,1,0:T(8,128)} %copy-done.3, f32[128,32,128]{0,2,1:T(8,128)S(1)} %bitcast.144, f32[128,32]{0,1:T(8,128)S(1)} %copy.143, f32[128,32]{0,1:T(8,128)S(1)} %copy.140), kind=kOutput, calls=%fused_computation.47 | convolution fusion | flops 403734528 | bytes 4325376 | tf_op jit(solution)/shard_map/transpose(jvp(shp,sn->hpn))/dot_general | solution.py:66
  134.0 1.9 fusion.33
  138.6 2.2 collective-permute-done.3
  140.9 2.4 %convolution_add_fusion = f32[2048,256]{1,0:T(8,128)S(1)} fusion(f32[2048,256]{1,0:T(8,128)} %collective-permute-done.2, pred[]{:T(512)S(6)} %eq.4, bf16[128,4096]{1,0:T(8,128)(2,1)} %bitcast.152, bf16[128,128]{1,0:T(8,128)(2,1)S(1)} %fusion.34, bf16[128,128]{1,0:T(8,128)(2,1)S(1)} %fusion.33), kind=kOutput, calls=%fused_computation.4 | convolution fusion | flops 135135232 | bytes 5308417 | tf_op jit(solution)/shard_map/dot_general | solution.py:107
  143.7 41.5 %all_to_all.21 = f32[64,40,256]{2,1,0:T(8,128)} all-to-all(f32[64,40,256]{2,1,0:T(8,128)S(1)} %pad_maximum_fusion.1), channel_id=1, replica_groups=mesh['cz'=16,'core'=2,'dp'=4] {'cz','dp'}, dimensions={0} | all-to-all | bytes 5242880 | tf_op jit(solution)/shard_map/all_to_all | solution.py:119
  185.2 1.9 reduce_sum.104
  187.4 32.9 %all_to_all.22 = f32[64,32,256]{2,1,0:T(8,128)} all-to-all(f32[64,32,256]{2,1,0:T(8,128)S(1)} %broadcast_in_dim.56), channel_id=1, replica_groups=mesh['cz'=16,'core'=2,'dp'=4] {'cz','dp'}, dimensions={0} | all-to-all | bytes 4194304 | tf_op jit(solution)/shard_map/all_to_all | solution.py:122
  220.3 3.2 %collective-permute-start.4 = (f32[2048,256]{1,0:T(8,128)}, f32[2048,256]{1,0:T(8,128)S(1)}, u32[]{:S(2)}, u32[]{:S(2)}) collective-permute-start(f32[2048,256]{1,0:T(8,128)} %bitcast.32), channel_id=1, source_target_pairs={{0,4},{4,0},{1,5},{5,1},{2,6},{6,2},{3,7},{7,3},{8,12},{12,8},{9,1... | collective-permute-start | bytes 6291464 | tf_op jit(solution)/shard_map/ppermute | solution.py:123
  223.5 2.7 %fusion.10 = bf16[128,32,128]{0,2,1:T(8,128)(2,1)} fusion(f32[128,32,128]{0,2,1:T(8,128)S(1)} %copy-done.8, f32[128,32]{0,1:T(8,128)S(1)} %copy.143, bf16[32,128,128]{2,1,0:T(8,128)(2,1)S(1)} %bitcast.149, f32[128,128]{0,1:T(8,128)S(1)} %copy-done.14, f32[32,128]{1,0:T(8,128)S(1)} %copy-done.12, f32[128,32]{0,1:T(8,128)S(1)} %copy.140, ...), kind=kOutput, calls=%fused_computation.22 | convolution fusion | flops 406323200 | bytes 4325376 | tf_op jit(solution)/shard_map/transpose(jvp(hts,shp->thp))/dot_general | solution.py:63
  226.3 2.3 copy.155
  229.0 1.9 broadcast_select_fusion.1
  230.9 2.3 pad_maximum_fusion
  (112 shorter events, 32.2 us)
Async XLA Ops:
  0.6 5.4 %copy-start = (bf16[4096,256]{1,0:T(8,128)(2,1)S(1)}, bf16[4096,256]{1,0:T(8,128)(2,1)}, u32[]{:S(2)}) copy-start(bf16[4096,256]{1,0:T(8,128)(2,1)} %param.9) | copy-start | bytes 6291460
  0.6 2.7 %copy-start.15 = (f32[1,128,32]{1,2,0:T(8,128)S(1)}, f32[1,128,32]{1,2,0:T(8,128)}, u32[]{:S(2)}) copy-start(f32[1,128,32]{1,2,0:T(8,128)} %param.11) | copy-start | bytes 49156
  0.7 2.8 %copy-start.21 = (f32[32]{0:T(128)S(1)}, f32[32]{0:T(128)}, u32[]{:S(2)}) copy-start(f32[32]{0:T(128)} %param.12) | copy-start | bytes 388
  8.5 2.9 %copy-start.4 = (f32[32,128,128]{2,1,0:T(8,128)}, f32[32,128,128]{2,1,0:T(8,128)S(1)}, u32[]{:S(2)}) copy-start(f32[32,128,128]{2,1,0:T(8,128)S(1)} %fusion.2) | copy-start | bytes 6291460
  11.5 2.9 %copy-start.20 = (f32[32,1,1]{0,2,1:T(1,128)S(1)}, f32[32,1,1]{0,2,1:T(1,128)}, u32[]{:S(2)}) copy-start(f32[32,1,1]{0,2,1:T(1,128)} %get-tuple-element.48) | copy-start | bytes 388
  13.0 5.7 %collective-permute-start = (f32[32,136,128]{2,1,0:T(8,128)}, f32[32,136,128]{2,1,0:T(8,128)}, u32[]{:S(2)}, u32[]{:S(2)}) collective-permute-start(f32[32,136,128]{2,1,0:T(8,128)} %pad_maximum_fusion.2), channel_id=1, source_target_pairs={{0,4},{4,0},{1,5},{5,1},{2,6},{6,2},{3,7},{7,3},{8,12},{12,8},{9,1... | collective-permute-start | bytes 6684680 | tf_op jit(solution)/shard_map/ppermute | solution.py:21
  24.7 42.0 %all-to-all-start = ((f32[32,136,128]{2,1,0:T(8,128)}), f32[32,136,128]{2,1,0:T(8,128)}, u32[]{:S(2)}, u32[]{:S(2)}) async-start(f32[32,136,128]{2,1,0:T(8,128)} %pad_maximum_fusion.3), calls=%async_computation | async-start | bytes 4456448 | tf_op jit(solution)/shard_map/all_to_all | solution.py:29
  103.6 10.6 %collective-permute-start.1 = (f32[32,136,128]{2,1,0:T(8,128)}, f32[32,136,128]{2,1,0:T(8,128)}, u32[]{:S(2)}, u32[]{:S(2)}) collective-permute-start(f32[32,136,128]{2,1,0:T(8,128)} %all_to_all.20), channel_id=1, source_target_pairs={{0,4},{4,0},{1,5},{5,1},{2,6},{6,2},{3,7},{7,3},{8,12},{12,8},{9,1... | collective-permute-start | bytes 6684680 | tf_op jit(solution)/shard_map/ppermute | solution.py:40
  106.5 3.5 %copy-start.11 = (f32[32,128]{1,0:T(8,128)}, f32[32,128]{1,0:T(8,128)S(1)}, u32[]{:S(2)}) copy-start(f32[32,128]{1,0:T(8,128)S(1)} %reduce_window_sum.46) | copy-start | bytes 49156
  106.6 3.4 %copy-start.16 = (pred[128,128]{0,1:T(8,128)(4,1)}, pred[128,128]{0,1:T(8,128)(4,1)S(1)}, u32[]{:S(2)}) copy-start(pred[128,128]{0,1:T(8,128)(4,1)S(1)} %iota_compare_fusion) | copy-start | bytes 49156
  106.8 3.3 %copy-start.13 = (f32[128,128]{0,1:T(8,128)}, f32[128,128]{0,1:T(8,128)S(1)}, u32[]{:S(2)}) copy-start(f32[128,128]{0,1:T(8,128)S(1)} %fusion.78) | copy-start | bytes 196612
  118.3 3.2 %copy-start.3 = (f32[32,128,128]{2,1,0:T(8,128)}, f32[32,128,128]{2,1,0:T(8,128)S(1)}, u32[]{:S(2)}) copy-start(f32[32,128,128]{2,1,0:T(8,128)S(1)} %get-tuple-element.37) | copy-start | bytes 6291460
  118.3 3.2 %copy-start.5 = (f32[32,128,128]{2,1,0:T(8,128)}, f32[32,128,128]{2,1,0:T(8,128)S(1)}, u32[]{:S(2)}) copy-start(f32[32,128,128]{2,1,0:T(8,128)S(1)} %get-tuple-element.36) | copy-start | bytes 6291460
  130.4 3.6 %copy-start.6 = (f32[32,128,128]{2,1,0:T(8,128)S(1)}, f32[32,128,128]{2,1,0:T(8,128)}, u32[]{:S(2)}) copy-start(f32[32,128,128]{2,1,0:T(8,128)} %copy-done.5) | copy-start | bytes 6291460
  130.4 3.6 %copy-start.10 = (f32[128,128]{1,0:T(8,128)S(1)}, f32[128,128]{1,0:T(8,128)}, u32[]{:S(2)}) copy-start(f32[128,128]{1,0:T(8,128)} %fusion.83) | copy-start | bytes 196612
  135.9 2.3 copy-start.22
  136.4 4.5 %collective-permute-start.2 = (f32[2048,256]{1,0:T(8,128)S(1)}, f32[2048,256]{1,0:T(8,128)}, u32[]{:S(2)}, u32[]{:S(2)}) collective-permute-start(f32[2048,256]{1,0:T(8,128)S(1)} %fusion.50), channel_id=1, source_target_pairs={{0,4},{4,0},{1,5},{5,1},{2,6},{6,2},{3,7},{7,3},{8,12},{12,8},{9,1... | collective-permute-start | bytes 6291464 | tf_op jit(solution)/shard_map/ppermute | solution.py:111
  138.3 2.5 %collective-permute-start.3 = (f32[8,256]{1,0:T(8,128)S(1)}, f32[8,256]{1,0:T(8,128)S(1)}, u32[]{:S(2)}, u32[]{:S(2)}) collective-permute-start(f32[8,256]{1,0:T(8,128)S(1)} %scatter.7), channel_id=1, source_target_pairs={{0,4},{4,0},{1,5},{5,1},{2,6},{6,2},{3,7},{7,3},{8,12},{12,8},{9,1... | collective-permute-start | bytes 24584 | tf_op jit(solution)/shard_map/ppermute | solution.py:112
  187.4 36.1 %copy-start.8 = (f32[128,32,128]{0,2,1:T(8,128)S(1)}, f32[128,32,128]{0,2,1:T(8,128)}, u32[]{:S(2)}) copy-start(f32[128,32,128]{0,2,1:T(8,128)} %get-tuple-element.55) | copy-start | bytes 6291460
  187.4 36.1 %copy-start.12 = (f32[32,128]{1,0:T(8,128)S(1)}, f32[32,128]{1,0:T(8,128)}, u32[]{:S(2)}) copy-start(f32[32,128]{1,0:T(8,128)} %copy-done.11) | copy-start | bytes 49156
  187.4 36.1 %copy-start.14 = (f32[128,128]{0,1:T(8,128)S(1)}, f32[128,128]{0,1:T(8,128)}, u32[]{:S(2)}) copy-start(f32[128,128]{0,1:T(8,128)} %copy-done.13) | copy-start | bytes 196612
  187.4 36.1 %copy-start.17 = (pred[128,128]{0,1:T(8,128)(4,1)S(1)}, pred[128,128]{0,1:T(8,128)(4,1)}, u32[]{:S(2)}) copy-start(pred[128,128]{0,1:T(8,128)(4,1)} %copy-done.16) | copy-start | bytes 49156
  220.3 8.7 %collective-permute-start.4 = (f32[2048,256]{1,0:T(8,128)}, f32[2048,256]{1,0:T(8,128)S(1)}, u32[]{:S(2)}, u32[]{:S(2)}) collective-permute-start(f32[2048,256]{1,0:T(8,128)} %bitcast.32), channel_id=1, source_target_pairs={{0,4},{4,0},{1,5},{5,1},{2,6},{6,2},{3,7},{7,3},{8,12},{12,8},{9,1... | collective-permute-start | bytes 6291464 | tf_op jit(solution)/shard_map/ppermute | solution.py:123
  230.9 2.4 %copy-start.1 = (bf16[4096,256]{1,0:T(8,128)(2,1)S(1)}, bf16[4096,256]{1,0:T(8,128)(2,1)}, u32[]{:S(2)}) copy-start(bf16[4096,256]{1,0:T(8,128)(2,1)} %param.9) | copy-start | bytes 6291460
  (5 other events, 8.1 us)

commit v14 on v13

--- a/solution.py
+++ b/solution.py
@@ -18,7 +18,9 @@
     def marked(value, logs):
         return jnp.concatenate([value, jnp.broadcast_to(logs[:, None, None], (heads, 8, state))], axis=1)
 
-    got = lax.ppermute(marked(jnp.where(first, own_state, back_term), log_total), "core", swap)
+    ahead = lax.ppermute(marked(own_state, log_total), "core", [(0, 1)])
+    behind = lax.ppermute(marked(back_term, log_total), "core", [(1, 0)])
+    got = jnp.where(first, behind, ahead)
     partner = got[:, :width]
     partner_log = got[:, width, 0]
     pair_log = log_total + partner_log

time: 234 us -> 238 us (1.017)
  starting transfers between devices: 15.3 us -> 19.8 us
    ppermute x1 -> x2, starting transfers between devices: 1.38 us -> 5.92 us  [the longest x1 4.64 us: exchange(): behind = lax.ppermute(marked(back_term, log_total), 'core', [(1, 0)])]
    ppermute x1 -> x2, waiting for transfers between devices: 4.22 us -> 5.18 us  [the longest x1 3.64 us: exchange(): ahead = lax.ppermute(marked(own_state, log_total), 'core', [(0, 1)])]
  transfers between devices with their start and end apart: 6 -> 7, of which waited for: 3 -> 4; matrix products, arithmetic and copies ran while one was open for 7% -> 6% of each run, Pallas kernels for 0% -> 0%
where the time goes in v14:
time: 238 us; the launch traced here: 237 us
  blocking collectives  106 us (45%)
  waiting for transfers between devices  42.2 us (18%)
  matrix products  28.2 us (12%)
  other arithmetic  23.4 us (10%)
  starting transfers between devices  19.8 us (8%)
  local copies, waits for them, and re-layouts  16.5 us (7%)
    all_to_all x1, blocking collectives, per_device(): pieces = lax.all_to_all(parcel, axes, 0, 0, tiled=True)  41.5 us
    all_to_all x1, waiting for transfers between devices, exchange(): lax.all_to_all(marked(combined, pair_log), 'cz', 0, 0, tiled=True)  34.8 us
    all_to_all x1, blocking collectives, per_device(): lax.all_to_all(spread, axes, 0, 0, tiled=True).reshape(half, cols)  32.9 us
    all_to_all x1, blocking collectives, exchange(): back = lax.all_to_all(res, 'cz', 0, 0, tiled=True)  31.9 us
    all_to_all x1, starting transfers between devices, exchange(): lax.all_to_all(marked(combined, pair_log), 'cz', 0, 0, tiled=True)  7.75 us
    dot_general x2, matrix products, block_forward(): jnp.einsum('shp,sn->hpn', inputs * tail[:, :, None], b_in, precision=HIGH)  6.77 us
    dot_general x2, matrix products, block_forward(): y_intra = jnp.einsum('hts,shp->thp', mixing, inputs, precision=HIGH)  5.98 us
  transfers between devices with their start and end apart: 7, of which 4 were waited for; matrix products, arithmetic and copies ran while one was open for 6% of the time, Pallas kernels for 0%

profile of v14, /device:TPU:1, one launch (start us, length us, event | category | flops | bytes accessed | tf_op | source)
XLA Modules:
  0.0 237.3 jit_solution(7067100925842636616)
XLA Ops:
  0.7 2.8 %copy.124 = f32[1,128,4096]{1,2,0:T(8,128)} copy(bf16[1,128,4096]{2,1,0:T(8,128)(2,1)} %param.10) | data formatting | bytes 3145728 | tf_op jit(solution)/shard_map/convert_element_type | solution.py:93
  9.1 2.7 %pad_maximum_fusion.1 = (f32[32,136,128]{2,1,0:T(8,128)}, f32[32,136,128]{2,1,0:T(8,128)}) fusion(f32[32,8,128]{2,1,0:T(8,128)S(1)} %broadcast_in_dim.48, f32[32,128,128]{2,1,0:T(8,128)S(1)} %fusion.15, f32[32,128,128]{2,1,0:T(8,128)S(1)} %fusion.2), kind=kLoop, calls=%fused_computation.1 | loop fusion | flops 1114112 | bytes 8781824 | tf_op jit(solution)/shard_map/concatenate | solution.py:19
  11.8 4.6 %collective-permute-start = (f32[32,136,128]{2,1,0:T(8,128)}, f32[32,136,128]{2,1,0:T(8,128)}, u32[]{:S(2)}, u32[]{:S(2)}) collective-permute-start(f32[32,136,128]{2,1,0:T(8,128)} %get-tuple-element.43), channel_id=1, source_target_pairs={{4,0},{5,1},{6,2},{7,3},{12,8},{13,9},{14,10},{15,11},{20,16},{21,... | collective-permute-start | bytes 6684680 | tf_op jit(solution)/shard_map/ppermute | solution.py:22
  19.4 3.6 %collective-permute-done.1 = f32[32,136,128]{2,1,0:T(8,128)} collective-permute-done((f32[32,136,128]{2,1,0:T(8,128)}, f32[32,136,128]{2,1,0:T(8,128)}, u32[]{:S(2)}, u32[]{:S(2)}) %collective-permute-start.1) | collective-permute-done | bytes 2228256 | tf_op jit(solution)/shard_map/ppermute | solution.py:21
  28.0 7.8 %all-to-all-start = ((f32[32,136,128]{2,1,0:T(8,128)}), f32[32,136,128]{2,1,0:T(8,128)}, u32[]{:S(2)}, u32[]{:S(2)}) async-start(f32[32,136,128]{2,1,0:T(8,128)} %pad_maximum_fusion.4), calls=%async_computation | async-start | bytes 4456448 | tf_op jit(solution)/shard_map/all_to_all | solution.py:31
  35.7 34.8 %all-to-all-done = f32[32,136,128]{2,1,0:T(8,128)} async-done(((f32[32,136,128]{2,1,0:T(8,128)}), f32[32,136,128]{2,1,0:T(8,128)}, u32[]{:S(2)}, u32[]{:S(2)}) %all-to-all-start) | async-done | bytes 2228256 | tf_op jit(solution)/shard_map/all_to_all | solution.py:31
  71.8 3.1 %fusion.20 = f32[16,2,136,128]{3,0,2,1:T(8,128)S(1)} fusion(f32[16,2,136,128]{3,2,1,0:T(8,128)} %bitcast.8, f32[16,2]{0,1:T(2,128)S(1)} %copy.132, f32[16,2]{0,1:T(2,128)S(1)} %copy.130, pred[16,16]{1,0:T(8,128)(4,1)S(1)} %get-tuple-element.56, pred[16,16]{1,0:T(8,128)(4,1)S(1)} %get-tuple-element.57, pred[]{:T(512)S(6)} %eq.4), kind=kOutput, calls=%fused_computation.39 | convolution fusion | flops 53479936 | bytes 4457217 | tf_op jit(solution)/shard_map/djh,jhpn->dhpn/dot_general | solution.py:40
  75.7 31.9 %all_to_all.20 = f32[32,136,128]{2,1,0:T(8,128)} all-to-all(f32[32,136,128]{2,1,0:T(8,128)S(1)} %bitcast.148), channel_id=1, replica_groups=mesh['cz'=16,'core'=2,'dp'=4] {'cz'}, dimensions={0} | all-to-all | bytes 4456448 | tf_op jit(solution)/shard_map/all_to_all | solution.py:41
  107.6 2.5 %collective-permute-start.2 = (f32[32,136,128]{2,1,0:T(8,128)}, f32[32,136,128]{2,1,0:T(8,128)}, u32[]{:S(2)}, u32[]{:S(2)}) collective-permute-start(f32[32,136,128]{2,1,0:T(8,128)} %all_to_all.20), channel_id=1, source_target_pairs={{0,4},{4,0},{1,5},{5,1},{2,6},{6,2},{3,7},{7,3},{8,12},{12,8},{9,1... | collective-permute-start | bytes 6684680 | tf_op jit(solution)/shard_map/ppermute | solution.py:42
  110.8 3.2 %fusion.24 = (f32[32,128]{1,0:T(8,128)}, f32[32,128]{1,0:T(8,128)S(1)}, f32[128,128]{0,1:T(8,128)}) fusion(f32[128,128]{0,1:T(8,128)S(1)} %fusion.78, f32[32,128]{1,0:T(8,128)S(1)} %reduce_window_sum.46, pred[128,128]{0,1:T(8,128)(4,1)S(1)} %iota_compare_fusion, bf16[32,128,128]{2,1,0:T(8,128)(2,1)S(1)} %bitcast.144, f32[128,32,128]{0,2,1:T(8,128)S(1)} %bitcast.140, ...), kind=kOutput, calls=%fused_computation.41 | convolution fusion | flops 407871488 | bytes 3358720 | tf_op jit(solution)/shard_map/transpose(jvp(hts,shp->thp))/dot_general | solution.py:65
  118.2 4.1 %multiply_reduce_fusion = (f32[32]{0:T(128)}, f32[32,128,128]{2,1,0:T(8,128)S(1)}, f32[32,128,128]{2,1,0:T(8,128)S(1)}) fusion(f32[32,136,128]{2,1,0:T(8,128)} %copy-done.9, f32[32,136,128]{2,1,0:T(8,128)} %all_to_all.20, f32[32]{0:T(128)} %get-tuple-element.30, f32[32,136,128]{2,1,0:T(8,128)} %collective-permute-done.2, pred[]{:T(512)S(6)} %eq.4), kind=kLoop, calls=%fused_computation.24 | loop fusion | flops 3145696 | bytes 10486017 | tf_op jit(solution)/shard_map/transpose(jvp())/reduce_sum | solution.py:69
  122.3 3.2 %multiply_reduce_fusion.1 = (f32[128,32]{0,1:T(8,128)}, f32[128,32,128]{0,2,1:T(8,128)}) fusion(f32[128,32,128]{0,2,1:T(8,128)S(1)} %bitcast.141, f32[128,32]{0,1:T(8,128)S(1)} %copy.143, f32[32,128,128]{2,1,0:T(8,128)S(1)} %get-tuple-element.37, bf16[128,256]{1,0:T(8,128)(2,1)S(1)} %convolution_convert_fusion), kind=kOutput, calls=%fused_computation.25 | convolution fusion | flops 404221952 | bytes 6356992 | tf_op jit(solution)/shard_map/transpose(jvp(shp,sn->hpn))/dot_general | solution.py:68
  134.4 3.6 %fusion.34 = bf16[128,128]{1,0:T(8,128)(2,1)S(1)} fusion(f32[128,128]{1,0:T(8,128)S(1)} %fusion.76, f32[32,128,128]{2,1,0:T(8,128)} %copy-done.6, f32[128,32,128]{0,2,1:T(8,128)S(1)} %bitcast.142, f32[128,32]{0,1:T(8,128)S(1)} %copy.143, f32[128,32]{0,1:T(8,128)S(1)} %copy.140), kind=kOutput, calls=%fused_computation.48 | convolution fusion | flops 403734528 | bytes 4325376 | tf_op jit(solution)/shard_map/transpose(jvp(shp,sn->hpn))/dot_general | solution.py:68
  138.0 1.9 fusion.33
  142.6 2.2 collective-permute-done.4
  144.9 2.4 %convolution_add_fusion = f32[2048,256]{1,0:T(8,128)S(1)} fusion(f32[2048,256]{1,0:T(8,128)} %collective-permute-done.3, pred[]{:T(512)S(6)} %eq.4, bf16[128,4096]{1,0:T(8,128)(2,1)} %bitcast.150, bf16[128,128]{1,0:T(8,128)(2,1)S(1)} %fusion.34, bf16[128,128]{1,0:T(8,128)(2,1)S(1)} %fusion.33), kind=kOutput, calls=%fused_computation.6 | convolution fusion | flops 135135232 | bytes 5308417 | tf_op jit(solution)/shard_map/dot_general | solution.py:109
  147.7 41.5 %all_to_all.21 = f32[64,40,256]{2,1,0:T(8,128)} all-to-all(f32[64,40,256]{2,1,0:T(8,128)S(1)} %pad_maximum_fusion.3), channel_id=1, replica_groups=mesh['cz'=16,'core'=2,'dp'=4] {'cz','dp'}, dimensions={0} | all-to-all | bytes 5242880 | tf_op jit(solution)/shard_map/all_to_all | solution.py:121
  189.2 1.9 reduce_sum.104
  191.4 32.9 %all_to_all.22 = f32[64,32,256]{2,1,0:T(8,128)} all-to-all(f32[64,32,256]{2,1,0:T(8,128)S(1)} %broadcast_in_dim.59), channel_id=1, replica_groups=mesh['cz'=16,'core'=2,'dp'=4] {'cz','dp'}, dimensions={0} | all-to-all | bytes 4194304 | tf_op jit(solution)/shard_map/all_to_all | solution.py:124
  224.3 3.2 %collective-permute-start.5 = (f32[2048,256]{1,0:T(8,128)}, f32[2048,256]{1,0:T(8,128)S(1)}, u32[]{:S(2)}, u32[]{:S(2)}) collective-permute-start(f32[2048,256]{1,0:T(8,128)} %bitcast.32), channel_id=1, source_target_pairs={{0,4},{4,0},{1,5},{5,1},{2,6},{6,2},{3,7},{7,3},{8,12},{12,8},{9,1... | collective-permute-start | bytes 6291464 | tf_op jit(solution)/shard_map/ppermute | solution.py:125
  227.5 2.7 %fusion.10 = bf16[128,32,128]{0,2,1:T(8,128)(2,1)} fusion(f32[128,32,128]{0,2,1:T(8,128)S(1)} %copy-done.11, f32[128,32]{0,1:T(8,128)S(1)} %copy.143, bf16[32,128,128]{2,1,0:T(8,128)(2,1)S(1)} %bitcast.147, f32[128,128]{0,1:T(8,128)S(1)} %copy-done.17, f32[32,128]{1,0:T(8,128)S(1)} %copy-done.15, f32[128,32]{0,1:T(8,128)S(1)} %copy.140, ...), kind=kOutput, calls=%fused_computation.23 | convolution fusion | flops 406323200 | bytes 4325376 | tf_op jit(solution)/shard_map/transpose(jvp(hts,shp->thp))/dot_general | solution.py:65
  230.2 2.3 copy.155
  233.0 1.9 broadcast_select_fusion.2
  234.9 2.3 pad_maximum_fusion
  (115 shorter events, 33.2 us)
Async XLA Ops:
  0.6 5.0 %copy-start = (bf16[4096,256]{1,0:T(8,128)(2,1)S(1)}, bf16[4096,256]{1,0:T(8,128)(2,1)}, u32[]{:S(2)}) copy-start(bf16[4096,256]{1,0:T(8,128)(2,1)} %param.9) | copy-start | bytes 6291460
  0.6 2.8 %copy-start.18 = (f32[1,128,32]{1,2,0:T(8,128)S(1)}, f32[1,128,32]{1,2,0:T(8,128)}, u32[]{:S(2)}) copy-start(f32[1,128,32]{1,2,0:T(8,128)} %param.11) | copy-start | bytes 49156
  0.7 2.9 %copy-start.21 = (f32[32]{0:T(128)S(1)}, f32[32]{0:T(128)}, u32[]{:S(2)}) copy-start(f32[32]{0:T(128)} %param.12) | copy-start | bytes 388
  9.0 2.8 %copy-start.4 = (f32[32,128,128]{2,1,0:T(8,128)}, f32[32,128,128]{2,1,0:T(8,128)S(1)}, u32[]{:S(2)}) copy-start(f32[32,128,128]{2,1,0:T(8,128)S(1)} %fusion.2) | copy-start | bytes 6291460
  11.8 7.6 %collective-permute-start = (f32[32,136,128]{2,1,0:T(8,128)}, f32[32,136,128]{2,1,0:T(8,128)}, u32[]{:S(2)}, u32[]{:S(2)}) collective-permute-start(f32[32,136,128]{2,1,0:T(8,128)} %get-tuple-element.43), channel_id=1, source_target_pairs={{4,0},{5,1},{6,2},{7,3},{12,8},{13,9},{14,10},{15,11},{20,16},{21,... | collective-permute-start | bytes 6684680 | tf_op jit(solution)/shard_map/ppermute | solution.py:22
  16.4 6.6 %collective-permute-start.1 = (f32[32,136,128]{2,1,0:T(8,128)}, f32[32,136,128]{2,1,0:T(8,128)}, u32[]{:S(2)}, u32[]{:S(2)}) collective-permute-start(f32[32,136,128]{2,1,0:T(8,128)} %get-tuple-element.42), channel_id=1, source_target_pairs={{0,4},{1,5},{2,6},{3,7},{8,12},{9,13},{10,14},{11,15},{16,20},{17,... | collective-permute-start | bytes 6684680 | tf_op jit(solution)/shard_map/ppermute | solution.py:21
  17.8 8.1 %copy-start.5 = (f32[32,128,128]{2,1,0:T(8,128)S(1)}, f32[32,128,128]{2,1,0:T(8,128)}, u32[]{:S(2)}) copy-start(f32[32,128,128]{2,1,0:T(8,128)} %copy-done.4) | copy-start | bytes 6291460
  28.0 42.6 %all-to-all-start = ((f32[32,136,128]{2,1,0:T(8,128)}), f32[32,136,128]{2,1,0:T(8,128)}, u32[]{:S(2)}, u32[]{:S(2)}) async-start(f32[32,136,128]{2,1,0:T(8,128)} %pad_maximum_fusion.4), calls=%async_computation | async-start | bytes 4456448 | tf_op jit(solution)/shard_map/all_to_all | solution.py:31
  75.7 35.1 %copy-start.3 = (f32[1,128,4096]{1,2,0:T(8,128)S(1)}, f32[1,128,4096]{1,2,0:T(8,128)}, u32[]{:S(2)}) copy-start(f32[1,128,4096]{1,2,0:T(8,128)} %copy.124) | copy-start | bytes 6291460
  107.6 10.6 %collective-permute-start.2 = (f32[32,136,128]{2,1,0:T(8,128)}, f32[32,136,128]{2,1,0:T(8,128)}, u32[]{:S(2)}, u32[]{:S(2)}) collective-permute-start(f32[32,136,128]{2,1,0:T(8,128)} %all_to_all.20), channel_id=1, source_target_pairs={{0,4},{4,0},{1,5},{5,1},{2,6},{6,2},{3,7},{7,3},{8,12},{12,8},{9,1... | collective-permute-start | bytes 6684680 | tf_op jit(solution)/shard_map/ppermute | solution.py:42
  110.5 3.5 %copy-start.14 = (f32[32,128]{1,0:T(8,128)}, f32[32,128]{1,0:T(8,128)S(1)}, u32[]{:S(2)}) copy-start(f32[32,128]{1,0:T(8,128)S(1)} %reduce_window_sum.46) | copy-start | bytes 49156
  110.6 3.4 %copy-start.19 = (pred[128,128]{0,1:T(8,128)(4,1)}, pred[128,128]{0,1:T(8,128)(4,1)S(1)}, u32[]{:S(2)}) copy-start(pred[128,128]{0,1:T(8,128)(4,1)S(1)} %iota_compare_fusion) | copy-start | bytes 49156
  110.8 3.3 %copy-start.16 = (f32[128,128]{0,1:T(8,128)}, f32[128,128]{0,1:T(8,128)S(1)}, u32[]{:S(2)}) copy-start(f32[128,128]{0,1:T(8,128)S(1)} %fusion.78) | copy-start | bytes 196612
  122.2 3.2 %copy-start.6 = (f32[32,128,128]{2,1,0:T(8,128)}, f32[32,128,128]{2,1,0:T(8,128)S(1)}, u32[]{:S(2)}) copy-start(f32[32,128,128]{2,1,0:T(8,128)S(1)} %get-tuple-element.37) | copy-start | bytes 6291460
  122.3 3.2 %copy-start.7 = (f32[32,128,128]{2,1,0:T(8,128)}, f32[32,128,128]{2,1,0:T(8,128)S(1)}, u32[]{:S(2)}) copy-start(f32[32,128,128]{2,1,0:T(8,128)S(1)} %get-tuple-element.36) | copy-start | bytes 6291460
  134.4 3.6 %copy-start.8 = (f32[32,128,128]{2,1,0:T(8,128)S(1)}, f32[32,128,128]{2,1,0:T(8,128)}, u32[]{:S(2)}) copy-start(f32[32,128,128]{2,1,0:T(8,128)} %copy-done.7) | copy-start | bytes 6291460
  134.4 3.6 %copy-start.13 = (f32[128,128]{1,0:T(8,128)S(1)}, f32[128,128]{1,0:T(8,128)}, u32[]{:S(2)}) copy-start(f32[128,128]{1,0:T(8,128)} %fusion.83) | copy-start | bytes 196612
  140.4 4.5 %collective-permute-start.3 = (f32[2048,256]{1,0:T(8,128)S(1)}, f32[2048,256]{1,0:T(8,128)}, u32[]{:S(2)}, u32[]{:S(2)}) collective-permute-start(f32[2048,256]{1,0:T(8,128)S(1)} %fusion.50), channel_id=1, source_target_pairs={{0,4},{4,0},{1,5},{5,1},{2,6},{6,2},{3,7},{7,3},{8,12},{12,8},{9,1... | collective-permute-start | bytes 6291464 | tf_op jit(solution)/shard_map/ppermute | solution.py:113
  142.3 2.5 %collective-permute-start.4 = (f32[8,256]{1,0:T(8,128)S(1)}, f32[8,256]{1,0:T(8,128)S(1)}, u32[]{:S(2)}, u32[]{:S(2)}) collective-permute-start(f32[8,256]{1,0:T(8,128)S(1)} %scatter.7), channel_id=1, source_target_pairs={{0,4},{4,0},{1,5},{5,1},{2,6},{6,2},{3,7},{7,3},{8,12},{12,8},{9,1... | collective-permute-start | bytes 24584 | tf_op jit(solution)/shard_map/ppermute | solution.py:114
  191.3 36.1 %copy-start.11 = (f32[128,32,128]{0,2,1:T(8,128)S(1)}, f32[128,32,128]{0,2,1:T(8,128)}, u32[]{:S(2)}) copy-start(f32[128,32,128]{0,2,1:T(8,128)} %get-tuple-element.55) | copy-start | bytes 6291460
  191.4 36.1 %copy-start.15 = (f32[32,128]{1,0:T(8,128)S(1)}, f32[32,128]{1,0:T(8,128)}, u32[]{:S(2)}) copy-start(f32[32,128]{1,0:T(8,128)} %copy-done.14) | copy-start | bytes 49156
  191.4 36.1 %copy-start.17 = (f32[128,128]{0,1:T(8,128)S(1)}, f32[128,128]{0,1:T(8,128)}, u32[]{:S(2)}) copy-start(f32[128,128]{0,1:T(8,128)} %copy-done.16) | copy-start | bytes 196612
  191.4 36.1 %copy-start.20 = (pred[128,128]{0,1:T(8,128)(4,1)S(1)}, pred[128,128]{0,1:T(8,128)(4,1)}, u32[]{:S(2)}) copy-start(pred[128,128]{0,1:T(8,128)(4,1)} %copy-done.19) | copy-start | bytes 49156
  224.3 8.7 %collective-permute-start.5 = (f32[2048,256]{1,0:T(8,128)}, f32[2048,256]{1,0:T(8,128)S(1)}, u32[]{:S(2)}, u32[]{:S(2)}) collective-permute-start(f32[2048,256]{1,0:T(8,128)} %bitcast.32), channel_id=1, source_target_pairs={{0,4},{4,0},{1,5},{5,1},{2,6},{6,2},{3,7},{7,3},{8,12},{12,8},{9,1... | collective-permute-start | bytes 6291464 | tf_op jit(solution)/shard_map/ppermute | solution.py:125
  (6 other events, 10.9 us)

commit v15 on v13

--- a/solution.py
+++ b/solution.py
@@ -109,12 +109,11 @@
     rate_rows = jnp.zeros((8, cols), jnp.float32).at[0, :heads].set(d_rate)
     swap = [(0, 1), (1, 0)]
     paired = keep + lax.ppermute(give, "core", swap)
-    rate_pair = rate_rows + lax.ppermute(rate_rows, "core", swap)
     axes = ("cz", "dp")
     total = lax.axis_size(axes)
     chunk = half // total
     parcel = jnp.concatenate(
-        [paired.reshape(total, chunk, cols), jnp.broadcast_to(rate_pair[None], (total, 8, cols))], axis=1
+        [paired.reshape(total, chunk, cols), jnp.broadcast_to(rate_rows[None], (total, 8, cols))], axis=1
     )
     pieces = lax.all_to_all(parcel, axes, 0, 0, tiled=True)
     mine_sum = jnp.sum(pieces, axis=0)
@@ -124,7 +123,8 @@
     d_wbc = jnp.concatenate(
         [jnp.where(first, own_half, other_half), jnp.where(first, other_half, own_half)], axis=0
     )
-    d_alog = mine_sum[chunk, :heads]
+    partial = mine_sum[chunk, :heads]
+    d_alog = partial + lax.ppermute(partial, "core", swap)
     return (d_x[None], d_wbc, d_alog)
 
 

time: 234 us -> 234 us (level)
    ppermute x1, waiting for transfers between devices: 0.01 us -> 2.54 us  [per_device(): paired = keep + lax.ppermute(give, 'core', swap)]
where the time goes in v15:
time: 234 us; the launch traced here: 233 us
  blocking collectives  106 us (45%)
  waiting for transfers between devices  41 us (18%)
  matrix products  29.3 us (13%)
  other arithmetic  23.7 us (10%)
  local copies, waits for them, and re-layouts  17 us (7%)
  starting transfers between devices  14.9 us (6%)
    all_to_all x1, blocking collectives, per_device(): pieces = lax.all_to_all(parcel, axes, 0, 0, tiled=True)  41.5 us
    all_to_all x1, waiting for transfers between devices, exchange(): lax.all_to_all(marked(combined, pair_log), 'cz', 0, 0, tiled=True)  34.3 us
    all_to_all x1, blocking collectives, per_device(): lax.all_to_all(spread, axes, 0, 0, tiled=True).reshape(half, cols)  33.1 us
    all_to_all x1, blocking collectives, exchange(): back = lax.all_to_all(res, 'cz', 0, 0, tiled=True)  31.8 us
    all_to_all x1, starting transfers between devices, exchange(): lax.all_to_all(marked(combined, pair_log), 'cz', 0, 0, tiled=True)  7.75 us
    dot_general x2, matrix products, block_forward(): jnp.einsum('shp,sn->hpn', inputs * tail[:, :, None], b_in, precision=HIGH)  6.76 us
    dot_general x2, matrix products, block_forward(): y_intra = jnp.einsum('hts,shp->thp', mixing, inputs, precision=HIGH)  6.01 us
    unnamed x50, local copies, waits for them, and re-layouts  5.37 us
  transfers between devices with their start and end apart: 6, of which 3 were waited for; matrix products, arithmetic and copies ran while one was open for 7% of the time, Pallas kernels for 0%

profile of v15, /device:TPU:1, one launch (start us, length us, event | category | flops | bytes accessed | tf_op | source)
XLA Modules:
  0.0 233.4 jit_solution(3010439795102696483)
XLA Ops:
  0.7 2.7 %copy.121 = f32[1,128,4096]{1,2,0:T(8,128)} copy(bf16[1,128,4096]{2,1,0:T(8,128)(2,1)} %param.10) | data formatting | bytes 3145728 | tf_op jit(solution)/shard_map/convert_element_type | solution.py:91
  9.4 2.0 broadcast_select_fusion.2
  14.5 4.2 %collective-permute-done = f32[32,136,128]{2,1,0:T(8,128)} collective-permute-done((f32[32,136,128]{2,1,0:T(8,128)}, f32[32,136,128]{2,1,0:T(8,128)}, u32[]{:S(2)}, u32[]{:S(2)}) %collective-permute-start) | collective-permute-done | bytes 2228256 | tf_op jit(solution)/shard_map/ppermute | solution.py:21
  20.5 2.6 %multiply_add_fusion = f32[32,128,128]{2,1,0:T(8,128)S(1)} fusion(f32[32,128,128]{2,1,0:T(8,128)} %copy-done.4, f32[32,128,128]{2,1,0:T(8,128)} %get-tuple-element.53, f32[32,136,128]{2,1,0:T(8,128)} %collective-permute-done, f32[32]{0:T(128)S(1)} %fusion.107, pred[]{:T(512)S(6)} %eq.4), kind=kLoop, calls=%fused_computation.30 | loop fusion | flops 1572864 | bytes 8388737 | tf_op jit(solution)/shard_map/add | solution.py:26
  24.7 7.8 %all-to-all-start = ((f32[32,136,128]{2,1,0:T(8,128)}), f32[32,136,128]{2,1,0:T(8,128)}, u32[]{:S(2)}, u32[]{:S(2)}) async-start(f32[32,136,128]{2,1,0:T(8,128)} %pad_maximum_fusion.3), calls=%async_computation | async-start | bytes 4456448 | tf_op jit(solution)/shard_map/all_to_all | solution.py:29
  32.4 34.3 %all-to-all-done = f32[32,136,128]{2,1,0:T(8,128)} async-done(((f32[32,136,128]{2,1,0:T(8,128)}), f32[32,136,128]{2,1,0:T(8,128)}, u32[]{:S(2)}, u32[]{:S(2)}) %all-to-all-start) | async-done | bytes 2228256 | tf_op jit(solution)/shard_map/all_to_all | solution.py:29
  68.0 3.1 %fusion.20 = f32[16,2,136,128]{3,0,2,1:T(8,128)S(1)} fusion(f32[16,2,136,128]{3,2,1,0:T(8,128)} %bitcast.8, f32[16,2]{0,1:T(2,128)S(1)} %copy.132, f32[16,2]{0,1:T(2,128)S(1)} %copy.130, pred[16,16]{1,0:T(8,128)(4,1)S(1)} %get-tuple-element.56, pred[16,16]{1,0:T(8,128)(4,1)S(1)} %get-tuple-element.57, pred[]{:T(512)S(6)} %eq.4), kind=kOutput, calls=%fused_computation.38 | convolution fusion | flops 53479936 | bytes 4457217 | tf_op jit(solution)/shard_map/djh,jhpn->dhpn/dot_general | solution.py:38
  71.8 31.8 %all_to_all.20 = f32[32,136,128]{2,1,0:T(8,128)} all-to-all(f32[32,136,128]{2,1,0:T(8,128)S(1)} %bitcast.152), channel_id=1, replica_groups=mesh['cz'=16,'core'=2,'dp'=4] {'cz'}, dimensions={0} | all-to-all | bytes 4456448 | tf_op jit(solution)/shard_map/all_to_all | solution.py:39
  103.6 2.5 %collective-permute-start.1 = (f32[32,136,128]{2,1,0:T(8,128)}, f32[32,136,128]{2,1,0:T(8,128)}, u32[]{:S(2)}, u32[]{:S(2)}) collective-permute-start(f32[32,136,128]{2,1,0:T(8,128)} %all_to_all.20), channel_id=1, source_target_pairs={{0,4},{4,0},{1,5},{5,1},{2,6},{6,2},{3,7},{7,3},{8,12},{12,8},{9,1... | collective-permute-start | bytes 6684680 | tf_op jit(solution)/shard_map/ppermute | solution.py:40
  106.8 3.3 %fusion.24 = (f32[32,128]{1,0:T(8,128)}, f32[32,128]{1,0:T(8,128)S(1)}, f32[128,128]{0,1:T(8,128)}) fusion(f32[128,128]{0,1:T(8,128)S(1)} %fusion.78, f32[32,128]{1,0:T(8,128)S(1)} %reduce_window_sum.46, pred[128,128]{0,1:T(8,128)(4,1)S(1)} %iota_compare_fusion, bf16[32,128,128]{2,1,0:T(8,128)(2,1)S(1)} %bitcast.148, f32[128,32,128]{0,2,1:T(8,128)S(1)} %bitcast.144, ...), kind=kOutput, calls=%fused_computation.40 | convolution fusion | flops 407871488 | bytes 3358720 | tf_op jit(solution)/shard_map/transpose(jvp(hts,shp->thp))/dot_general | solution.py:63
  114.2 4.1 %multiply_reduce_fusion = (f32[32]{0:T(128)}, f32[32,128,128]{2,1,0:T(8,128)S(1)}, f32[32,128,128]{2,1,0:T(8,128)S(1)}) fusion(f32[32,136,128]{2,1,0:T(8,128)} %collective-permute-done, f32[32,136,128]{2,1,0:T(8,128)} %all_to_all.20, f32[32]{0:T(128)} %get-tuple-element.30, f32[32,136,128]{2,1,0:T(8,128)} %collective-permute-done.1, pred[]{:T(512)S(6)} %eq.4), kind=kLoop, calls=%fused_computation.23 | loop fusion | flops 3145696 | bytes 10486017 | tf_op jit(solution)/shard_map/transpose(jvp())/reduce_sum | solution.py:67
  118.3 3.2 %multiply_reduce_fusion.1 = (f32[128,32]{0,1:T(8,128)}, f32[128,32,128]{0,2,1:T(8,128)}) fusion(f32[128,32,128]{0,2,1:T(8,128)S(1)} %bitcast.145, f32[128,32]{0,1:T(8,128)S(1)} %copy.143, f32[32,128,128]{2,1,0:T(8,128)S(1)} %get-tuple-element.37, bf16[128,256]{1,0:T(8,128)(2,1)S(1)} %convolution_convert_fusion), kind=kOutput, calls=%fused_computation.24 | convolution fusion | flops 404221952 | bytes 6356992 | tf_op jit(solution)/shard_map/transpose(jvp(shp,sn->hpn))/dot_general | solution.py:66
  130.4 3.6 %fusion.34 = bf16[128,128]{1,0:T(8,128)(2,1)S(1)} fusion(f32[128,128]{1,0:T(8,128)S(1)} %fusion.76, f32[32,128,128]{2,1,0:T(8,128)} %copy-done.3, f32[128,32,128]{0,2,1:T(8,128)S(1)} %bitcast.146, f32[128,32]{0,1:T(8,128)S(1)} %copy.143, f32[128,32]{0,1:T(8,128)S(1)} %copy.140), kind=kOutput, calls=%fused_computation.47 | convolution fusion | flops 403734528 | bytes 4325376 | tf_op jit(solution)/shard_map/transpose(jvp(shp,sn->hpn))/dot_general | solution.py:66
  134.0 1.9 fusion.33
  138.3 2.5 %collective-permute-done.2 = f32[2048,256]{1,0:T(8,128)} collective-permute-done((f32[2048,256]{1,0:T(8,128)S(1)}, f32[2048,256]{1,0:T(8,128)}, u32[]{:S(2)}, u32[]{:S(2)}) %collective-permute-start.2) | collective-permute-done | bytes 2097184 | tf_op jit(solution)/shard_map/ppermute | solution.py:111
  140.8 2.4 %convolution_add_fusion = f32[2048,256]{1,0:T(8,128)S(1)} fusion(f32[2048,256]{1,0:T(8,128)} %collective-permute-done.2, pred[]{:T(512)S(6)} %eq.4, bf16[128,4096]{1,0:T(8,128)(2,1)} %bitcast.154, bf16[128,128]{1,0:T(8,128)(2,1)S(1)} %fusion.34, bf16[128,128]{1,0:T(8,128)(2,1)S(1)} %fusion.33), kind=kOutput, calls=%fused_computation.4 | convolution fusion | flops 135135232 | bytes 5308417 | tf_op jit(solution)/shard_map/dot_general | solution.py:107
  143.6 41.5 %all_to_all.21 = f32[64,40,256]{2,1,0:T(8,128)} all-to-all(f32[64,40,256]{2,1,0:T(8,128)S(1)} %pad_maximum_fusion.1), channel_id=1, replica_groups=mesh['cz'=16,'core'=2,'dp'=4] {'cz','dp'}, dimensions={0} | all-to-all | bytes 5242880 | tf_op jit(solution)/shard_map/all_to_all | solution.py:118
  185.1 1.9 reduce_sum.104
  187.3 33.1 %all_to_all.22 = f32[64,32,256]{2,1,0:T(8,128)} all-to-all(f32[64,32,256]{2,1,0:T(8,128)S(1)} %broadcast_in_dim.100), channel_id=1, replica_groups=mesh['cz'=16,'core'=2,'dp'=4] {'cz','dp'}, dimensions={0} | all-to-all | bytes 4194304 | tf_op jit(solution)/shard_map/all_to_all | solution.py:121
  220.3 3.2 %collective-permute-start.3 = (f32[2048,256]{1,0:T(8,128)}, f32[2048,256]{1,0:T(8,128)S(1)}, u32[]{:S(2)}, u32[]{:S(2)}) collective-permute-start(f32[2048,256]{1,0:T(8,128)} %bitcast.32), channel_id=1, source_target_pairs={{0,4},{4,0},{1,5},{5,1},{2,6},{6,2},{3,7},{7,3},{8,12},{12,8},{9,1... | collective-permute-start | bytes 6291464 | tf_op jit(solution)/shard_map/ppermute | solution.py:122
  223.6 2.7 %fusion.10 = bf16[128,32,128]{0,2,1:T(8,128)(2,1)} fusion(f32[128,32,128]{0,2,1:T(8,128)S(1)} %copy-done.8, f32[128,32]{0,1:T(8,128)S(1)} %copy.143, bf16[32,128,128]{2,1,0:T(8,128)(2,1)S(1)} %bitcast.151, f32[128,128]{0,1:T(8,128)S(1)} %copy-done.14, f32[32,128]{1,0:T(8,128)S(1)} %copy-done.12, f32[128,32]{0,1:T(8,128)S(1)} %copy.140, ...), kind=kOutput, calls=%fused_computation.22 | convolution fusion | flops 406323200 | bytes 4325376 | tf_op jit(solution)/shard_map/transpose(jvp(hts,shp->thp))/dot_general | solution.py:63
  226.3 2.3 copy.155
  229.1 1.9 broadcast_select_fusion.1
  231.0 2.3 pad_maximum_fusion
  (111 shorter events, 31.7 us)
Async XLA Ops:
  0.6 5.4 %copy-start = (bf16[4096,256]{1,0:T(8,128)(2,1)S(1)}, bf16[4096,256]{1,0:T(8,128)(2,1)}, u32[]{:S(2)}) copy-start(bf16[4096,256]{1,0:T(8,128)(2,1)} %param.9) | copy-start | bytes 6291460
  0.6 2.7 %copy-start.15 = (f32[1,128,32]{1,2,0:T(8,128)S(1)}, f32[1,128,32]{1,2,0:T(8,128)}, u32[]{:S(2)}) copy-start(f32[1,128,32]{1,2,0:T(8,128)} %param.11) | copy-start | bytes 49156
  0.7 2.8 %copy-start.21 = (f32[32]{0:T(128)S(1)}, f32[32]{0:T(128)}, u32[]{:S(2)}) copy-start(f32[32]{0:T(128)} %param.12) | copy-start | bytes 388
  8.5 2.9 %copy-start.4 = (f32[32,128,128]{2,1,0:T(8,128)}, f32[32,128,128]{2,1,0:T(8,128)S(1)}, u32[]{:S(2)}) copy-start(f32[32,128,128]{2,1,0:T(8,128)S(1)} %fusion.2) | copy-start | bytes 6291460
  11.5 2.9 %copy-start.20 = (f32[32,1,1]{0,2,1:T(1,128)S(1)}, f32[32,1,1]{0,2,1:T(1,128)}, u32[]{:S(2)}) copy-start(f32[32,1,1]{0,2,1:T(1,128)} %get-tuple-element.48) | copy-start | bytes 388
  13.0 5.7 %collective-permute-start = (f32[32,136,128]{2,1,0:T(8,128)}, f32[32,136,128]{2,1,0:T(8,128)}, u32[]{:S(2)}, u32[]{:S(2)}) collective-permute-start(f32[32,136,128]{2,1,0:T(8,128)} %pad_maximum_fusion.2), channel_id=1, source_target_pairs={{0,4},{4,0},{1,5},{5,1},{2,6},{6,2},{3,7},{7,3},{8,12},{12,8},{9,1... | collective-permute-start | bytes 6684680 | tf_op jit(solution)/shard_map/ppermute | solution.py:21
  24.7 42.0 %all-to-all-start = ((f32[32,136,128]{2,1,0:T(8,128)}), f32[32,136,128]{2,1,0:T(8,128)}, u32[]{:S(2)}, u32[]{:S(2)}) async-start(f32[32,136,128]{2,1,0:T(8,128)} %pad_maximum_fusion.3), calls=%async_computation | async-start | bytes 4456448 | tf_op jit(solution)/shard_map/all_to_all | solution.py:29
  103.6 10.6 %collective-permute-start.1 = (f32[32,136,128]{2,1,0:T(8,128)}, f32[32,136,128]{2,1,0:T(8,128)}, u32[]{:S(2)}, u32[]{:S(2)}) collective-permute-start(f32[32,136,128]{2,1,0:T(8,128)} %all_to_all.20), channel_id=1, source_target_pairs={{0,4},{4,0},{1,5},{5,1},{2,6},{6,2},{3,7},{7,3},{8,12},{12,8},{9,1... | collective-permute-start | bytes 6684680 | tf_op jit(solution)/shard_map/ppermute | solution.py:40
  106.5 3.5 %copy-start.11 = (f32[32,128]{1,0:T(8,128)}, f32[32,128]{1,0:T(8,128)S(1)}, u32[]{:S(2)}) copy-start(f32[32,128]{1,0:T(8,128)S(1)} %reduce_window_sum.46) | copy-start | bytes 49156
  106.6 3.4 %copy-start.16 = (pred[128,128]{0,1:T(8,128)(4,1)}, pred[128,128]{0,1:T(8,128)(4,1)S(1)}, u32[]{:S(2)}) copy-start(pred[128,128]{0,1:T(8,128)(4,1)S(1)} %iota_compare_fusion) | copy-start | bytes 49156
  106.8 3.3 %copy-start.13 = (f32[128,128]{0,1:T(8,128)}, f32[128,128]{0,1:T(8,128)S(1)}, u32[]{:S(2)}) copy-start(f32[128,128]{0,1:T(8,128)S(1)} %fusion.78) | copy-start | bytes 196612
  118.3 3.2 %copy-start.3 = (f32[32,128,128]{2,1,0:T(8,128)}, f32[32,128,128]{2,1,0:T(8,128)S(1)}, u32[]{:S(2)}) copy-start(f32[32,128,128]{2,1,0:T(8,128)S(1)} %get-tuple-element.37) | copy-start | bytes 6291460
  118.3 3.2 %copy-start.5 = (f32[32,128,128]{2,1,0:T(8,128)}, f32[32,128,128]{2,1,0:T(8,128)S(1)}, u32[]{:S(2)}) copy-start(f32[32,128,128]{2,1,0:T(8,128)S(1)} %get-tuple-element.36) | copy-start | bytes 6291460
  130.4 3.6 %copy-start.6 = (f32[32,128,128]{2,1,0:T(8,128)S(1)}, f32[32,128,128]{2,1,0:T(8,128)}, u32[]{:S(2)}) copy-start(f32[32,128,128]{2,1,0:T(8,128)} %copy-done.5) | copy-start | bytes 6291460
  130.4 3.6 %copy-start.10 = (f32[128,128]{1,0:T(8,128)S(1)}, f32[128,128]{1,0:T(8,128)}, u32[]{:S(2)}) copy-start(f32[128,128]{1,0:T(8,128)} %fusion.83) | copy-start | bytes 196612
  135.9 2.3 copy-start.22
  136.4 4.4 %collective-permute-start.2 = (f32[2048,256]{1,0:T(8,128)S(1)}, f32[2048,256]{1,0:T(8,128)}, u32[]{:S(2)}, u32[]{:S(2)}) collective-permute-start(f32[2048,256]{1,0:T(8,128)S(1)} %fusion.50), channel_id=1, source_target_pairs={{0,4},{4,0},{1,5},{5,1},{2,6},{6,2},{3,7},{7,3},{8,12},{12,8},{9,1... | collective-permute-start | bytes 6291464 | tf_op jit(solution)/shard_map/ppermute | solution.py:111
  187.2 36.3 %copy-start.8 = (f32[128,32,128]{0,2,1:T(8,128)S(1)}, f32[128,32,128]{0,2,1:T(8,128)}, u32[]{:S(2)}) copy-start(f32[128,32,128]{0,2,1:T(8,128)} %get-tuple-element.55) | copy-start | bytes 6291460
  187.2 36.3 %copy-start.12 = (f32[32,128]{1,0:T(8,128)S(1)}, f32[32,128]{1,0:T(8,128)}, u32[]{:S(2)}) copy-start(f32[32,128]{1,0:T(8,128)} %copy-done.11) | copy-start | bytes 49156
  187.2 36.3 %copy-start.14 = (f32[128,128]{0,1:T(8,128)S(1)}, f32[128,128]{0,1:T(8,128)}, u32[]{:S(2)}) copy-start(f32[128,128]{0,1:T(8,128)} %copy-done.13) | copy-start | bytes 196612
  187.3 36.3 %copy-start.17 = (pred[128,128]{0,1:T(8,128)(4,1)S(1)}, pred[128,128]{0,1:T(8,128)(4,1)}, u32[]{:S(2)}) copy-start(pred[128,128]{0,1:T(8,128)(4,1)} %copy-done.16) | copy-start | bytes 49156
  220.3 8.8 %collective-permute-start.3 = (f32[2048,256]{1,0:T(8,128)}, f32[2048,256]{1,0:T(8,128)S(1)}, u32[]{:S(2)}, u32[]{:S(2)}) collective-permute-start(f32[2048,256]{1,0:T(8,128)} %bitcast.32), channel_id=1, source_target_pairs={{0,4},{4,0},{1,5},{5,1},{2,6},{6,2},{3,7},{7,3},{8,12},{12,8},{9,1... | collective-permute-start | bytes 6291464 | tf_op jit(solution)/shard_map/ppermute | solution.py:122
  226.3 2.3 collective-permute-start.4
  231.0 2.4 %copy-start.1 = (bf16[4096,256]{1,0:T(8,128)(2,1)S(1)}, bf16[4096,256]{1,0:T(8,128)(2,1)}, u32[]{:S(2)}) copy-start(bf16[4096,256]{1,0:T(8,128)(2,1)} %param.9) | copy-start | bytes 6291460
  (5 other events, 8.1 us)
